TPU v7x, 32 devices: a whole 2x2x4 slice. The times are simulated.
32 devices in a mesh: groups: 2 (over y), space: 4 (over z), sub: 2 (over x), ch: 2 (over core).
Axes of the slice: x: 2, y: 2, z: 4, core: 2. Of those that a mesh axis runs over, the one named last changes fastest.
Arguments:
- volumes: bfloat16 [4, 4, 32, 4, 256], P(('groups', 'sub'), None, None, 'space'), parts along dimension 0, may hold values from -6 to 6
- cotangent: bfloat16 [4, 4, 128, 2, 64], P(('groups', 'sub'), 'space', 'ch'), parts along dimension 0, may hold values from -6 to 6
- first_weight: bfloat16 [256, 128], P(None, 'ch'), may hold values from -0.375 to 0.375
- second_weight: bfloat16 [3456, 128], P(None, 'ch'), may hold values from -0.109375 to 0.109375
Outputs:
- block_out: bfloat16 [4, 4, 128, 2, 64], P(('groups', 'sub'), 'space', 'ch'), parts along dimension 0
- volume_grad: bfloat16 [4, 4, 32, 4, 256], P(('groups', 'sub'), None, 'ch', 'space'), parts along dimension 0
- first_grad: float32 [256, 256], P(('space', 'sub'), ('groups', 'ch')), parts along dimension 1
- second_grad: float32 [3456, 256], P(('space', 'sub'), ('groups', 'ch')), parts along dimension 1
There are 2 independent parts, one for each index of `groups`. A program takes and returns all parts, laid end to end along the dimension named above; an argument that names none is the same for every part. Nothing has to cross between parts.
All inputs are finite; a program needn't handle non-finite values.
Results may differ from a plain program's by a relative error of at most 0.005.
Values may be sent and summed in bfloat16 or wider, within the bound.
No kernel may reach another device: no remote copies, remote signals or barrier semaphores. Data moves between devices by JAX's collectives and lax.ppermute only.
A program may use at most 64 MiB of HBM per device.

v0:
```python
import math

import jax
import jax.numpy as jnp
from jax import lax
from jax.sharding import PartitionSpec as P

XY = 16


def to_depth(sample, side):
    chans, depth = (sample.shape[0], sample.shape[1])
    blocks = sample.reshape(chans, depth // 2, 2, side // 2, 2, side // 2, 2)
    blocks = blocks.transpose(2, 4, 6, 0, 1, 3, 5)
    return blocks.reshape(8 * chans, depth // 2 * (side // 2) * (side // 2))


def from_depth(cols, chans, depth, side):
    blocks = cols.reshape(2, 2, 2, chans, depth // 2, side // 2, side // 2)
    blocks = blocks.transpose(3, 4, 0, 5, 1, 6, 2)
    return blocks.reshape(chans, depth, side * side)


def plane_stack(padded, plane, depth, side, flip):
    chans = padded.shape[0]
    windows = []
    for inner in range(9):
        b, c = (inner // 3, inner % 3)
        if flip:
            window = padded[
                :, 2 - plane : 2 - plane + depth, 2 - b : 2 - b + side, 2 - c : 2 - c + side
            ]
        else:
            window = padded[:, plane : plane + depth, b : b + side, c : c + side]
        windows.append(window.reshape(chans, depth * side * side))
    return jnp.concatenate(windows, axis=0)


def conv_forward(hidden, weight):
    chans, depth, side = (hidden.shape[0], hidden.shape[1], hidden.shape[2])
    padded = jnp.pad(hidden, ((0, 0), (1, 1), (1, 1), (1, 1)))
    total = jnp.zeros((weight.shape[1], depth * side * side), jnp.float32)
    for plane in range(3):
        stacked = plane_stack(padded, plane, depth, side, False)
        piece = weight[plane * 9 * chans : (plane + 1) * 9 * chans]
        total = total + lax.dot_general(
            piece, stacked, (((0,), (0,)), ((), ())), preferred_element_type=jnp.float32
        )
    return total


def conv_weight_grad(hidden, cot):
    chans, depth, side = (hidden.shape[0], hidden.shape[1], hidden.shape[2])
    padded = jnp.pad(hidden, ((0, 0), (1, 1), (1, 1), (1, 1)))
    pieces = []
    for plane in range(3):
        stacked = plane_stack(padded, plane, depth, side, False)
        pieces.append(
            lax.dot_general(
                stacked, cot, (((1,), (1,)), ((), ())), preferred_element_type=jnp.float32
            )
        )
    return jnp.concatenate(pieces, axis=0)


def conv_back(cot, weight_rows):
    chans, depth, side = (cot.shape[0], cot.shape[1], cot.shape[2])
    padded = jnp.pad(cot, ((0, 0), (1, 1), (1, 1), (1, 1)))
    total = jnp.zeros((weight_rows.shape[1], depth * side * side), jnp.float32)
    for plane in range(3):
        stacked = plane_stack(padded, plane, depth, side, True)
        group = weight_rows[plane * 9 : (plane + 1) * 9]
        lhs = group.transpose(1, 0, 2).reshape(group.shape[1], 9 * group.shape[2])
        total = total + jnp.dot(lhs, stacked, preferred_element_type=jnp.float32)
    return total


def silu_slope(pre):
    sig = jax.nn.sigmoid(pre)
    return sig * (1.0 + pre * (1.0 - sig))


def body(volumes, cotangent, first_weight, second_weight):
    chans = volumes.shape[2]
    half_c = chans // lax.axis_size("ch")
    pair_index = lax.axis_index("ch")
    half_o = first_weight.shape[1]
    sample = lax.all_to_all(volumes, "space", split_axis=1, concat_axis=3, tiled=True)
    depth = sample.shape[3]
    sample = sample.reshape(chans, depth, XY * XY)
    half_z, half_s = (depth // 2, XY // 2)
    voxels = half_z * half_s * half_s
    cols = to_depth(sample, XY)
    pre = lax.dot_general(
        first_weight, cols, (((0,), (0,)), ((), ())), preferred_element_type=jnp.float32
    )
    hidden = jax.nn.silu(pre).astype(jnp.bfloat16)
    grid = lax.all_gather(hidden.reshape(half_o, half_z, half_s, half_s), "ch", axis=0, tiled=True)
    width = grid.shape[0]
    out = conv_forward(grid, second_weight)
    block_out = out.astype(jnp.bfloat16).reshape(1, 1, half_o, half_z, half_s * half_s)
    cot = cotangent.reshape(half_o, voxels)
    factor = 1.0 / math.sqrt(lax.axis_size("space") * lax.axis_size("sub") * voxels)
    grad_second = conv_weight_grad(grid, cot) * factor
    cot_grid = cot.reshape(half_o, half_z, half_s, half_s)
    local_rows = second_weight.reshape(27, width, half_o)
    hidden_grad = lax.psum_scatter(
        conv_back(cot_grid, local_rows), "ch", scatter_dimension=0, tiled=True
    )
    pre_grad = (hidden_grad * silu_slope(pre)).astype(jnp.bfloat16)
    grad_first = (
        lax.dot_general(
            cols, pre_grad, (((1,), (1,)), ((), ())), preferred_element_type=jnp.float32
        )
        * factor
    )
    all_pre_grad, all_first = (
        lax.all_gather(pre_grad, "ch", axis=0, tiled=True),
        lax.all_gather(first_weight, "ch", axis=1, tiled=True),
    )
    first_rows = lax.dynamic_slice_in_dim(
        all_first.reshape(8, chans, width), pair_index * half_c, half_c, 1
    )
    grad_cols = jnp.dot(
        first_rows.reshape(8 * half_c, width), all_pre_grad, preferred_element_type=jnp.float32
    )
    grad_sample = from_depth(grad_cols, half_c, depth, XY).astype(jnp.bfloat16)
    volume_grad = lax.all_to_all(
        grad_sample.reshape(1, 1, half_c, depth, XY * XY),
        "space",
        split_axis=3,
        concat_axis=1,
        tiled=True,
    )
    first_grad, second_grad = (
        lax.psum_scatter(grad_first, ("space", "sub"), scatter_dimension=0, tiled=True),
        lax.psum_scatter(grad_second, ("space", "sub"), scatter_dimension=0, tiled=True),
    )
    return (block_out, volume_grad, first_grad, second_grad)


def solution(mesh):
    return jax.shard_map(
        body,
        mesh=mesh,
        in_specs=(
            P(("groups", "sub"), None, None, "space", None),
            P(("groups", "sub"), "space", "ch", None, None),
            P(None, "ch"),
            P(None, "ch"),
        ),
        out_specs=(
            P(("groups", "sub"), "space", "ch", None, None),
            P(("groups", "sub"), None, "ch", "space", None),
            P(("space", "sub"), ("groups", "ch")),
            P(("space", "sub"), ("groups", "ch")),
        ),
        check_vma=False,
    )
```

profile of v0, /device:TPU:0, one launch (start us, length us, event | category | flops | bytes accessed | tf_op | source)
XLA Modules:
  0.0 169.6 jit_solution(6316466751185191411)
XLA Ops:
  7.2 0.9 copy.38
  8.2 1.1 fusion.9
  9.9 0.3 fusion.10
  10.3 0.3 convolution_add_fusion.1
  10.8 0.9 fusion.2
  11.7 11.9 %all_to_all.33 = bf16[1,4,32,1,256]{4,2,3,0,1:T(8,128)(2,1)S(1)} all-to-all(bf16[1,4,32,1,256]{4,2,3,0,1:T(8,128)(2,1)S(1)} %bitcast.202), channel_id=1, replica_groups=mesh['groups'=2,'space'=4,'sub'=2,'ch'=2] {'space'}, dimensions={1} | all-to-all | bytes 131072 | tf_op jit(solution)/shard_map/all_to_all | solution.py:88
  23.8 0.2 copy.32
  24.3 0.9 multiply_convert_fusion
  25.3 0.3 copy.34
  25.6 2.2 %all_gather.9 = bf16[128,2,8,8]{3,2,1,0:T(8,128)(2,1)S(1)} all-gather(bf16[64,2,8,8]{3,2,1,0:T(8,128)(2,1)S(1)} %copy.34), channel_id=1, replica_groups=mesh['groups'=2,'space'=4,'sub'=2,'ch'=2] {'ch'}, dimensions={0}, use_global_device_ids=true | all-gather | bytes 49152 | tf_op jit(solution)/shard_map/all_gather | solution.py:98
  27.8 0.4 copy.35
  28.5 0.2 fusion.11
  28.9 0.2 fusion.12
  29.3 0.2 fusion.13
  29.6 1.8 %copy.58 = f32[3456,64]{1,0:T(8,128)} copy(f32[3456,64]{0,1:T(8,128)S(1)} %maximum_multiply_fusion) | data formatting | bytes 1769472
  31.4 2.0 %all_gather.10 = bf16[256,128]{0,1:T(8,128)(2,1)S(1)} all-gather(bf16[256,64]{0,1:T(8,128)(2,1)S(1)} %copy-done.2), channel_id=1, replica_groups=mesh['groups'=2,'space'=4,'sub'=2,'ch'=2] {'ch'}, dimensions={1}, use_global_device_ids=true | all-gather | bytes 98304 | tf_op jit(solution)/shard_map/all_gather | solution.py:119
  33.5 1.8 %all_gather.11 = bf16[128,128]{1,0:T(8,128)(2,1)S(1)} all-gather(bf16[64,128]{1,0:T(8,128)(2,1)S(1)} %get-tuple-element.19), channel_id=1, replica_groups=mesh['groups'=2,'space'=4,'sub'=2,'ch'=2] {'ch'}, dimensions={0}, use_global_device_ids=true | all-gather | bytes 49152 | tf_op jit(solution)/shard_map/all_gather | solution.py:118
  35.6 0.8 copy.56
  36.4 0.2 fusion
  36.6 0.3 copy.47
  36.9 0.7 copy.48
  37.6 3.3 %all-to-all-start.1 = ((bf16[1,1,16,4,256]{4,2,1,0,3:T(8,128)(2,1)}), bf16[1,1,16,4,256]{4,2,1,0,3:T(8,128)(2,1)S(1)}, u32[]{:S(2)}, u32[]{:S(2)}) async-start(bf16[1,1,16,4,256]{4,2,1,0,3:T(8,128)(2,1)} %copy.48), calls=%async_computation.2 | async-start | bytes 65536 | tf_op jit(solution)/shard_map/all_to_all | solution.py:128
  41.0 0.2 fusion.7
  41.2 0.2 convolution_add_fusion.3
  41.4 0.2 reduce-scatter.10.cloned.1.call-update
  41.6 0.2 fusion.4
  41.9 0.7 reshape.272
  42.6 4.0 %all-to-all-done.1 = bf16[1,1,16,4,256]{4,2,1,0,3:T(8,128)(2,1)S(1)} async-done(((bf16[1,1,16,4,256]{4,2,1,0,3:T(8,128)(2,1)}), bf16[1,1,16,4,256]{4,2,1,0,3:T(8,128)(2,1)S(1)}, u32[]{:S(2)}, u32[]{:S(2)}) %all-to-all-start.1) | async-done | bytes 32800 | tf_op jit(solution)/shard_map/all_to_all | solution.py:128
  46.6 51.3 %reduce-scatter.12.cloned.1.call-done = f32[432,64]{1,0:T(8,128)} async-done(((f32[3456,64]{1,0:T(8,128)}), f32[432,64]{1,0:T(8,128)}) %reduce-scatter.12.cloned.1.call-update) | async-done | bytes 110608
  97.9 1.7 %copy.59 = f32[432,64]{0,1:T(8,128)} copy(f32[432,64]{1,0:T(8,128)} %reduce-scatter.12.cloned.1.call-done) | data formatting | bytes 221184
  99.6 62.9 %reduce-scatter.10.cloned.1.call-done = f32[32,64]{1,0:T(8,128)} async-done(((f32[256,64]{1,0:T(8,128)}), f32[32,64]{1,0:T(8,128)}) %reduce-scatter.10.cloned.1.call-update) | async-done | bytes 8208
  162.5 0.6 copy.85
  (60 shorter events, 2.5 us)
Async XLA Ops:
  7.2 17.1 %reduce-scatter.8.cloned.1.call-start = ((), (), s32[]{:S(2)}) async-start(), calls=%async_computation.5 | async-start | bytes 98304 | tf_op jit(solution)/shard_map/reduce_scatter | solution.py:107
  9.6 2.1 %copy-start.1 = (bf16[1,4,32,1,256]{4,2,3,1,0:T(8,128)(2,1)S(1)}, bf16[1,4,32,1,256]{4,2,3,1,0:T(8,128)(2,1)}, u32[]{:S(2)}) copy-start(bf16[1,4,32,1,256]{4,2,3,1,0:T(8,128)(2,1)} %param.4) | copy-start | bytes 196612
  9.9 14.4 %copy-start.2 = (bf16[256,64]{0,1:T(8,128)(2,1)S(1)}, bf16[256,64]{0,1:T(8,128)(2,1)}, u32[]{:S(2)}) copy-start(bf16[256,64]{0,1:T(8,128)(2,1)} %param.6) | copy-start | bytes 98308
  11.7 86.2 %reduce-scatter.12.cloned.1.call-start = ((), (), s32[]{:S(2)}) async-start(), calls=%async_computation.7 | async-start | bytes 1990656
  31.4 9.6 %copy-start = (bf16[3456,64]{0,1:T(8,128)(2,1)S(1)}, bf16[3456,64]{0,1:T(8,128)(2,1)}, u32[]{:S(2)}) copy-start(bf16[3456,64]{0,1:T(8,128)(2,1)} %param.7) | copy-start | bytes 1327108
  37.6 8.9 %all-to-all-start.1 = ((bf16[1,1,16,4,256]{4,2,1,0,3:T(8,128)(2,1)}), bf16[1,1,16,4,256]{4,2,1,0,3:T(8,128)(2,1)S(1)}, u32[]{:S(2)}, u32[]{:S(2)}) async-start(bf16[1,1,16,4,256]{4,2,1,0,3:T(8,128)(2,1)} %copy.48), calls=%async_computation.2 | async-start | bytes 65536 | tf_op jit(solution)/shard_map/all_to_all | solution.py:128
  40.9 121.6 %reduce-scatter.10.cloned.1.call-start = ((), (), s32[]{:S(2)}) async-start(), calls=%async_computation.6 | async-start | bytes 147456
Sparse Core Ops, SparseCore 0:
  11.8 10.2 reduce-scatter.7
  31.5 66.3 reduce-scatter.11
  101.8 60.6 reduce-scatter.9
where the time goes:
time: 170 us
  waiting for transfers between devices  118 us (69%)
  blocking collectives  17.9 us (11%)
  between operations  14.2 us (8%)
  local copies, waits for them, and re-layouts  11.6 us (7%)
  matrix products  4.07 us (2%)
  starting transfers between devices  3.39 us (2%)
    unnamed x5, waiting for transfers between devices  114 us
    all_to_all x1, blocking collectives, body(): lax.all_to_all(volumes, 'space', split_axis=1, concat_axis=3, tiled=True)  11.9 us
    unnamed x35, local copies, waits for them, and re-layouts  6.03 us
    all_to_all x1, waiting for transfers between devices, body(): lax.all_to_all(grad_sample.reshape(1, 1, half_c, depth, XY * XY), 'space'...  3.98 us
  transfers between devices with their start and end apart: 4, of which 3 were waited for; matrix products, arithmetic and copies ran while one was open for 4% of the time, Pallas kernels for 0%

commit v1 on v0

--- a/solution.py
+++ b/solution.py
@@ -75,6 +75,26 @@
     return total
 
 
+def halving_scatter(x, names):
+    sizes = [lax.axis_size(n) for n in names]
+    labels = []
+    for name, size in zip(names, sizes):
+        bits = size.bit_length() - 1
+        labels += [(name, j) for j in reversed(range(bits))]
+    rows = x.shape[0] // math.prod(sizes)
+    x = x.reshape((2,) * len(labels) + (rows,) + x.shape[1:])
+    for name, size in reversed(list(zip(names, sizes))):
+        for j in range(size.bit_length() - 1):
+            pos = labels.index((name, j))
+            bit = (lax.axis_index(name) >> j) & 1
+            mine = lax.dynamic_index_in_dim(x, bit, axis=pos, keepdims=False)
+            other = lax.dynamic_index_in_dim(x, 1 - bit, axis=pos, keepdims=False)
+            perm = [(i, i ^ (1 << j)) for i in range(size)]
+            x = mine + lax.ppermute(other, name, perm)
+            labels.pop(pos)
+    return x
+
+
 def silu_slope(pre):
     sig = jax.nn.sigmoid(pre)
     return sig * (1.0 + pre * (1.0 - sig))
@@ -104,9 +124,7 @@
     grad_second = conv_weight_grad(grid, cot) * factor
     cot_grid = cot.reshape(half_o, half_z, half_s, half_s)
     local_rows = second_weight.reshape(27, width, half_o)
-    hidden_grad = lax.psum_scatter(
-        conv_back(cot_grid, local_rows), "ch", scatter_dimension=0, tiled=True
-    )
+    hidden_grad = halving_scatter(conv_back(cot_grid, local_rows), ("ch",))
     pre_grad = (hidden_grad * silu_slope(pre)).astype(jnp.bfloat16)
     grad_first = (
         lax.dot_general(
@@ -133,8 +151,8 @@
         tiled=True,
     )
     first_grad, second_grad = (
-        lax.psum_scatter(grad_first, ("space", "sub"), scatter_dimension=0, tiled=True),
-        lax.psum_scatter(grad_second, ("space", "sub"), scatter_dimension=0, tiled=True),
+        halving_scatter(grad_first, ("space", "sub")),
+        halving_scatter(grad_second, ("space", "sub")),
     )
     return (block_out, volume_grad, first_grad, second_grad)
 

time: 170 us -> 62.1 us (0.37)
  waiting for transfers between devices: 118 us -> 17.6 us
  starting transfers between devices: 3.39 us -> 22.1 us
  between operations: 14.2 us -> 1.17 us
  blocking collectives: 17.9 us -> 5.85 us
  other arithmetic: 0.06 us -> 1.77 us
    unnamed x5 -> x0, waiting for transfers between devices: 114 us -> none
    ppermute x0 -> x7, waiting for transfers between devices: none -> 17.4 us  [halving_scatter(): x = mine + lax.ppermute(other, name, perm)]
    all_to_all x1 -> x0, blocking collectives: 11.9 us -> none  [body(): lax.all_to_all(volumes, 'space', split_axis=1, concat_axis=3, tiled=True)]
    ppermute x0 -> x7, starting transfers between devices: none -> 10.8 us  [halving_scatter(): x = mine + lax.ppermute(other, name, perm)]
    all_to_all x0 -> x1, starting transfers between devices: none -> 6.36 us  [body(): lax.all_to_all(volumes, 'space', split_axis=1, concat_axis=3, tiled=True)]
    all_to_all x1, waiting for transfers between devices: 3.98 us -> 0.01 us  [body(): lax.all_to_all(grad_sample.reshape(1, 1, half_c, depth, XY * XY), 'space'...]
    unnamed x35 -> x33, local copies, waits for them, and re-layouts: 6.03 us -> 2.81 us
    add x0 -> x6, other arithmetic: none -> 1.71 us  [halving_scatter(): x = mine + lax.ppermute(other, name, perm)]
  transfers between devices with their start and end apart: 4 -> 9, of which waited for: 3 -> 4; matrix products, arithmetic and copies ran while one was open for 4% -> 16% of each run, Pallas kernels for 0% -> 0%
where the time goes in v1:
time: 62.1 us; the launch traced here: 61.6 us
  starting transfers between devices  22.1 us (36%)
  waiting for transfers between devices  17.6 us (28%)
  local copies, waits for them, and re-layouts  10.5 us (17%)
  blocking collectives  5.85 us (9%)
  matrix products  2.67 us (4%)
  other arithmetic  1.77 us (3%)
  between operations  1.17 us (2%)
    ppermute x7, waiting for transfers between devices, halving_scatter(): x = mine + lax.ppermute(other, name, perm)  17.4 us
    ppermute x7, starting transfers between devices, halving_scatter(): x = mine + lax.ppermute(other, name, perm)  10.8 us
    all_to_all x1, starting transfers between devices, body(): lax.all_to_all(volumes, 'space', split_axis=1, concat_axis=3, tiled=True)  6.36 us
    all_to_all x1, starting transfers between devices, body(): lax.all_to_all(grad_sample.reshape(1, 1, half_c, depth, XY * XY), 'space'...  4.96 us
    unnamed x33, local copies, waits for them, and re-layouts  2.81 us
    all_gather x1, blocking collectives, body(): lax.all_gather(hidden.reshape(half_o, half_z, half_s, half_s), 'ch', axis...  2.18 us
    all_gather x1, blocking collectives, body(): lax.all_gather(first_weight, 'ch', axis=1, tiled=True)  1.84 us
    all_gather x1, blocking collectives, body(): lax.all_gather(pre_grad, 'ch', axis=0, tiled=True)  1.83 us
  transfers between devices with their start and end apart: 9, of which 4 were waited for; matrix products, arithmetic and copies ran while one was open for 16% of the time, Pallas kernels for 0%

profile of v1, /device:TPU:0, one launch (start us, length us, event | category | flops | bytes accessed | tf_op | source)
XLA Modules:
  0.0 61.6 jit_solution(1976951385503044176)
XLA Ops:
  0.6 6.4 %all-to-all-start = ((bf16[1,4,32,1,256]{4,2,3,0,1:T(8,128)(2,1)}), bf16[1,4,32,1,256]{4,2,3,0,1:T(8,128)(2,1)S(1)}, u32[]{:S(2)}, u32[]{:S(2)}) async-start(bf16[1,4,32,1,256]{4,2,3,0,1:T(8,128)(2,1)} %bitcast.244), calls=%async_computation | async-start | bytes 131072 | tf_op jit(solution)/shard_map/all_to_all | solution.py:108
  7.3 0.8 %copy-done = bf16[3456,64]{0,1:T(8,128)(2,1)S(1)} copy-done((bf16[3456,64]{0,1:T(8,128)(2,1)S(1)}, bf16[3456,64]{0,1:T(8,128)(2,1)}, u32[]{:S(2)}) %copy-start) | copy-done | bytes 442392
  8.7 0.3 fusion.11
  9.2 0.3 convolution_add_fusion.1
  9.6 0.3 convolution_add_fusion
  10.0 0.6 %copy-done.1 = bf16[256,64]{0,1:T(8,128)(2,1)S(1)} copy-done((bf16[256,64]{0,1:T(8,128)(2,1)S(1)}, bf16[256,64]{0,1:T(8,128)(2,1)}, u32[]{:S(2)}) %copy-start.1) | copy-done | bytes 32792
  10.6 1.8 %all_gather.10 = bf16[256,128]{0,1:T(8,128)(2,1)S(1)} all-gather(bf16[256,64]{0,1:T(8,128)(2,1)S(1)} %copy-done.1), channel_id=1, replica_groups=mesh['groups'=2,'space'=4,'sub'=2,'ch'=2] {'ch'}, dimensions={1}, use_global_device_ids=true | all-gather | bytes 98304 | tf_op jit(solution)/shard_map/all_gather | solution.py:137
  13.7 1.8 %all_gather.11 = bf16[128,128]{1,0:T(8,128)(2,1)S(1)} all-gather(bf16[64,128]{1,0:T(8,128)(2,1)S(1)} %get-tuple-element.19), channel_id=1, replica_groups=mesh['groups'=2,'space'=4,'sub'=2,'ch'=2] {'ch'}, dimensions={0}, use_global_device_ids=true | all-gather | bytes 49152 | tf_op jit(solution)/shard_map/all_gather | solution.py:136
  15.6 0.3 copy.33
  15.9 2.2 %all_gather.9 = bf16[128,2,8,8]{3,2,1,0:T(8,128)(2,1)S(1)} all-gather(bf16[64,2,8,8]{3,2,1,0:T(8,128)(2,1)S(1)} %copy.33), channel_id=1, replica_groups=mesh['groups'=2,'space'=4,'sub'=2,'ch'=2] {'ch'}, dimensions={0}, use_global_device_ids=true | all-gather | bytes 49152 | tf_op jit(solution)/shard_map/all_gather | solution.py:118
  18.1 0.4 copy.34
  19.5 1.6 %collective-permute-start.1 = (f32[2,2,32,64]{3,2,1,0:T(8,128)S(1)}, f32[2,2,32,64]{3,2,1,0:T(8,128)S(1)}, u32[]{:S(2)}, u32[]{:S(2)}) collective-permute-start(f32[2,2,32,64]{3,2,1,0:T(8,128)S(1)} %dynamic-slice_bitcast_fusion.1), channel_id=1, source_target_pairs={{0,2},{2,0},{1,3},{3,1},{4,6},{6,4},{5,7},{7,5},{8,10},{10,8},{9,1... | collective-permute-start | bytes 98312 | tf_op jit(solution)/shard_map/ppermute | solution.py:93
  21.3 0.3 copy.43
  21.6 0.7 %copy.44 = bf16[1,1,16,4,256]{4,2,1,0,3:T(8,128)(2,1)} copy(bf16[1,1,16,4,256]{2,4,3,1,0:T(8,128)(2,1)S(1)} %bitcast.175) | data formatting | bytes 65536 | tf_op jit(solution)/shard_map/convert_element_type | solution.py:145
  22.3 5.0 %all-to-all-start.1 = ((bf16[1,1,16,4,256]{4,2,1,0,3:T(8,128)(2,1)}), bf16[1,1,16,4,256]{4,2,1,0,3:T(8,128)(2,1)S(1)}, u32[]{:S(2)}, u32[]{:S(2)}) async-start(bf16[1,1,16,4,256]{4,2,1,0,3:T(8,128)(2,1)} %copy.44), calls=%async_computation.1 | async-start | bytes 65536 | tf_op jit(solution)/shard_map/all_to_all | solution.py:146
  28.4 1.4 %mul.45 = f32[2,2,2,432,64]{3,2,1,0,4:T(2,128)S(1)} reshape(f32[3456,64]{0,1:T(8,128)S(1)} %maximum_multiply_fusion) | data formatting | bytes 1769472 | tf_op jit(solution)/shard_map/mul | solution.py:124
  29.8 1.1 %constant_dynamic-slice_fusion.3 = (f32[2,2,1,432,64]{3,2,1,0,4:T(1,128)S(1)}, f32[2,2,1,432,64]{3,2,1,0,4:T(1,128)S(1)}) fusion(f32[2,2,2,432,64]{3,2,1,0,4:T(2,128)S(1)} %mul.45, s32[]{:T(128)S(6)} %select_n.43, s32[]{:T(128)S(6)} %select_n.44), kind=kLoop, calls=%fused_computation.111 | loop fusion | bytes 1769480 | tf_op jit(solution)/shard_map/jit(dynamic_index_in_dim)/dynamic_slice | solution.py:90
  30.9 0.3 copy.57
  31.1 0.6 collective-permute-start.4
  31.9 0.7 %reshape.282 = bf16[1,1,64,2,64]{4,3,2,1,0:T(2,128)(2,1)} reshape(bf16[64,128]{1,0:T(8,128)(2,1)S(1)} %fusion.3) | data formatting | bytes 32768 | tf_op jit(solution)/shard_map/reshape | solution.py:121
  32.7 2.1 %collective-permute-start.2 = (f32[2,32,64]{2,1,0:T(8,128)S(1)}, f32[2,32,64]{2,1,0:T(8,128)S(1)}, u32[]{:S(2)}, u32[]{:S(2)}) collective-permute-start(f32[2,32,64]{2,1,0:T(8,128)S(1)} %dynamic-slice_bitcast_fusion.2), channel_id=1, source_target_pairs={{0,4},{4,0},{8,12},{12,8},{1,5},{5,1},{9,13},{13,9},{2,6},{6,2},{1... | collective-permute-start | bytes 49160 | tf_op jit(solution)/shard_map/ppermute | solution.py:93
  34.8 9.8 %collective-permute-done.4 = f32[2,2,432,64]{2,1,0,3:T(2,128)S(1)} collective-permute-done((f32[2,2,432,64]{2,1,0,3:T(2,128)S(1)}, f32[2,2,432,64]{2,1,0,3:T(2,128)S(1)}, u32[]{:S(2)}, u32[]{:S(2)}) %collective-permute-start.4) | collective-permute-done | bytes 442400 | tf_op jit(solution)/shard_map/ppermute | solution.py:93
  44.6 0.3 bitcast_add_fusion
  45.0 0.5 constant_dynamic-slice_fusion.1
  45.5 1.8 %collective-permute-start.5 = (f32[2,432,64]{1,2,0:T(8,128)S(1)}, f32[2,432,64]{1,2,0:T(8,128)S(1)}, u32[]{:S(2)}, u32[]{:S(2)}) collective-permute-start(f32[2,432,64]{1,2,0:T(8,128)S(1)} %bitcast.183), channel_id=1, source_target_pairs={{0,4},{4,0},{8,12},{12,8},{1,5},{5,1},{9,13},{13,9},{2,6},{6,2},{1... | collective-permute-start | bytes 663560 | tf_op jit(solution)/shard_map/ppermute | solution.py:93
  47.3 2.4 %collective-permute-start.3 = (f32[32,64]{1,0:T(8,128)S(1)}, f32[32,64]{1,0:T(8,128)S(1)}, u32[]{:S(2)}, u32[]{:S(2)}) collective-permute-start(f32[32,64]{1,0:T(8,128)S(1)} %dynamic-slice_bitcast_fusion.4), channel_id=1, source_target_pairs={{0,8},{4,12},{8,0},{12,4},{1,9},{5,13},{9,1},{13,5},{2,10},{6,14},... | collective-permute-start | bytes 24584 | tf_op jit(solution)/shard_map/ppermute | solution.py:93
  49.8 3.1 %collective-permute-done.5 = f32[2,432,64]{1,2,0:T(8,128)S(1)} collective-permute-done((f32[2,432,64]{1,2,0:T(8,128)S(1)}, f32[2,432,64]{1,2,0:T(8,128)S(1)}, u32[]{:S(2)}, u32[]{:S(2)}) %collective-permute-start.5) | collective-permute-done | bytes 221216 | tf_op jit(solution)/shard_map/ppermute | solution.py:93
  53.0 2.2 %collective-permute-start.6 = (f32[432,64]{0,1:T(8,128)S(1)}, f32[432,64]{0,1:T(8,128)S(1)}, u32[]{:S(2)}, u32[]{:S(2)}) collective-permute-start(f32[432,64]{0,1:T(8,128)S(1)} %dynamic-slice_bitcast_fusion), channel_id=1, source_target_pairs={{0,8},{4,12},{8,0},{12,4},{1,9},{5,13},{9,1},{13,5},{2,10},{6,14},... | collective-permute-start | bytes 331784 | tf_op jit(solution)/shard_map/ppermute | solution.py:93
  55.2 0.6 bitcast_add_fusion.6
  55.8 4.5 %collective-permute-done.6 = f32[432,64]{0,1:T(8,128)S(1)} collective-permute-done((f32[432,64]{0,1:T(8,128)S(1)}, f32[432,64]{0,1:T(8,128)S(1)}, u32[]{:S(2)}, u32[]{:S(2)}) %collective-permute-start.6) | collective-permute-done | bytes 110624 | tf_op jit(solution)/shard_map/ppermute | solution.py:93
  60.3 0.7 %bitcast_add_fusion.2 = f32[432,64]{0,1:T(8,128)} fusion(f32[432,64]{0,1:T(8,128)S(1)} %collective-permute-done.6, f32[2,432,64]{1,2,0:T(8,128)S(1)} %bitcast_add_fusion.1, s32[]{:T(128)S(6)} %select_n.47), kind=kLoop, calls=%fused_computation.67 | loop fusion | flops 27648 | bytes 331780 | tf_op jit(solution)/shard_map/add | solution.py:93
  61.0 0.6 copy.84
  (80 shorter events, 5.0 us)
Async XLA Ops:
  0.6 6.4 %copy-start.2 = (bf16[1,1,64,2,64]{4,3,2,1,0:T(2,128)(2,1)S(1)}, bf16[1,1,64,2,64]{4,3,2,1,0:T(2,128)(2,1)}, u32[]{:S(2)}) copy-start(bf16[1,1,64,2,64]{4,3,2,1,0:T(2,128)(2,1)} %param.5) | copy-start | bytes 49156
  0.6 12.1 %all-to-all-start = ((bf16[1,4,32,1,256]{4,2,3,0,1:T(8,128)(2,1)}), bf16[1,4,32,1,256]{4,2,3,0,1:T(8,128)(2,1)S(1)}, u32[]{:S(2)}, u32[]{:S(2)}) async-start(bf16[1,4,32,1,256]{4,2,3,0,1:T(8,128)(2,1)} %bitcast.244), calls=%async_computation | async-start | bytes 131072 | tf_op jit(solution)/shard_map/all_to_all | solution.py:108
  7.1 1.0 %copy-start = (bf16[3456,64]{0,1:T(8,128)(2,1)S(1)}, bf16[3456,64]{0,1:T(8,128)(2,1)}, u32[]{:S(2)}) copy-start(bf16[3456,64]{0,1:T(8,128)(2,1)} %param.7) | copy-start | bytes 1327108
  9.8 0.8 %copy-start.1 = (bf16[256,64]{0,1:T(8,128)(2,1)S(1)}, bf16[256,64]{0,1:T(8,128)(2,1)}, u32[]{:S(2)}) copy-start(bf16[256,64]{0,1:T(8,128)(2,1)} %param.6) | copy-start | bytes 98308
  9.9 3.5 %collective-permute-start = (f32[64,128]{1,0:T(8,128)S(1)}, f32[64,128]{1,0:T(8,128)S(1)}, u32[]{:S(2)}, u32[]{:S(2)}) collective-permute-start(f32[64,128]{1,0:T(8,128)S(1)} %dynamic-slice_bitcast_fusion.3), channel_id=1, source_target_pairs={{0,1},{1,0},{2,3},{3,2},{4,5},{5,4},{6,7},{7,6},{8,9},{9,8},{10,11... | collective-permute-start | bytes 98312 | tf_op jit(solution)/shard_map/ppermute | solution.py:93
  19.5 13.2 %collective-permute-start.1 = (f32[2,2,32,64]{3,2,1,0:T(8,128)S(1)}, f32[2,2,32,64]{3,2,1,0:T(8,128)S(1)}, u32[]{:S(2)}, u32[]{:S(2)}) collective-permute-start(f32[2,2,32,64]{3,2,1,0:T(8,128)S(1)} %dynamic-slice_bitcast_fusion.1), channel_id=1, source_target_pairs={{0,2},{2,0},{1,3},{3,1},{4,6},{6,4},{5,7},{7,5},{8,10},{10,8},{9,1... | collective-permute-start | bytes 98312 | tf_op jit(solution)/shard_map/ppermute | solution.py:93
  22.3 27.4 %all-to-all-start.1 = ((bf16[1,1,16,4,256]{4,2,1,0,3:T(8,128)(2,1)}), bf16[1,1,16,4,256]{4,2,1,0,3:T(8,128)(2,1)S(1)}, u32[]{:S(2)}, u32[]{:S(2)}) async-start(bf16[1,1,16,4,256]{4,2,1,0,3:T(8,128)(2,1)} %copy.44), calls=%async_computation.1 | async-start | bytes 65536 | tf_op jit(solution)/shard_map/all_to_all | solution.py:146
  31.1 13.5 %collective-permute-start.4 = (f32[2,2,432,64]{2,1,0,3:T(2,128)S(1)}, f32[2,2,432,64]{2,1,0,3:T(2,128)S(1)}, u32[]{:S(2)}, u32[]{:S(2)}) collective-permute-start(f32[2,2,432,64]{2,1,0,3:T(2,128)S(1)} %bitcast.181), channel_id=1, source_target_pairs={{0,2},{2,0},{1,3},{3,1},{4,6},{6,4},{5,7},{7,5},{8,10},{10,8},{9,1... | collective-permute-start | bytes 1327112 | tf_op jit(solution)/shard_map/ppermute | solution.py:93
  32.7 14.6 %collective-permute-start.2 = (f32[2,32,64]{2,1,0:T(8,128)S(1)}, f32[2,32,64]{2,1,0:T(8,128)S(1)}, u32[]{:S(2)}, u32[]{:S(2)}) collective-permute-start(f32[2,32,64]{2,1,0:T(8,128)S(1)} %dynamic-slice_bitcast_fusion.2), channel_id=1, source_target_pairs={{0,4},{4,0},{8,12},{12,8},{1,5},{5,1},{9,13},{13,9},{2,6},{6,2},{1... | collective-permute-start | bytes 49160 | tf_op jit(solution)/shard_map/ppermute | solution.py:93
  45.5 7.4 %collective-permute-start.5 = (f32[2,432,64]{1,2,0:T(8,128)S(1)}, f32[2,432,64]{1,2,0:T(8,128)S(1)}, u32[]{:S(2)}, u32[]{:S(2)}) collective-permute-start(f32[2,432,64]{1,2,0:T(8,128)S(1)} %bitcast.183), channel_id=1, source_target_pairs={{0,4},{4,0},{8,12},{12,8},{1,5},{5,1},{9,13},{13,9},{2,6},{6,2},{1... | collective-permute-start | bytes 663560 | tf_op jit(solution)/shard_map/ppermute | solution.py:93
  47.3 7.9 %collective-permute-start.3 = (f32[32,64]{1,0:T(8,128)S(1)}, f32[32,64]{1,0:T(8,128)S(1)}, u32[]{:S(2)}, u32[]{:S(2)}) collective-permute-start(f32[32,64]{1,0:T(8,128)S(1)} %dynamic-slice_bitcast_fusion.4), channel_id=1, source_target_pairs={{0,8},{4,12},{8,0},{12,4},{1,9},{5,13},{9,1},{13,5},{2,10},{6,14},... | collective-permute-start | bytes 24584 | tf_op jit(solution)/shard_map/ppermute | solution.py:93
  53.0 7.3 %collective-permute-start.6 = (f32[432,64]{0,1:T(8,128)S(1)}, f32[432,64]{0,1:T(8,128)S(1)}, u32[]{:S(2)}, u32[]{:S(2)}) collective-permute-start(f32[432,64]{0,1:T(8,128)S(1)} %dynamic-slice_bitcast_fusion), channel_id=1, source_target_pairs={{0,8},{4,12},{8,0},{12,4},{1,9},{5,13},{9,1},{13,5},{2,10},{6,14},... | collective-permute-start | bytes 331784 | tf_op jit(solution)/shard_map/ppermute | solution.py:93

commit v2 on v1

--- a/solution.py
+++ b/solution.py
@@ -95,6 +95,41 @@
     return x
 
 
+def doubling_gather(x, names):
+    for name in reversed(names):
+        size = lax.axis_size(name)
+        for j in range(size.bit_length() - 1):
+            perm = [(i, i ^ (1 << j)) for i in range(size)]
+            x = jnp.concatenate([x, lax.ppermute(x, name, perm)], axis=0)
+    return x
+
+
+def second_grad_rows(hidden_all, cot_all, names, total_rows):
+    count, chans, depth, side = hidden_all.shape[0], hidden_all.shape[1], hidden_all.shape[2], hidden_all.shape[3]
+    shards = math.prod(lax.axis_size(n) for n in names)
+    rows = total_rows // shards
+    index = 0
+    for name in names:
+        index = index * lax.axis_size(name) + lax.axis_index(name)
+    first = index * rows
+    tap0 = first // chans
+    taps = min(27, (rows + 2 * chans - 2) // chans)
+    padded = jnp.pad(hidden_all, ((0, 0), (0, 0), (1, 1), (1, 1), (1, 1)))
+    pieces = []
+    for slot in range(taps):
+        tap = jnp.minimum(tap0 + slot, 26)
+        window = lax.dynamic_slice(
+            padded, (0, 0, tap // 9, (tap // 3) % 3, tap % 3), (count, chans, depth, side, side)
+        ).reshape(count, chans, depth * side * side)
+        pieces.append(
+            lax.dot_general(
+                window, cot_all, (((0, 2), (0, 2)), ((), ())), preferred_element_type=jnp.float32
+            )
+        )
+    stacked = jnp.concatenate(pieces, axis=0)
+    return lax.dynamic_slice_in_dim(stacked, first - tap0 * chans, rows, 0)
+
+
 def silu_slope(pre):
     sig = jax.nn.sigmoid(pre)
     return sig * (1.0 + pre * (1.0 - sig))
@@ -121,7 +156,23 @@
     block_out = out.astype(jnp.bfloat16).reshape(1, 1, half_o, half_z, half_s * half_s)
     cot = cotangent.reshape(half_o, voxels)
     factor = 1.0 / math.sqrt(lax.axis_size("space") * lax.axis_size("sub") * voxels)
-    grad_second = conv_weight_grad(grid, cot) * factor
+    shards = lax.axis_size("space") * lax.axis_size("sub")
+    gather_second = shards * (width + half_o) * voxels * 2 <= 1 << 22
+    if gather_second:
+        both = doubling_gather(
+            jnp.concatenate([grid.reshape(width, voxels), cot], axis=0)[None], ("space", "sub")
+        )
+        grad_second = (
+            second_grad_rows(
+                both[:, :width].reshape(both.shape[0], width, half_z, half_s, half_s),
+                both[:, width:],
+                ("space", "sub"),
+                second_weight.shape[0],
+            )
+            * factor
+        )
+    else:
+        grad_second = conv_weight_grad(grid, cot) * factor
     cot_grid = cot.reshape(half_o, half_z, half_s, half_s)
     local_rows = second_weight.reshape(27, width, half_o)
     hidden_grad = halving_scatter(conv_back(cot_grid, local_rows), ("ch",))
@@ -152,7 +203,7 @@
     )
     first_grad, second_grad = (
         halving_scatter(grad_first, ("space", "sub")),
-        halving_scatter(grad_second, ("space", "sub")),
+        grad_second if gather_second else halving_scatter(grad_second, ("space", "sub")),
     )
     return (block_out, volume_grad, first_grad, second_grad)
 

time: 62.1 us -> 54.7 us (0.88)
  waiting for transfers between devices: 17.6 us -> 13.9 us
  local copies, waits for them, and re-layouts: 10.5 us -> 8.24 us
  starting transfers between devices: 22.1 us -> 20.3 us
    ppermute x7 -> x4, waiting for transfers between devices: 17.4 us -> 1.55 us  [halving_scatter(): x = mine + lax.ppermute(other, name, perm)]
    ppermute x0 -> x3, waiting for transfers between devices: none -> 8.98 us  [doubling_gather(): x = jnp.concatenate([x, lax.ppermute(x, name, perm)], axis=0)]
    ppermute x0 -> x3, starting transfers between devices: none -> 4.16 us  [doubling_gather(): x = jnp.concatenate([x, lax.ppermute(x, name, perm)], axis=0)]
    ppermute x7 -> x4, starting transfers between devices: 10.8 us -> 6.98 us  [halving_scatter(): x = mine + lax.ppermute(other, name, perm)]
    all_to_all x1, waiting for transfers between devices: 0.15 us -> 3.33 us  [body(): lax.all_to_all(volumes, 'space', split_axis=1, concat_axis=3, tiled=True)]
    all_to_all x1, starting transfers between devices: 4.96 us -> 3.26 us  [body(): lax.all_to_all(grad_sample.reshape(1, 1, half_c, depth, XY * XY), 'space'...]
    mul x1 -> x0, local copies, waits for them, and re-layouts: 1.37 us -> none  [body(): grad_second = conv_weight_grad(grid, cot) * factor]
    add x6 -> x3, other arithmetic: 1.71 us -> 0.63 us  [halving_scatter(): x = mine + lax.ppermute(other, name, perm)]
  transfers between devices with their start and end apart: 9 -> 9, of which waited for: 4 -> 5; matrix products, arithmetic and copies ran while one was open for 16% -> 8% of each run, Pallas kernels for 0% -> 0%
where the time goes in v2:
time: 54.7 us; the launch traced here: 54.3 us
  starting transfers between devices  20.3 us (37%)
  waiting for transfers between devices  13.9 us (25%)
  local copies, waits for them, and re-layouts  8.24 us (15%)
  blocking collectives  5.85 us (11%)
  matrix products  2.88 us (5%)
  between operations  1.71 us (3%)
  other arithmetic  1.46 us (3%)
    ppermute x3, waiting for transfers between devices, doubling_gather(): x = jnp.concatenate([x, lax.ppermute(x, name, perm)], axis=0)  8.98 us
    ppermute x4, starting transfers between devices, halving_scatter(): x = mine + lax.ppermute(other, name, perm)  6.98 us
    all_to_all x1, starting transfers between devices, body(): lax.all_to_all(volumes, 'space', split_axis=1, concat_axis=3, tiled=True)  5.88 us
    ppermute x3, starting transfers between devices, doubling_gather(): x = jnp.concatenate([x, lax.ppermute(x, name, perm)], axis=0)  4.16 us
    all_to_all x1, waiting for transfers between devices, body(): lax.all_to_all(volumes, 'space', split_axis=1, concat_axis=3, tiled=True)  3.33 us
    all_to_all x1, starting transfers between devices, body(): lax.all_to_all(grad_sample.reshape(1, 1, half_c, depth, XY * XY), 'space'...  3.26 us
    all_gather x1, blocking collectives, body(): lax.all_gather(hidden.reshape(half_o, half_z, half_s, half_s), 'ch', axis...  2.18 us
    unnamed x40, local copies, waits for them, and re-layouts  1.97 us
  transfers between devices with their start and end apart: 9, of which 5 were waited for; matrix products, arithmetic and copies ran while one was open for 8% of the time, Pallas kernels for 0%

profile of v2, /device:TPU:0, one launch (start us, length us, event | category | flops | bytes accessed | tf_op | source)
XLA Modules:
  0.0 54.3 jit_solution(1986381209264989773)
XLA Ops:
  0.7 0.9 %copy.47 = bf16[1,1,64,2,64]{2,4,3,1,0:T(8,128)(2,1)S(1)} copy(bf16[1,1,64,2,64]{4,3,2,1,0:T(2,128)(2,1)} %param.5) | data formatting | bytes 32768 | tf_op args[1]
  3.3 0.3 fusion.18
  3.7 0.3 fusion.17
  4.1 0.3 fusion.2
  4.4 0.6 %collective-permute-start = (f32[64,128]{1,0:T(8,128)S(1)}, f32[64,128]{1,0:T(8,128)S(1)}, u32[]{:S(2)}, u32[]{:S(2)}) collective-permute-start(f32[64,128]{1,0:T(8,128)S(1)} %dynamic-slice_bitcast_fusion.2), channel_id=1, source_target_pairs={{0,1},{1,0},{2,3},{3,2},{4,5},{5,4},{6,7},{7,6},{8,9},{9,8},{10,11... | collective-permute-start | bytes 98312 | tf_op jit(solution)/shard_map/ppermute | solution.py:93
  4.9 5.9 %all-to-all-start = ((bf16[1,4,32,1,256]{4,2,3,0,1:T(8,128)(2,1)}), bf16[1,4,32,1,256]{4,2,3,0,1:T(8,128)(2,1)S(1)}, u32[]{:S(2)}, u32[]{:S(2)}) async-start(bf16[1,4,32,1,256]{4,2,3,0,1:T(8,128)(2,1)} %bitcast), calls=%async_computation | async-start | bytes 131072 | tf_op jit(solution)/shard_map/all_to_all | solution.py:143
  10.8 1.8 %all_gather.10 = bf16[256,128]{0,1:T(8,128)(2,1)S(1)} all-gather(bf16[256,64]{0,1:T(8,128)(2,1)S(1)} %copy-done.2), channel_id=1, replica_groups=mesh['groups'=2,'space'=4,'sub'=2,'ch'=2] {'ch'}, dimensions={1}, use_global_device_ids=true | all-gather | bytes 98304 | tf_op jit(solution)/shard_map/all_gather | solution.py:188
  13.2 3.3 %all-to-all-done = bf16[1,4,32,1,256]{4,2,3,0,1:T(8,128)(2,1)S(1)} async-done(((bf16[1,4,32,1,256]{4,2,3,0,1:T(8,128)(2,1)}), bf16[1,4,32,1,256]{4,2,3,0,1:T(8,128)(2,1)S(1)}, u32[]{:S(2)}, u32[]{:S(2)}) %all-to-all-start) | async-done | bytes 65568 | tf_op jit(solution)/shard_map/all_to_all | solution.py:143
  16.7 0.2 copy.41
  17.5 0.3 copy.43
  17.8 2.2 %all_gather.9 = bf16[128,2,8,8]{3,2,1,0:T(8,128)(2,1)S(1)} all-gather(bf16[64,2,8,8]{3,2,1,0:T(8,128)(2,1)S(1)} %copy.43), channel_id=1, replica_groups=mesh['groups'=2,'space'=4,'sub'=2,'ch'=2] {'ch'}, dimensions={0}, use_global_device_ids=true | all-gather | bytes 49152 | tf_op jit(solution)/shard_map/all_gather | solution.py:153
  19.9 0.4 copy.44
  20.5 1.8 %all_gather.11 = bf16[128,128]{1,0:T(8,128)(2,1)S(1)} all-gather(bf16[64,128]{1,0:T(8,128)(2,1)S(1)} %get-tuple-element.19), channel_id=1, replica_groups=mesh['groups'=2,'space'=4,'sub'=2,'ch'=2] {'ch'}, dimensions={0}, use_global_device_ids=true | all-gather | bytes 49152 | tf_op jit(solution)/shard_map/all_gather | solution.py:187
  22.6 0.2 fusion.14
  23.2 1.6 %collective-permute-start.1 = (f32[2,2,32,64]{3,2,1,0:T(8,128)S(1)}, f32[2,2,32,64]{3,2,1,0:T(8,128)S(1)}, u32[]{:S(2)}, u32[]{:S(2)}) collective-permute-start(f32[2,2,32,64]{3,2,1,0:T(8,128)S(1)} %dynamic-slice_bitcast_fusion), channel_id=1, source_target_pairs={{0,2},{2,0},{1,3},{3,1},{4,6},{6,4},{5,7},{7,5},{8,10},{10,8},{9,1... | collective-permute-start | bytes 98312 | tf_op jit(solution)/shard_map/ppermute | solution.py:93
  25.4 0.3 fusion
  25.8 0.7 %reshape.270 = bf16[1,1,64,2,64]{4,3,2,1,0:T(2,128)(2,1)} reshape(bf16[64,128]{1,0:T(8,128)(2,1)S(1)} %fusion.9) | data formatting | bytes 32768 | tf_op jit(solution)/shard_map/reshape | solution.py:156
  26.6 0.3 copy.60
  26.8 0.7 %copy.61 = bf16[1,1,16,4,256]{4,2,1,0,3:T(8,128)(2,1)} copy(bf16[1,1,16,4,256]{2,4,3,1,0:T(8,128)(2,1)S(1)} %bitcast.191) | data formatting | bytes 65536 | tf_op jit(solution)/shard_map/convert_element_type | solution.py:196
  27.6 3.3 %all-to-all-start.1 = ((bf16[1,1,16,4,256]{4,2,1,0,3:T(8,128)(2,1)}), bf16[1,1,16,4,256]{4,2,1,0,3:T(8,128)(2,1)S(1)}, u32[]{:S(2)}, u32[]{:S(2)}) async-start(bf16[1,1,16,4,256]{4,2,1,0,3:T(8,128)(2,1)} %copy.61), calls=%async_computation.1 | async-start | bytes 65536 | tf_op jit(solution)/shard_map/all_to_all | solution.py:197
  30.9 2.0 %collective-permute-start.2 = (f32[2,32,64]{2,1,0:T(8,128)S(1)}, f32[2,32,64]{2,1,0:T(8,128)S(1)}, u32[]{:S(2)}, u32[]{:S(2)}) collective-permute-start(f32[2,32,64]{2,1,0:T(8,128)S(1)} %dynamic-slice_bitcast_fusion.1), channel_id=1, source_target_pairs={{0,4},{4,0},{8,12},{12,8},{1,5},{5,1},{9,13},{13,9},{2,6},{6,2},{1... | collective-permute-start | bytes 49160 | tf_op jit(solution)/shard_map/ppermute | solution.py:93
  32.9 0.5 collective-permute-start.4
  33.5 1.5 %collective-permute-done.2 = f32[2,32,64]{2,1,0:T(8,128)S(1)} collective-permute-done((f32[2,32,64]{2,1,0:T(8,128)S(1)}, f32[2,32,64]{2,1,0:T(8,128)S(1)}, u32[]{:S(2)}, u32[]{:S(2)}) %collective-permute-start.2) | collective-permute-done | bytes 16416 | tf_op jit(solution)/shard_map/ppermute | solution.py:93
  35.0 2.0 %collective-permute-done.4 = bf16[1,192,128]{2,1,0:T(8,128)(2,1)S(1)} collective-permute-done((bf16[1,192,128]{2,1,0:T(8,128)(2,1)S(1)}, bf16[1,192,128]{2,1,0:T(8,128)(2,1)S(1)}, u32[]{:S(2)}, u32[]{:S(2)}) %collective-permute-start.4) | collective-permute-done | bytes 49184 | tf_op jit(solution)/shard_map/ppermute | solution.py:103
  37.2 2.8 %collective-permute-start.3 = (f32[32,64]{1,0:T(8,128)S(1)}, f32[32,64]{1,0:T(8,128)S(1)}, u32[]{:S(2)}, u32[]{:S(2)}) collective-permute-start(f32[32,64]{1,0:T(8,128)S(1)} %dynamic-slice_bitcast_fusion.3), channel_id=1, source_target_pairs={{0,8},{4,12},{8,0},{12,4},{1,9},{5,13},{9,1},{13,5},{2,10},{6,14},... | collective-permute-start | bytes 24584 | tf_op jit(solution)/shard_map/ppermute | solution.py:93
  40.0 1.7 %collective-permute-done.5 = bf16[2,192,128]{2,1,0:T(8,128)(2,1)S(1)} collective-permute-done((bf16[2,192,128]{2,1,0:T(8,128)(2,1)S(1)}, bf16[2,192,128]{2,1,0:T(8,128)(2,1)S(1)}, u32[]{:S(2)}, u32[]{:S(2)}) %collective-permute-start.5) | collective-permute-done | bytes 98336 | tf_op jit(solution)/shard_map/ppermute | solution.py:103
  41.8 3.5 %collective-permute-start.6 = (bf16[4,192,128]{2,1,0:T(8,128)(2,1)S(1)}, bf16[4,192,128]{2,1,0:T(8,128)(2,1)S(1)}, u32[]{:S(2)}, u32[]{:S(2)}) collective-permute-start(bf16[4,192,128]{2,1,0:T(8,128)(2,1)S(1)} %pad_maximum_fusion.3), channel_id=1, source_target_pairs={{0,8},{4,12},{8,0},{12,4},{1,9},{5,13},{9,1},{13,5},{2,10},{6,14},... | collective-permute-start | bytes 589832 | tf_op jit(solution)/shard_map/ppermute | solution.py:103
  45.2 0.6 %bitcast_add_fusion.3 = f32[32,64]{1,0:T(8,128)} fusion(f32[32,64]{1,0:T(8,128)S(1)} %collective-permute-done.3, f32[2,32,64]{2,1,0:T(8,128)S(1)} %bitcast_add_fusion.1, s32[]{:T(128)S(6)} %select_n.163), kind=kLoop, calls=%fused_computation.131 | loop fusion | flops 2048 | bytes 24580 | tf_op jit(solution)/shard_map/add | solution.py:93
  45.8 5.3 %collective-permute-done.6 = bf16[4,192,128]{2,1,0:T(8,128)(2,1)S(1)} collective-permute-done((bf16[4,192,128]{2,1,0:T(8,128)(2,1)S(1)}, bf16[4,192,128]{2,1,0:T(8,128)(2,1)S(1)}, u32[]{:S(2)}, u32[]{:S(2)}) %collective-permute-start.6) | collective-permute-done | bytes 196640 | tf_op jit(solution)/shard_map/ppermute | solution.py:103
  51.7 0.5 pad_dynamic-slice_fusion
  52.9 0.8 %dynamic-slice_multiply_fusion = f32[432,64]{0,1:T(8,128)} fusion(f32[640,64]{0,1:T(8,128)S(1)} %fusion.3, s32[]{:T(128)S(6)} %select_n.201), kind=kLoop, calls=%fused_computation.82 | loop fusion | flops 27648 | bytes 221188 | tf_op jit(solution)/shard_map/mul | solution.py:166
  53.7 0.6 %copy.115 = bf16[1,4,16,1,256]{4,2,3,1,0:T(8,128)(2,1)} copy(bf16[1,4,16,1,256]{4,2,3,1,0:T(8,128)(2,1)S(1)} %bitcast.252) | data formatting | bytes 65536
  (99 shorter events, 5.4 us)
Async XLA Ops:
  0.6 1.1 %copy-start.1 = (bf16[1,1,64,2,64]{4,3,2,1,0:T(2,128)(2,1)S(1)}, bf16[1,1,64,2,64]{4,3,2,1,0:T(2,128)(2,1)}, u32[]{:S(2)}) copy-start(bf16[1,1,64,2,64]{4,3,2,1,0:T(2,128)(2,1)} %param.5) | copy-start | bytes 49156
  0.6 1.2 %copy-start = (bf16[3456,64]{0,1:T(8,128)(2,1)S(1)}, bf16[3456,64]{0,1:T(8,128)(2,1)}, u32[]{:S(2)}) copy-start(bf16[3456,64]{0,1:T(8,128)(2,1)} %param.7) | copy-start | bytes 1327108
  4.0 6.9 %copy-start.2 = (bf16[256,64]{0,1:T(8,128)(2,1)S(1)}, bf16[256,64]{0,1:T(8,128)(2,1)}, u32[]{:S(2)}) copy-start(bf16[256,64]{0,1:T(8,128)(2,1)} %param.6) | copy-start | bytes 98308
  4.4 12.8 %collective-permute-start = (f32[64,128]{1,0:T(8,128)S(1)}, f32[64,128]{1,0:T(8,128)S(1)}, u32[]{:S(2)}, u32[]{:S(2)}) collective-permute-start(f32[64,128]{1,0:T(8,128)S(1)} %dynamic-slice_bitcast_fusion.2), channel_id=1, source_target_pairs={{0,1},{1,0},{2,3},{3,2},{4,5},{5,4},{6,7},{7,6},{8,9},{9,8},{10,11... | collective-permute-start | bytes 98312 | tf_op jit(solution)/shard_map/ppermute | solution.py:93
  4.9 11.6 %all-to-all-start = ((bf16[1,4,32,1,256]{4,2,3,0,1:T(8,128)(2,1)}), bf16[1,4,32,1,256]{4,2,3,0,1:T(8,128)(2,1)S(1)}, u32[]{:S(2)}, u32[]{:S(2)}) async-start(bf16[1,4,32,1,256]{4,2,3,0,1:T(8,128)(2,1)} %bitcast), calls=%async_computation | async-start | bytes 131072 | tf_op jit(solution)/shard_map/all_to_all | solution.py:143
  23.2 7.7 %collective-permute-start.1 = (f32[2,2,32,64]{3,2,1,0:T(8,128)S(1)}, f32[2,2,32,64]{3,2,1,0:T(8,128)S(1)}, u32[]{:S(2)}, u32[]{:S(2)}) collective-permute-start(f32[2,2,32,64]{3,2,1,0:T(8,128)S(1)} %dynamic-slice_bitcast_fusion), channel_id=1, source_target_pairs={{0,2},{2,0},{1,3},{3,1},{4,6},{6,4},{5,7},{7,5},{8,10},{10,8},{9,1... | collective-permute-start | bytes 98312 | tf_op jit(solution)/shard_map/ppermute | solution.py:93
  27.6 12.5 %all-to-all-start.1 = ((bf16[1,1,16,4,256]{4,2,1,0,3:T(8,128)(2,1)}), bf16[1,1,16,4,256]{4,2,1,0,3:T(8,128)(2,1)S(1)}, u32[]{:S(2)}, u32[]{:S(2)}) async-start(bf16[1,1,16,4,256]{4,2,1,0,3:T(8,128)(2,1)} %copy.61), calls=%async_computation.1 | async-start | bytes 65536 | tf_op jit(solution)/shard_map/all_to_all | solution.py:197
  30.9 4.1 %collective-permute-start.2 = (f32[2,32,64]{2,1,0:T(8,128)S(1)}, f32[2,32,64]{2,1,0:T(8,128)S(1)}, u32[]{:S(2)}, u32[]{:S(2)}) collective-permute-start(f32[2,32,64]{2,1,0:T(8,128)S(1)} %dynamic-slice_bitcast_fusion.1), channel_id=1, source_target_pairs={{0,4},{4,0},{8,12},{12,8},{1,5},{5,1},{9,13},{13,9},{2,6},{6,2},{1... | collective-permute-start | bytes 49160 | tf_op jit(solution)/shard_map/ppermute | solution.py:93
  32.9 4.1 %collective-permute-start.4 = (bf16[1,192,128]{2,1,0:T(8,128)(2,1)S(1)}, bf16[1,192,128]{2,1,0:T(8,128)(2,1)S(1)}, u32[]{:S(2)}, u32[]{:S(2)}) collective-permute-start(bf16[1,192,128]{2,1,0:T(8,128)(2,1)S(1)} %maximum_bitcast_fusion), channel_id=1, source_target_pairs={{0,2},{2,0},{1,3},{3,1},{4,6},{6,4},{5,7},{7,5},{8,10},{10,8},{9,1... | collective-permute-start | bytes 147464 | tf_op jit(solution)/shard_map/ppermute | solution.py:103
  37.0 4.7 %collective-permute-start.5 = (bf16[2,192,128]{2,1,0:T(8,128)(2,1)S(1)}, bf16[2,192,128]{2,1,0:T(8,128)(2,1)S(1)}, u32[]{:S(2)}, u32[]{:S(2)}) collective-permute-start(bf16[2,192,128]{2,1,0:T(8,128)(2,1)S(1)} %pad_maximum_fusion.5), channel_id=1, source_target_pairs={{0,4},{4,0},{8,12},{12,8},{1,5},{5,1},{9,13},{13,9},{2,6},{6,2},{1... | collective-permute-start | bytes 294920 | tf_op jit(solution)/shard_map/ppermute | solution.py:103
  37.2 8.0 %collective-permute-start.3 = (f32[32,64]{1,0:T(8,128)S(1)}, f32[32,64]{1,0:T(8,128)S(1)}, u32[]{:S(2)}, u32[]{:S(2)}) collective-permute-start(f32[32,64]{1,0:T(8,128)S(1)} %dynamic-slice_bitcast_fusion.3), channel_id=1, source_target_pairs={{0,8},{4,12},{8,0},{12,4},{1,9},{5,13},{9,1},{13,5},{2,10},{6,14},... | collective-permute-start | bytes 24584 | tf_op jit(solution)/shard_map/ppermute | solution.py:93
  41.8 9.4 %collective-permute-start.6 = (bf16[4,192,128]{2,1,0:T(8,128)(2,1)S(1)}, bf16[4,192,128]{2,1,0:T(8,128)(2,1)S(1)}, u32[]{:S(2)}, u32[]{:S(2)}) collective-permute-start(bf16[4,192,128]{2,1,0:T(8,128)(2,1)S(1)} %pad_maximum_fusion.3), channel_id=1, source_target_pairs={{0,8},{4,12},{8,0},{12,4},{1,9},{5,13},{9,1},{13,5},{2,10},{6,14},... | collective-permute-start | bytes 589832 | tf_op jit(solution)/shard_map/ppermute | solution.py:103

commit v3 on v2

--- a/solution.py
+++ b/solution.py
@@ -4,6 +4,7 @@
 import jax.numpy as jnp
 from jax import lax
 from jax.sharding import PartitionSpec as P
+
 
 XY = 16
 
@@ -50,7 +51,7 @@
 
 
 def conv_weight_grad(hidden, cot):
-    chans, depth, side = (hidden.shape[0], hidden.shape[1], hidden.shape[2])
+    depth, side = (hidden.shape[1], hidden.shape[2])
     padded = jnp.pad(hidden, ((0, 0), (1, 1), (1, 1), (1, 1)))
     pieces = []
     for plane in range(3):
@@ -64,7 +65,7 @@
 
 
 def conv_back(cot, weight_rows):
-    chans, depth, side = (cot.shape[0], cot.shape[1], cot.shape[2])
+    depth, side = (cot.shape[1], cot.shape[2])
     padded = jnp.pad(cot, ((0, 0), (1, 1), (1, 1), (1, 1)))
     total = jnp.zeros((weight_rows.shape[1], depth * side * side), jnp.float32)
     for plane in range(3):
@@ -92,15 +93,6 @@
             perm = [(i, i ^ (1 << j)) for i in range(size)]
             x = mine + lax.ppermute(other, name, perm)
             labels.pop(pos)
-    return x
-
-
-def doubling_gather(x, names):
-    for name in reversed(names):
-        size = lax.axis_size(name)
-        for j in range(size.bit_length() - 1):
-            perm = [(i, i ^ (1 << j)) for i in range(size)]
-            x = jnp.concatenate([x, lax.ppermute(x, name, perm)], axis=0)
     return x
 
 
@@ -130,12 +122,40 @@
     return lax.dynamic_slice_in_dim(stacked, first - tap0 * chans, rows, 0)
 
 
+def group_index(names):
+    index = 0
+    for name in names:
+        index = index * lax.axis_size(name) + lax.axis_index(name)
+    return index
+
+
+def direct_gather(x, names):
+    count = math.prod(lax.axis_size(n) for n in names)
+    pieces = [x]
+    for d in range(1, count):
+        pieces.append(lax.ppermute(x, names, [(k, k ^ d) for k in range(count)]))
+    return jnp.concatenate(pieces, axis=0)
+
+
+def direct_scatter(x, names):
+    count = math.prod(lax.axis_size(n) for n in names)
+    if count > 8:
+        return halving_scatter(x, names)
+    index = group_index(names)
+    blocks = x.reshape((count, x.shape[0] // count) + x.shape[1:])
+    total = lax.dynamic_index_in_dim(blocks, index, keepdims=False)
+    for d in range(1, count):
+        piece = lax.dynamic_index_in_dim(blocks, index ^ d, keepdims=False)
+        total = total + lax.ppermute(piece, names, [(k, k ^ d) for k in range(count)])
+    return total
+
+
 def silu_slope(pre):
     sig = jax.nn.sigmoid(pre)
     return sig * (1.0 + pre * (1.0 - sig))
 
 
-def body(volumes, cotangent, first_weight, second_weight):
+def block(volumes, cotangent, first_weight, second_weight):
     chans = volumes.shape[2]
     half_c = chans // lax.axis_size("ch")
     pair_index = lax.axis_index("ch")
@@ -159,7 +179,7 @@
     shards = lax.axis_size("space") * lax.axis_size("sub")
     gather_second = shards * (width + half_o) * voxels * 2 <= 1 << 22
     if gather_second:
-        both = doubling_gather(
+        both = direct_gather(
             jnp.concatenate([grid.reshape(width, voxels), cot], axis=0)[None], ("space", "sub")
         )
         grad_second = (
@@ -183,10 +203,8 @@
         )
         * factor
     )
-    all_pre_grad, all_first = (
-        lax.all_gather(pre_grad, "ch", axis=0, tiled=True),
-        lax.all_gather(first_weight, "ch", axis=1, tiled=True),
-    )
+    all_pre_grad = lax.all_gather(pre_grad, "ch", axis=0, tiled=True)
+    all_first = lax.all_gather(first_weight, "ch", axis=1, tiled=True)
     first_rows = lax.dynamic_slice_in_dim(
         all_first.reshape(8, chans, width), pair_index * half_c, half_c, 1
     )
@@ -201,16 +219,20 @@
         concat_axis=1,
         tiled=True,
     )
-    first_grad, second_grad = (
-        halving_scatter(grad_first, ("space", "sub")),
-        grad_second if gather_second else halving_scatter(grad_second, ("space", "sub")),
+    first_grad = direct_scatter(grad_first, ("space", "sub"))
+    second_grad = (
+        grad_second if gather_second else halving_scatter(grad_second, ("space", "sub"))
     )
     return (block_out, volume_grad, first_grad, second_grad)
 
 
 def solution(mesh):
+    return step_of(mesh)
+
+
+def step_of(mesh):
     return jax.shard_map(
-        body,
+        block,
         mesh=mesh,
         in_specs=(
             P(("groups", "sub"), None, None, "space", None),

time: 54.7 us -> 62.8 us (1.15)
  starting transfers between devices: 20.3 us -> 32.2 us
  waiting for transfers between devices: 13.9 us -> 9.91 us
    ppermute x3 -> x14, starting transfers between devices: 4.16 us -> 22.5 us  [the longest x7 11.3 us: direct_gather(): pieces.append(lax.ppermute(x, names, [(k, k ^ d) for k in range(count)]))]
    ppermute x4 -> x1, starting transfers between devices: 6.98 us -> 0.56 us  [halving_scatter(): x = mine + lax.ppermute(other, name, perm)]
    ppermute x3 -> x14, waiting for transfers between devices: 8.98 us -> 6.63 us  [the longest x7 6.62 us: direct_gather(): pieces.append(lax.ppermute(x, names, [(k, k ^ d) for k in range(count)]))]
    ppermute x4 -> x1, waiting for transfers between devices: 1.55 us -> 0.01 us  [halving_scatter(): x = mine + lax.ppermute(other, name, perm)]
    unnamed x40 -> x46, local copies, waits for them, and re-layouts: 1.97 us -> 2.03 us
  transfers between devices with their start and end apart: 9 -> 17, of which waited for: 5 -> 4; matrix products, arithmetic and copies ran while one was open for 8% -> 6% of each run, Pallas kernels for 0% -> 0%
where the time goes in v3:
time: 62.8 us; the launch traced here: 62.4 us
  starting transfers between devices  32.2 us (51%)
  waiting for transfers between devices  9.91 us (16%)
  local copies, waits for them, and re-layouts  8.32 us (13%)
  blocking collectives  5.85 us (9%)
  matrix products  2.88 us (5%)
  between operations  1.81 us (3%)
  other arithmetic  1.39 us (2%)
    ppermute x7, starting transfers between devices, direct_gather(): pieces.append(lax.ppermute(x, names, [(k, k ^ d) for k in range(count)]))  11.3 us
    ppermute x7, starting transfers between devices, direct_scatter(): lax.ppermute(piece, names, [(k, k ^ d) for k in range(count)])  11.2 us
    ppermute x7, waiting for transfers between devices, direct_gather(): pieces.append(lax.ppermute(x, names, [(k, k ^ d) for k in range(count)]))  6.62 us
    all_to_all x1, starting transfers between devices, block(): lax.all_to_all(volumes, 'space', split_axis=1, concat_axis=3, tiled=True)  5.88 us
    all_to_all x1, waiting for transfers between devices, block(): lax.all_to_all(volumes, 'space', split_axis=1, concat_axis=3, tiled=True)  3.27 us
    all_to_all x1, starting transfers between devices, block(): lax.all_to_all(grad_sample.reshape(1, 1, half_c, depth, XY * XY), 'space'...  3.26 us
    all_gather x1, blocking collectives, block(): lax.all_gather(hidden.reshape(half_o, half_z, half_s, half_s), 'ch', axis...  2.18 us
    unnamed x46, local copies, waits for them, and re-layouts  2.03 us
  transfers between devices with their start and end apart: 17, of which 4 were waited for; matrix products, arithmetic and copies ran while one was open for 6% of the time, Pallas kernels for 0%

profile of v3, /device:TPU:0, one launch (start us, length us, event | category | flops | bytes accessed | tf_op | source)
XLA Modules:
  0.0 62.4 jit_solution(493037229759692701)
XLA Ops:
  0.7 0.9 %copy.53 = bf16[1,1,64,2,64]{2,4,3,1,0:T(8,128)(2,1)S(1)} copy(bf16[1,1,64,2,64]{4,3,2,1,0:T(2,128)(2,1)} %param.5) | data formatting | bytes 32768 | tf_op args[1]
  3.3 0.3 fusion.29
  4.1 0.3 fusion.2
  4.4 0.6 collective-permute-start
  4.9 5.9 %all-to-all-start = ((bf16[1,4,32,1,256]{4,2,3,0,1:T(8,128)(2,1)}), bf16[1,4,32,1,256]{4,2,3,0,1:T(8,128)(2,1)S(1)}, u32[]{:S(2)}, u32[]{:S(2)}) async-start(bf16[1,4,32,1,256]{4,2,3,0,1:T(8,128)(2,1)} %bitcast), calls=%async_computation | async-start | bytes 131072 | tf_op jit(solution)/shard_map/all_to_all | solution.py:163
  10.8 1.8 %all_gather.10 = bf16[256,128]{0,1:T(8,128)(2,1)S(1)} all-gather(bf16[256,64]{0,1:T(8,128)(2,1)S(1)} %copy-done.2), channel_id=1, replica_groups=mesh['groups'=2,'space'=4,'sub'=2,'ch'=2] {'ch'}, dimensions={1}, use_global_device_ids=true | all-gather | bytes 98304 | tf_op jit(solution)/shard_map/all_gather | solution.py:207
  13.3 3.3 %all-to-all-done = bf16[1,4,32,1,256]{4,2,3,0,1:T(8,128)(2,1)S(1)} async-done(((bf16[1,4,32,1,256]{4,2,3,0,1:T(8,128)(2,1)}), bf16[1,4,32,1,256]{4,2,3,0,1:T(8,128)(2,1)S(1)}, u32[]{:S(2)}, u32[]{:S(2)}) %all-to-all-start) | async-done | bytes 65568 | tf_op jit(solution)/shard_map/all_to_all | solution.py:163
  17.8 2.2 %all_gather.9 = bf16[128,2,8,8]{3,2,1,0:T(8,128)(2,1)S(1)} all-gather(bf16[64,2,8,8]{3,2,1,0:T(8,128)(2,1)S(1)} %copy.49), channel_id=1, replica_groups=mesh['groups'=2,'space'=4,'sub'=2,'ch'=2] {'ch'}, dimensions={0}, use_global_device_ids=true | all-gather | bytes 49152 | tf_op jit(solution)/shard_map/all_gather | solution.py:173
  19.9 0.4 copy.50
  20.5 1.8 %all_gather.11 = bf16[128,128]{1,0:T(8,128)(2,1)S(1)} all-gather(bf16[64,128]{1,0:T(8,128)(2,1)S(1)} %get-tuple-element.26), channel_id=1, replica_groups=mesh['groups'=2,'space'=4,'sub'=2,'ch'=2] {'ch'}, dimensions={0}, use_global_device_ids=true | all-gather | bytes 49152 | tf_op jit(solution)/shard_map/all_gather | solution.py:206
  23.4 1.9 %collective-permute-start.7 = (f32[32,64]{1,0:T(8,128)S(1)}, f32[32,64]{1,0:T(8,128)S(1)}, u32[]{:S(2)}, u32[]{:S(2)}) collective-permute-start(f32[32,64]{1,0:T(8,128)S(1)} %get-tuple-element.20), channel_id=1, source_target_pairs={{0,14},{2,12},{4,10},{6,8},{8,6},{10,4},{12,2},{14,0},{1,15},{3,13... | collective-permute-start | bytes 24584 | tf_op jit(solution)/shard_map/ppermute | solution.py:149
  25.3 2.9 %collective-permute-start.6 = (f32[32,64]{1,0:T(8,128)S(1)}, f32[32,64]{1,0:T(8,128)S(1)}, u32[]{:S(2)}, u32[]{:S(2)}) collective-permute-start(f32[32,64]{1,0:T(8,128)S(1)} %get-tuple-element.21), channel_id=1, source_target_pairs={{0,12},{2,14},{4,8},{6,10},{8,4},{10,6},{12,0},{14,2},{1,13},{3,15... | collective-permute-start | bytes 24584 | tf_op jit(solution)/shard_map/ppermute | solution.py:149
  28.2 2.9 %collective-permute-start.4 = (f32[32,64]{1,0:T(8,128)S(1)}, f32[32,64]{1,0:T(8,128)S(1)}, u32[]{:S(2)}, u32[]{:S(2)}) collective-permute-start(f32[32,64]{1,0:T(8,128)S(1)} %get-tuple-element.23), channel_id=1, source_target_pairs={{0,8},{2,10},{4,12},{6,14},{8,0},{10,2},{12,4},{14,6},{1,9},{3,11}... | collective-permute-start | bytes 24584 | tf_op jit(solution)/shard_map/ppermute | solution.py:149
  31.8 0.3 fusion
  32.1 3.0 %collective-permute-start.2 = (f32[32,64]{1,0:T(8,128)S(1)}, f32[32,64]{1,0:T(8,128)S(1)}, u32[]{:S(2)}, u32[]{:S(2)}) collective-permute-start(f32[32,64]{1,0:T(8,128)S(1)} %get-tuple-element.25), channel_id=1, source_target_pairs={{0,4},{2,6},{4,0},{6,2},{8,12},{10,14},{12,8},{14,10},{1,5},{3,7},... | collective-permute-start | bytes 24584 | tf_op jit(solution)/shard_map/ppermute | solution.py:149
  35.0 0.5 collective-permute-start.1
  35.6 0.7 %reshape.270 = bf16[1,1,64,2,64]{4,3,2,1,0:T(2,128)(2,1)} reshape(bf16[64,128]{1,0:T(8,128)(2,1)S(1)} %fusion.9) | data formatting | bytes 32768 | tf_op jit(solution)/shard_map/reshape | solution.py:176
  36.3 0.3 copy.66
  36.6 0.7 %copy.67 = bf16[1,1,16,4,256]{4,2,1,0,3:T(8,128)(2,1)} copy(bf16[1,1,16,4,256]{2,4,3,1,0:T(8,128)(2,1)S(1)} %bitcast.204) | data formatting | bytes 65536 | tf_op jit(solution)/shard_map/convert_element_type | solution.py:214
  37.3 3.3 %all-to-all-start.1 = ((bf16[1,1,16,4,256]{4,2,1,0,3:T(8,128)(2,1)}), bf16[1,1,16,4,256]{4,2,1,0,3:T(8,128)(2,1)S(1)}, u32[]{:S(2)}, u32[]{:S(2)}) async-start(bf16[1,1,16,4,256]{4,2,1,0,3:T(8,128)(2,1)} %copy.67), calls=%async_computation.1 | async-start | bytes 65536 | tf_op jit(solution)/shard_map/all_to_all | solution.py:215
  40.6 1.6 %collective-permute-start.8 = (bf16[1,192,128]{2,1,0:T(8,128)(2,1)S(1)}, bf16[1,192,128]{2,1,0:T(8,128)(2,1)S(1)}, u32[]{:S(2)}, u32[]{:S(2)}) collective-permute-start(bf16[1,192,128]{2,1,0:T(8,128)(2,1)S(1)} %maximum_bitcast_fusion), channel_id=1, source_target_pairs={{0,2},{2,0},{4,6},{6,4},{8,10},{10,8},{12,14},{14,12},{1,3},{3,1},... | collective-permute-start | bytes 147464 | tf_op jit(solution)/shard_map/ppermute | solution.py:136
  42.1 1.9 %collective-permute-start.9 = (bf16[1,192,128]{2,1,0:T(8,128)(2,1)S(1)}, bf16[1,192,128]{2,1,0:T(8,128)(2,1)S(1)}, u32[]{:S(2)}, u32[]{:S(2)}) collective-permute-start(bf16[1,192,128]{2,1,0:T(8,128)(2,1)S(1)} %maximum_bitcast_fusion), channel_id=1, source_target_pairs={{0,4},{2,6},{4,0},{6,2},{8,12},{10,14},{12,8},{14,10},{1,5},{3,7},... | collective-permute-start | bytes 147464 | tf_op jit(solution)/shard_map/ppermute | solution.py:136
  44.1 2.8 %collective-permute-start.11 = (bf16[1,192,128]{2,1,0:T(8,128)(2,1)S(1)}, bf16[1,192,128]{2,1,0:T(8,128)(2,1)S(1)}, u32[]{:S(2)}, u32[]{:S(2)}) collective-permute-start(bf16[1,192,128]{2,1,0:T(8,128)(2,1)S(1)} %maximum_bitcast_fusion), channel_id=1, source_target_pairs={{0,8},{2,10},{4,12},{6,14},{8,0},{10,2},{12,4},{14,6},{1,9},{3,11}... | collective-permute-start | bytes 147464 | tf_op jit(solution)/shard_map/ppermute | solution.py:136
  47.0 1.0 %collective-permute-start.12 = (bf16[1,192,128]{2,1,0:T(8,128)(2,1)S(1)}, bf16[1,192,128]{2,1,0:T(8,128)(2,1)S(1)}, u32[]{:S(2)}, u32[]{:S(2)}) collective-permute-start(bf16[1,192,128]{2,1,0:T(8,128)(2,1)S(1)} %maximum_bitcast_fusion), channel_id=1, source_target_pairs={{0,10},{2,8},{4,14},{6,12},{8,2},{10,0},{12,6},{14,4},{1,11},{3,9}... | collective-permute-start | bytes 147464 | tf_op jit(solution)/shard_map/ppermute | solution.py:136
  48.0 0.6 fusion.22
  48.6 3.7 %collective-permute-start.13 = (bf16[1,192,128]{2,1,0:T(8,128)(2,1)S(1)}, bf16[1,192,128]{2,1,0:T(8,128)(2,1)S(1)}, u32[]{:S(2)}, u32[]{:S(2)}) collective-permute-start(bf16[1,192,128]{2,1,0:T(8,128)(2,1)S(1)} %maximum_bitcast_fusion), channel_id=1, source_target_pairs={{0,12},{2,14},{4,8},{6,10},{8,4},{10,6},{12,0},{14,2},{1,13},{3,15... | collective-permute-start | bytes 147464 | tf_op jit(solution)/shard_map/ppermute | solution.py:136
  52.6 0.3 collective-permute-done.12
  52.9 1.9 %collective-permute-done.13 = bf16[1,192,128]{2,1,0:T(8,128)(2,1)S(1)} collective-permute-done((bf16[1,192,128]{2,1,0:T(8,128)(2,1)S(1)}, bf16[1,192,128]{2,1,0:T(8,128)(2,1)S(1)}, u32[]{:S(2)}, u32[]{:S(2)}) %collective-permute-start.13) | collective-permute-done | bytes 49184 | tf_op jit(solution)/shard_map/ppermute | solution.py:136
  54.7 4.5 %collective-permute-done.14 = bf16[1,192,128]{2,1,0:T(8,128)(2,1)S(1)} collective-permute-done((bf16[1,192,128]{2,1,0:T(8,128)(2,1)S(1)}, bf16[1,192,128]{2,1,0:T(8,128)(2,1)S(1)}, u32[]{:S(2)}, u32[]{:S(2)}) %collective-permute-start.14) | collective-permute-done | bytes 49184 | tf_op jit(solution)/shard_map/ppermute | solution.py:136
  59.8 0.5 pad_dynamic-slice_fusion
  61.0 0.8 %dynamic-slice_multiply_fusion = f32[432,64]{0,1:T(8,128)} fusion(f32[640,64]{0,1:T(8,128)S(1)} %fusion.3, s32[]{:T(128)S(6)} %select_n.207), kind=kLoop, calls=%fused_computation.77 | loop fusion | flops 27648 | bytes 221188 | tf_op jit(solution)/shard_map/mul | solution.py:186
  61.8 0.6 copy.128
  (116 shorter events, 6.5 us)
Async XLA Ops:
  0.6 1.1 %copy-start.1 = (bf16[1,1,64,2,64]{4,3,2,1,0:T(2,128)(2,1)S(1)}, bf16[1,1,64,2,64]{4,3,2,1,0:T(2,128)(2,1)}, u32[]{:S(2)}) copy-start(bf16[1,1,64,2,64]{4,3,2,1,0:T(2,128)(2,1)} %param.5) | copy-start | bytes 49156
  0.6 1.2 %copy-start = (bf16[3456,64]{0,1:T(8,128)(2,1)S(1)}, bf16[3456,64]{0,1:T(8,128)(2,1)}, u32[]{:S(2)}) copy-start(bf16[3456,64]{0,1:T(8,128)(2,1)} %param.7) | copy-start | bytes 1327108
  4.0 6.9 %copy-start.2 = (bf16[256,64]{0,1:T(8,128)(2,1)S(1)}, bf16[256,64]{0,1:T(8,128)(2,1)}, u32[]{:S(2)}) copy-start(bf16[256,64]{0,1:T(8,128)(2,1)} %param.6) | copy-start | bytes 98308
  4.4 12.8 %collective-permute-start = (f32[64,128]{1,0:T(8,128)S(1)}, f32[64,128]{1,0:T(8,128)S(1)}, u32[]{:S(2)}, u32[]{:S(2)}) collective-permute-start(f32[64,128]{1,0:T(8,128)S(1)} %dynamic-slice_bitcast_fusion), channel_id=1, source_target_pairs={{0,1},{1,0},{2,3},{3,2},{4,5},{5,4},{6,7},{7,6},{8,9},{9,8},{10,11... | collective-permute-start | bytes 98312 | tf_op jit(solution)/shard_map/ppermute | solution.py:94
  4.9 11.6 %all-to-all-start = ((bf16[1,4,32,1,256]{4,2,3,0,1:T(8,128)(2,1)}), bf16[1,4,32,1,256]{4,2,3,0,1:T(8,128)(2,1)S(1)}, u32[]{:S(2)}, u32[]{:S(2)}) async-start(bf16[1,4,32,1,256]{4,2,3,0,1:T(8,128)(2,1)} %bitcast), calls=%async_computation | async-start | bytes 131072 | tf_op jit(solution)/shard_map/all_to_all | solution.py:163
  23.4 8.7 %collective-permute-start.7 = (f32[32,64]{1,0:T(8,128)S(1)}, f32[32,64]{1,0:T(8,128)S(1)}, u32[]{:S(2)}, u32[]{:S(2)}) collective-permute-start(f32[32,64]{1,0:T(8,128)S(1)} %get-tuple-element.20), channel_id=1, source_target_pairs={{0,14},{2,12},{4,10},{6,8},{8,6},{10,4},{12,2},{14,0},{1,15},{3,13... | collective-permute-start | bytes 24584 | tf_op jit(solution)/shard_map/ppermute | solution.py:149
  25.3 9.8 %collective-permute-start.6 = (f32[32,64]{1,0:T(8,128)S(1)}, f32[32,64]{1,0:T(8,128)S(1)}, u32[]{:S(2)}, u32[]{:S(2)}) collective-permute-start(f32[32,64]{1,0:T(8,128)S(1)} %get-tuple-element.21), channel_id=1, source_target_pairs={{0,12},{2,14},{4,8},{6,10},{8,4},{10,6},{12,0},{14,2},{1,13},{3,15... | collective-permute-start | bytes 24584 | tf_op jit(solution)/shard_map/ppermute | solution.py:149
  28.2 12.4 %collective-permute-start.5 = (f32[32,64]{1,0:T(8,128)S(1)}, f32[32,64]{1,0:T(8,128)S(1)}, u32[]{:S(2)}, u32[]{:S(2)}) collective-permute-start(f32[32,64]{1,0:T(8,128)S(1)} %get-tuple-element.22), channel_id=1, source_target_pairs={{0,10},{2,8},{4,14},{6,12},{8,2},{10,0},{12,6},{14,4},{1,11},{3,9}... | collective-permute-start | bytes 24584 | tf_op jit(solution)/shard_map/ppermute | solution.py:149
  28.2 14.0 %collective-permute-start.4 = (f32[32,64]{1,0:T(8,128)S(1)}, f32[32,64]{1,0:T(8,128)S(1)}, u32[]{:S(2)}, u32[]{:S(2)}) collective-permute-start(f32[32,64]{1,0:T(8,128)S(1)} %get-tuple-element.23), channel_id=1, source_target_pairs={{0,8},{2,10},{4,12},{6,14},{8,0},{10,2},{12,4},{14,6},{1,9},{3,11}... | collective-permute-start | bytes 24584 | tf_op jit(solution)/shard_map/ppermute | solution.py:149
  31.1 13.0 %collective-permute-start.3 = (f32[32,64]{1,0:T(8,128)S(1)}, f32[32,64]{1,0:T(8,128)S(1)}, u32[]{:S(2)}, u32[]{:S(2)}) collective-permute-start(f32[32,64]{1,0:T(8,128)S(1)} %get-tuple-element.24), channel_id=1, source_target_pairs={{0,6},{2,4},{4,2},{6,0},{8,14},{10,12},{12,10},{14,8},{1,7},{3,5},... | collective-permute-start | bytes 24584 | tf_op jit(solution)/shard_map/ppermute | solution.py:149
  32.1 12.1 %collective-permute-start.2 = (f32[32,64]{1,0:T(8,128)S(1)}, f32[32,64]{1,0:T(8,128)S(1)}, u32[]{:S(2)}, u32[]{:S(2)}) collective-permute-start(f32[32,64]{1,0:T(8,128)S(1)} %get-tuple-element.25), channel_id=1, source_target_pairs={{0,4},{2,6},{4,0},{6,2},{8,12},{10,14},{12,8},{14,10},{1,5},{3,7},... | collective-permute-start | bytes 24584 | tf_op jit(solution)/shard_map/ppermute | solution.py:149
  35.0 11.9 %collective-permute-start.1 = (f32[32,64]{1,0:T(8,128)S(1)}, f32[32,64]{1,0:T(8,128)S(1)}, u32[]{:S(2)}, u32[]{:S(2)}) collective-permute-start(f32[32,64]{1,0:T(8,128)S(1)} %get-tuple-element.19), channel_id=1, source_target_pairs={{0,2},{2,0},{4,6},{6,4},{8,10},{10,8},{12,14},{14,12},{1,3},{3,1},... | collective-permute-start | bytes 24584 | tf_op jit(solution)/shard_map/ppermute | solution.py:149
  37.3 17.4 %all-to-all-start.1 = ((bf16[1,1,16,4,256]{4,2,1,0,3:T(8,128)(2,1)}), bf16[1,1,16,4,256]{4,2,1,0,3:T(8,128)(2,1)S(1)}, u32[]{:S(2)}, u32[]{:S(2)}) async-start(bf16[1,1,16,4,256]{4,2,1,0,3:T(8,128)(2,1)} %copy.67), calls=%async_computation.1 | async-start | bytes 65536 | tf_op jit(solution)/shard_map/all_to_all | solution.py:215
  40.6 8.0 %collective-permute-start.8 = (bf16[1,192,128]{2,1,0:T(8,128)(2,1)S(1)}, bf16[1,192,128]{2,1,0:T(8,128)(2,1)S(1)}, u32[]{:S(2)}, u32[]{:S(2)}) collective-permute-start(bf16[1,192,128]{2,1,0:T(8,128)(2,1)S(1)} %maximum_bitcast_fusion), channel_id=1, source_target_pairs={{0,2},{2,0},{4,6},{6,4},{8,10},{10,8},{12,14},{14,12},{1,3},{3,1},... | collective-permute-start | bytes 147464 | tf_op jit(solution)/shard_map/ppermute | solution.py:136
  42.1 10.2 %collective-permute-start.9 = (bf16[1,192,128]{2,1,0:T(8,128)(2,1)S(1)}, bf16[1,192,128]{2,1,0:T(8,128)(2,1)S(1)}, u32[]{:S(2)}, u32[]{:S(2)}) collective-permute-start(bf16[1,192,128]{2,1,0:T(8,128)(2,1)S(1)} %maximum_bitcast_fusion), channel_id=1, source_target_pairs={{0,4},{2,6},{4,0},{6,2},{8,12},{10,14},{12,8},{14,10},{1,5},{3,7},... | collective-permute-start | bytes 147464 | tf_op jit(solution)/shard_map/ppermute | solution.py:136
  44.0 8.5 %collective-permute-start.10 = (bf16[1,192,128]{2,1,0:T(8,128)(2,1)S(1)}, bf16[1,192,128]{2,1,0:T(8,128)(2,1)S(1)}, u32[]{:S(2)}, u32[]{:S(2)}) collective-permute-start(bf16[1,192,128]{2,1,0:T(8,128)(2,1)S(1)} %maximum_bitcast_fusion), channel_id=1, source_target_pairs={{0,6},{2,4},{4,2},{6,0},{8,14},{10,12},{12,10},{14,8},{1,7},{3,5},... | collective-permute-start | bytes 147464 | tf_op jit(solution)/shard_map/ppermute | solution.py:136
  44.1 8.4 %collective-permute-start.11 = (bf16[1,192,128]{2,1,0:T(8,128)(2,1)S(1)}, bf16[1,192,128]{2,1,0:T(8,128)(2,1)S(1)}, u32[]{:S(2)}, u32[]{:S(2)}) collective-permute-start(bf16[1,192,128]{2,1,0:T(8,128)(2,1)S(1)} %maximum_bitcast_fusion), channel_id=1, source_target_pairs={{0,8},{2,10},{4,12},{6,14},{8,0},{10,2},{12,4},{14,6},{1,9},{3,11}... | collective-permute-start | bytes 147464 | tf_op jit(solution)/shard_map/ppermute | solution.py:136
  47.0 5.9 %collective-permute-start.12 = (bf16[1,192,128]{2,1,0:T(8,128)(2,1)S(1)}, bf16[1,192,128]{2,1,0:T(8,128)(2,1)S(1)}, u32[]{:S(2)}, u32[]{:S(2)}) collective-permute-start(bf16[1,192,128]{2,1,0:T(8,128)(2,1)S(1)} %maximum_bitcast_fusion), channel_id=1, source_target_pairs={{0,10},{2,8},{4,14},{6,12},{8,2},{10,0},{12,6},{14,4},{1,11},{3,9}... | collective-permute-start | bytes 147464 | tf_op jit(solution)/shard_map/ppermute | solution.py:136
  48.6 6.1 %collective-permute-start.13 = (bf16[1,192,128]{2,1,0:T(8,128)(2,1)S(1)}, bf16[1,192,128]{2,1,0:T(8,128)(2,1)S(1)}, u32[]{:S(2)}, u32[]{:S(2)}) collective-permute-start(bf16[1,192,128]{2,1,0:T(8,128)(2,1)S(1)} %maximum_bitcast_fusion), channel_id=1, source_target_pairs={{0,12},{2,14},{4,8},{6,10},{8,4},{10,6},{12,0},{14,2},{1,13},{3,15... | collective-permute-start | bytes 147464 | tf_op jit(solution)/shard_map/ppermute | solution.py:136
  52.4 6.9 %collective-permute-start.14 = (bf16[1,192,128]{2,1,0:T(8,128)(2,1)S(1)}, bf16[1,192,128]{2,1,0:T(8,128)(2,1)S(1)}, u32[]{:S(2)}, u32[]{:S(2)}) collective-permute-start(bf16[1,192,128]{2,1,0:T(8,128)(2,1)S(1)} %maximum_bitcast_fusion), channel_id=1, source_target_pairs={{0,14},{2,12},{4,10},{6,8},{8,6},{10,4},{12,2},{14,0},{1,15},{3,13... | collective-permute-start | bytes 147464 | tf_op jit(solution)/shard_map/ppermute | solution.py:136

commit v4 on v2

--- a/solution.py
+++ b/solution.py
@@ -4,6 +4,7 @@
 import jax.numpy as jnp
 from jax import lax
 from jax.sharding import PartitionSpec as P
+
 
 XY = 16
 
@@ -50,7 +51,7 @@
 
 
 def conv_weight_grad(hidden, cot):
-    chans, depth, side = (hidden.shape[0], hidden.shape[1], hidden.shape[2])
+    depth, side = (hidden.shape[1], hidden.shape[2])
     padded = jnp.pad(hidden, ((0, 0), (1, 1), (1, 1), (1, 1)))
     pieces = []
     for plane in range(3):
@@ -64,7 +65,7 @@
 
 
 def conv_back(cot, weight_rows):
-    chans, depth, side = (cot.shape[0], cot.shape[1], cot.shape[2])
+    depth, side = (cot.shape[1], cot.shape[2])
     padded = jnp.pad(cot, ((0, 0), (1, 1), (1, 1), (1, 1)))
     total = jnp.zeros((weight_rows.shape[1], depth * side * side), jnp.float32)
     for plane in range(3):
@@ -130,12 +131,104 @@
     return lax.dynamic_slice_in_dim(stacked, first - tap0 * chans, rows, 0)
 
 
+def ordered_gather(x, name):
+    size = lax.axis_size(name)
+    index = lax.axis_index(name)
+    x = x[None]
+    for j in range(size.bit_length() - 1):
+        got = lax.ppermute(x, name, [(i, i ^ (1 << j)) for i in range(size)])
+        low = ((index >> j) & 1) == 0
+        x = jnp.where(low, jnp.concatenate([x, got]), jnp.concatenate([got, x]))
+    return x
+
+
+def block_local(volumes, cotangent, first_weight, second_weight):
+    per, chans, planes = volumes.shape[1], volumes.shape[2], volumes.shape[3]
+    half_c = chans // lax.axis_size("ch")
+    pair_index = lax.axis_index("ch")
+    half_o = first_weight.shape[1]
+    spaces, subs = lax.axis_size("space"), lax.axis_size("sub")
+    depth = spaces * planes
+    half_z, half_s = (depth // 2, XY // 2)
+    voxels = half_z * half_s * half_s
+    factor = 1.0 / math.sqrt(spaces * subs * voxels)
+    all_first = lax.all_gather(first_weight, "ch", axis=1, tiled=True)
+    width = all_first.shape[1]
+    vol_size = volumes.size
+    flat = jnp.concatenate([volumes.reshape(-1), cotangent.reshape(-1)])
+    near = ordered_gather(flat, "space")
+    own = lax.dynamic_index_in_dim(
+        near[:, :vol_size].reshape(spaces, per, chans, planes, XY * XY),
+        lax.axis_index("space"),
+        axis=1,
+        keepdims=False,
+    )
+    sample = own.transpose(1, 0, 2, 3).reshape(chans, depth, XY * XY)
+    cols = to_depth(sample, XY)
+    pre = lax.dot_general(
+        all_first, cols, (((0,), (0,)), ((), ())), preferred_element_type=jnp.float32
+    )
+    grid = jax.nn.silu(pre).astype(jnp.bfloat16).reshape(width, half_z, half_s, half_s)
+    out = conv_forward(grid, second_weight)
+    block_out = out.astype(jnp.bfloat16).reshape(1, 1, half_o, half_z, half_s * half_s)
+    cot = cotangent.reshape(half_o, voxels)
+    cot_grid = cot.reshape(half_o, half_z, half_s, half_s)
+    local_rows = second_weight.reshape(27, width, half_o)
+    hidden_grad = halving_scatter(conv_back(cot_grid, local_rows), ("ch",))
+    pre_half = lax.dynamic_slice_in_dim(pre, pair_index * half_o, half_o, 0)
+    pre_grad = (hidden_grad * silu_slope(pre_half)).astype(jnp.bfloat16)
+    grad_first = (
+        lax.dot_general(
+            cols, pre_grad, (((1,), (1,)), ((), ())), preferred_element_type=jnp.float32
+        )
+        * factor
+    )
+    all_pre_grad = lax.all_gather(pre_grad, "ch", axis=0, tiled=True)
+    first_rows = lax.dynamic_slice_in_dim(
+        all_first.reshape(8, chans, width), pair_index * half_c, half_c, 1
+    )
+    grad_cols = jnp.dot(
+        first_rows.reshape(8 * half_c, width), all_pre_grad, preferred_element_type=jnp.float32
+    )
+    grad_sample = from_depth(grad_cols, half_c, depth, XY).astype(jnp.bfloat16)
+    volume_grad = lax.all_to_all(
+        grad_sample.reshape(1, 1, half_c, depth, XY * XY),
+        "space",
+        split_axis=3,
+        concat_axis=1,
+        tiled=True,
+    )
+    first_grad = halving_scatter(grad_first, ("space", "sub"))
+    far = ordered_gather(near, "sub")
+    count = subs * spaces
+    vols = far[:, :, :vol_size].reshape(subs, spaces, per, chans, planes, XY * XY)
+    samples = vols.transpose(0, 2, 3, 1, 4, 5).reshape(subs * per, chans, depth, XY * XY)
+    cols_all = jax.vmap(lambda s: to_depth(s, XY))(samples)
+    pre_all = jnp.einsum("ro,nrv->nov", all_first, cols_all, preferred_element_type=jnp.float32)
+    hidden_all = jax.nn.silu(pre_all).astype(jnp.bfloat16)
+    cot_all = far[:, :, vol_size:].reshape(count, half_o, voxels)
+    second_grad = (
+        second_grad_rows(
+            hidden_all.reshape(count, width, half_z, half_s, half_s),
+            cot_all,
+            ("space", "sub"),
+            second_weight.shape[0],
+        )
+        * factor
+    )
+    return (block_out, volume_grad, first_grad, second_grad)
+
+
 def silu_slope(pre):
     sig = jax.nn.sigmoid(pre)
     return sig * (1.0 + pre * (1.0 - sig))
 
 
-def body(volumes, cotangent, first_weight, second_weight):
+def block(volumes, cotangent, first_weight, second_weight):
+    shards = lax.axis_size("space") * lax.axis_size("sub")
+    local_bytes = (volumes.size + cotangent.size) * 2
+    if volumes.shape[1] == lax.axis_size("space") and shards * local_bytes <= 1 << 22:
+        return block_local(volumes, cotangent, first_weight, second_weight)
     chans = volumes.shape[2]
     half_c = chans // lax.axis_size("ch")
     pair_index = lax.axis_index("ch")
@@ -183,10 +276,8 @@
         )
         * factor
     )
-    all_pre_grad, all_first = (
-        lax.all_gather(pre_grad, "ch", axis=0, tiled=True),
-        lax.all_gather(first_weight, "ch", axis=1, tiled=True),
-    )
+    all_pre_grad = lax.all_gather(pre_grad, "ch", axis=0, tiled=True)
+    all_first = lax.all_gather(first_weight, "ch", axis=1, tiled=True)
     first_rows = lax.dynamic_slice_in_dim(
         all_first.reshape(8, chans, width), pair_index * half_c, half_c, 1
     )
@@ -201,16 +292,20 @@
         concat_axis=1,
         tiled=True,
     )
-    first_grad, second_grad = (
-        halving_scatter(grad_first, ("space", "sub")),
-        grad_second if gather_second else halving_scatter(grad_second, ("space", "sub")),
+    first_grad = halving_scatter(grad_first, ("space", "sub"))
+    second_grad = (
+        grad_second if gather_second else halving_scatter(grad_second, ("space", "sub"))
     )
     return (block_out, volume_grad, first_grad, second_grad)
 
 
 def solution(mesh):
+    return step_of(mesh)
+
+
+def step_of(mesh):
     return jax.shard_map(
-        body,
+        block,
         mesh=mesh,
         in_specs=(
             P(("groups", "sub"), None, None, "space", None),

time: 54.7 us -> 62.8 us (1.15)
  local copies, waits for them, and re-layouts: 8.24 us -> 20.8 us
  starting transfers between devices: 20.3 us -> 17.2 us
  other arithmetic: 1.46 us -> 4.45 us
  waiting for transfers between devices: 13.9 us -> 11.4 us
  blocking collectives: 5.85 us -> 3.68 us
    reshape x1 -> x2, local copies, waits for them, and re-layouts: 0.18 us -> 6.25 us  [to_depth(): return blocks.reshape(8 * chans, depth // 2 * (side // 2) * (side // 2))]
    all_to_all x2 -> x1, starting transfers between devices: 9.14 us -> 3.91 us  [block_local(): lax.all_to_all(grad_sample.reshape(1, 1, half_c, depth, XY * XY), 'space'...]
    transpose x1 -> x2, local copies, waits for them, and re-layouts: 0.24 us -> 3.86 us  [to_depth(): blocks = blocks.transpose(2, 4, 6, 0, 1, 3, 5)]
    all_to_all x2 -> x1, waiting for transfers between devices: 3.33 us -> 0.01 us  [block_local(): lax.all_to_all(grad_sample.reshape(1, 1, half_c, depth, XY * XY), 'space'...]
    ppermute x4, waiting for transfers between devices: 1.55 us -> 4.25 us  [halving_scatter(): x = mine + lax.ppermute(other, name, perm)]
    select_n x0 -> x4, other arithmetic: none -> 2.28 us  [ordered_gather(): x = jnp.where(low, jnp.concatenate([x, got]), jnp.concatenate([got, x]))]
    ppermute x3, starting transfers between devices: 4.16 us -> 6.37 us  [ordered_gather(): got = lax.ppermute(x, name, [(i, i ^ 1 << j) for i in range(size)])]
    all_gather x3 -> x2, blocking collectives: 5.85 us -> 3.68 us  [the longest x1 1.85 us: block_local(): all_first = lax.all_gather(first_weight, 'ch', axis=1, tiled=True)]
  transfers between devices with their start and end apart: 9 -> 8, of which waited for: 5 -> 4; matrix products, arithmetic and copies ran while one was open for 8% -> 13% of each run, Pallas kernels for 0% -> 0%
where the time goes in v4:
time: 62.8 us; the launch traced here: 62.4 us
  local copies, waits for them, and re-layouts  20.8 us (33%)
  starting transfers between devices  17.2 us (27%)
  waiting for transfers between devices  11.4 us (18%)
  other arithmetic  4.45 us (7%)
  blocking collectives  3.68 us (6%)
  matrix products  3.15 us (5%)
  between operations  1.78 us (3%)
    ppermute x3, waiting for transfers between devices, ordered_gather(): got = lax.ppermute(x, name, [(i, i ^ 1 << j) for i in range(size)])  7.19 us
    ppermute x4, starting transfers between devices, halving_scatter(): x = mine + lax.ppermute(other, name, perm)  6.9 us
    ppermute x3, starting transfers between devices, ordered_gather(): got = lax.ppermute(x, name, [(i, i ^ 1 << j) for i in range(size)])  6.37 us
    reshape x2, local copies, waits for them, and re-layouts, to_depth(): return blocks.reshape(8 * chans, depth // 2 * (side // 2) * (side // 2))  6.25 us
    ppermute x4, waiting for transfers between devices, halving_scatter(): x = mine + lax.ppermute(other, name, perm)  4.25 us
    all_to_all x1, starting transfers between devices, block_local(): lax.all_to_all(grad_sample.reshape(1, 1, half_c, depth, XY * XY), 'space'...  3.91 us
    transpose x2, local copies, waits for them, and re-layouts, to_depth(): blocks = blocks.transpose(2, 4, 6, 0, 1, 3, 5)  3.86 us
    unnamed x33, local copies, waits for them, and re-layouts  2.88 us
  transfers between devices with their start and end apart: 8, of which 4 were waited for; matrix products, arithmetic and copies ran while one was open for 13% of the time, Pallas kernels for 0%

profile of v4, /device:TPU:0, one launch (start us, length us, event | category | flops | bytes accessed | tf_op | source)
XLA Modules:
  0.0 62.4 jit_solution(8340228336509783353)
XLA Ops:
  0.6 0.9 %reshape.365 = bf16[8192]{0:T(1024)(128)(2,1)S(1)} reshape(bf16[1,1,64,2,64]{4,3,2,1,0:T(2,128)(2,1)} %param.5) | data formatting | bytes 32768 | tf_op jit(solution)/shard_map/reshape | solution.py:158
  1.5 0.9 %copy.109 = bf16[16,2,8,128]{3,1,2,0:T(2,128)(2,1)S(1)} copy(bf16[16,2,8,128]{3,2,1,0:T(8,128)(2,1)} %bitcast.316) | data formatting | bytes 131072
  2.5 3.1 %collective-permute-start = (bf16[1,40960]{1,0:T(2,128)(2,1)S(1)}, bf16[1,40960]{1,0:T(2,128)(2,1)S(1)}, u32[]{:S(2)}, u32[]{:S(2)}) collective-permute-start(bf16[1,40960]{1,0:T(2,128)(2,1)S(1)} %broadcast_in_dim.4), channel_id=1, source_target_pairs={{0,4},{4,0},{8,12},{12,8},{1,5},{5,1},{9,13},{13,9},{2,6},{6,2},{1... | collective-permute-start | bytes 245768 | tf_op jit(solution)/shard_map/ppermute | solution.py:139
  5.7 0.9 %copy.84 = bf16[1,1,64,2,64]{2,4,3,1,0:T(8,128)(2,1)S(1)} copy(bf16[1,1,64,2,64]{4,3,2,1,0:T(2,128)(2,1)} %param.5) | data formatting | bytes 32768 | tf_op args[1]
  9.0 1.9 %all_gather.6 = bf16[256,128]{0,1:T(8,128)(2,1)S(1)} all-gather(bf16[256,64]{0,1:T(8,128)(2,1)S(1)} %copy-done.1), channel_id=1, replica_groups=mesh['groups'=2,'space'=4,'sub'=2,'ch'=2] {'ch'}, dimensions={1}, use_global_device_ids=true | all-gather | bytes 98304 | tf_op jit(solution)/shard_map/all_gather | solution.py:155
  11.1 0.7 %broadcast_select_fusion = bf16[2,40960]{1,0:T(2,128)(2,1)S(1)} fusion(pred[]{:T(512)S(6)} %eq.21, bf16[1,40960]{1,0:T(2,128)(2,1)S(1)} %collective-permute-done, bf16[1,40960]{1,0:T(2,128)(2,1)S(1)} %broadcast_in_dim.4), kind=kLoop, calls=%fused_computation.80 | loop fusion | flops 737280 | bytes 327681 | tf_op jit(solution)/shard_map/jit(_where)/select_n | solution.py:141
  11.8 2.7 %collective-permute-start.1 = (bf16[2,40960]{1,0:T(2,128)(2,1)S(1)}, bf16[2,40960]{1,0:T(2,128)(2,1)S(1)}, u32[]{:S(2)}, u32[]{:S(2)}) collective-permute-start(bf16[2,40960]{1,0:T(2,128)(2,1)S(1)} %broadcast_select_fusion), channel_id=1, source_target_pairs={{0,8},{4,12},{8,0},{12,4},{1,9},{5,13},{9,1},{13,5},{2,10},{6,14},... | collective-permute-start | bytes 491528 | tf_op jit(solution)/shard_map/ppermute | solution.py:139
  14.5 0.7 %fusion.55 = bf16[1,2,40960]{2,1,0:T(2,128)(2,1)S(1)} fusion(bf16[1,40960]{1,0:T(2,128)(2,1)S(1)} %broadcast_in_dim.4, bf16[1,40960]{1,0:T(2,128)(2,1)S(1)} %collective-permute-done, pred[]{:T(512)S(6)} %eq.21), kind=kLoop, calls=%fused_computation.146 | loop fusion | flops 737280 | bytes 327681 | tf_op jit(solution)/shard_map/concatenate | solution.py:141
  15.2 7.2 %collective-permute-done.1 = bf16[2,40960]{1,0:T(2,128)(2,1)S(1)} collective-permute-done((bf16[2,40960]{1,0:T(2,128)(2,1)S(1)}, bf16[2,40960]{1,0:T(2,128)(2,1)S(1)}, u32[]{:S(2)}, u32[]{:S(2)}) %collective-permute-start.1) | collective-permute-done | bytes 163872 | tf_op jit(solution)/shard_map/ppermute | solution.py:139
  22.4 0.5 fusion.9
  24.0 1.8 %all_gather.7 = bf16[128,128]{1,0:T(8,128)(2,1)S(1)} all-gather(bf16[64,128]{1,0:T(8,128)(2,1)S(1)} %fusion.21), channel_id=1, replica_groups=mesh['groups'=2,'space'=4,'sub'=2,'ch'=2] {'ch'}, dimensions={0}, use_global_device_ids=true | all-gather | bytes 49152 | tf_op jit(solution)/shard_map/all_gather | solution.py:186
  28.5 0.7 %copy.91 = bf16[1,1,16,4,256]{4,2,1,0,3:T(8,128)(2,1)} copy(bf16[1,1,16,4,256]{2,4,3,1,0:T(8,128)(2,1)S(1)} %bitcast.242) | data formatting | bytes 65536 | tf_op jit(solution)/shard_map/convert_element_type | solution.py:193
  29.3 3.9 %all-to-all-start = ((bf16[1,1,16,4,256]{4,2,1,0,3:T(8,128)(2,1)}), bf16[1,1,16,4,256]{4,2,1,0,3:T(8,128)(2,1)S(1)}, u32[]{:S(2)}, u32[]{:S(2)}) async-start(bf16[1,1,16,4,256]{4,2,1,0,3:T(8,128)(2,1)} %copy.91), calls=%async_computation | async-start | bytes 65536 | tf_op jit(solution)/shard_map/all_to_all | solution.py:194
  33.3 1.6 %collective-permute-start.3 = (f32[2,2,32,64]{3,2,1,0:T(8,128)S(1)}, f32[2,2,32,64]{3,2,1,0:T(8,128)S(1)}, u32[]{:S(2)}, u32[]{:S(2)}) collective-permute-start(f32[2,2,32,64]{3,2,1,0:T(8,128)S(1)} %dynamic-slice_bitcast_fusion), channel_id=1, source_target_pairs={{0,2},{2,0},{1,3},{3,1},{4,6},{6,4},{5,7},{7,5},{8,10},{10,8},{9,1... | collective-permute-start | bytes 98312 | tf_op jit(solution)/shard_map/ppermute | solution.py:94
  34.8 0.6 maximum_select_fusion.1
  35.4 0.6 collective-permute-start.6
  36.1 1.5 %collective-permute-done.3 = f32[2,2,32,64]{3,2,1,0:T(8,128)S(1)} collective-permute-done((f32[2,2,32,64]{3,2,1,0:T(8,128)S(1)}, f32[2,2,32,64]{3,2,1,0:T(8,128)S(1)}, u32[]{:S(2)}, u32[]{:S(2)}) %collective-permute-start.3) | collective-permute-done | bytes 32800 | tf_op jit(solution)/shard_map/ppermute | solution.py:94
  37.6 2.3 %collective-permute-start.4 = (f32[2,32,64]{2,1,0:T(8,128)S(1)}, f32[2,32,64]{2,1,0:T(8,128)S(1)}, u32[]{:S(2)}, u32[]{:S(2)}) collective-permute-start(f32[2,32,64]{2,1,0:T(8,128)S(1)} %dynamic-slice_bitcast_fusion.1), channel_id=1, source_target_pairs={{0,4},{4,0},{8,12},{12,8},{1,5},{5,1},{9,13},{13,9},{2,6},{6,2},{1... | collective-permute-start | bytes 49160 | tf_op jit(solution)/shard_map/ppermute | solution.py:94
  39.9 1.9 %collective-permute-done.4 = f32[2,32,64]{2,1,0:T(8,128)S(1)} collective-permute-done((f32[2,32,64]{2,1,0:T(8,128)S(1)}, f32[2,32,64]{2,1,0:T(8,128)S(1)}, u32[]{:S(2)}, u32[]{:S(2)}) %collective-permute-start.4) | collective-permute-done | bytes 16416 | tf_op jit(solution)/shard_map/ppermute | solution.py:94
  41.8 3.0 %collective-permute-start.5 = (f32[32,64]{1,0:T(8,128)S(1)}, f32[32,64]{1,0:T(8,128)S(1)}, u32[]{:S(2)}, u32[]{:S(2)}) collective-permute-start(f32[32,64]{1,0:T(8,128)S(1)} %dynamic-slice_bitcast_fusion.3), channel_id=1, source_target_pairs={{0,8},{4,12},{8,0},{12,4},{1,9},{5,13},{9,1},{13,5},{2,10},{6,14},... | collective-permute-start | bytes 24584 | tf_op jit(solution)/shard_map/ppermute | solution.py:94
  45.0 0.7 %reshape.395 = bf16[1,1,64,2,64]{4,3,2,1,0:T(2,128)(2,1)} reshape(bf16[64,128]{1,0:T(8,128)(2,1)S(1)} %fusion.8) | data formatting | bytes 32768 | tf_op jit(solution)/shard_map/reshape | solution.py:173
  45.7 0.8 %collective-permute-done.5 = f32[32,64]{1,0:T(8,128)S(1)} collective-permute-done((f32[32,64]{1,0:T(8,128)S(1)}, f32[32,64]{1,0:T(8,128)S(1)}, u32[]{:S(2)}, u32[]{:S(2)}) %collective-permute-start.5) | collective-permute-done | bytes 8224 | tf_op jit(solution)/shard_map/ppermute | solution.py:94
  46.5 0.6 bitcast_add_fusion.3
  47.2 0.5 maximum_select_fusion
  48.0 0.4 reshape.429
  48.4 1.0 %copy.93 = bf16[2,4,32,4,1,256]{2,5,3,1,0,4:T(8,128)(2,1)S(1)} copy(bf16[2,4,32,4,1,256]{5,2,1,3,0,4:T(8,128)(2,1)S(1)} %bitcast.230) | data formatting | bytes 1048576 | tf_op jit(solution)/shard_map/transpose | solution.py:205
  49.5 3.6 %copy.94 = bf16[8,2,2,2,32,2,8,8]{4,3,2,1,7,6,5,0:T(2,128)(2,1)} copy(bf16[8,2,2,2,32,2,8,8]{4,3,7,2,6,1,5,0:T(2,128)(2,1)S(1)} %bitcast.229) | data formatting | bytes 1048576 | tf_op jit(solution)/shard_map/vmap()/transpose | solution.py:15
  53.1 6.1 %reshape.430 = bf16[8,256,128]{1,2,0:T(8,128)(2,1)S(1)} reshape(bf16[8,2,2,2,32,2,8,8]{4,3,2,1,7,6,5,0:T(2,128)(2,1)} %copy.94) | data formatting | bytes 1048576 | tf_op jit(solution)/shard_map/vmap()/reshape | solution.py:16
  59.2 0.3 multiply_convert_fusion
  59.8 0.5 pad_dynamic-slice_fusion
  61.1 0.8 %dynamic-slice_multiply_fusion = f32[432,64]{0,1:T(8,128)} fusion(f32[640,64]{0,1:T(8,128)S(1)} %fusion.1, s32[]{:T(128)S(6)} %select_n.262), kind=kLoop, calls=%fused_computation.84 | loop fusion | flops 27648 | bytes 221188 | tf_op jit(solution)/shard_map/mul | solution.py:211
  61.8 0.6 copy.140
  (96 shorter events, 7.4 us)
Async XLA Ops:
  0.6 6.1 %copy-start = (bf16[3456,64]{0,1:T(8,128)(2,1)S(1)}, bf16[3456,64]{0,1:T(8,128)(2,1)}, u32[]{:S(2)}) copy-start(bf16[3456,64]{0,1:T(8,128)(2,1)} %param.7) | copy-start | bytes 1327108
  2.5 8.5 %collective-permute-start = (bf16[1,40960]{1,0:T(2,128)(2,1)S(1)}, bf16[1,40960]{1,0:T(2,128)(2,1)S(1)}, u32[]{:S(2)}, u32[]{:S(2)}) collective-permute-start(bf16[1,40960]{1,0:T(2,128)(2,1)S(1)} %broadcast_in_dim.4), channel_id=1, source_target_pairs={{0,4},{4,0},{8,12},{12,8},{1,5},{5,1},{9,13},{13,9},{2,6},{6,2},{1... | collective-permute-start | bytes 245768 | tf_op jit(solution)/shard_map/ppermute | solution.py:139
  7.3 1.6 %copy-start.1 = (bf16[256,64]{0,1:T(8,128)(2,1)S(1)}, bf16[256,64]{0,1:T(8,128)(2,1)}, u32[]{:S(2)}) copy-start(bf16[256,64]{0,1:T(8,128)(2,1)} %param.6) | copy-start | bytes 98308
  8.5 15.5 %collective-permute-start.2 = (f32[64,128]{1,0:T(8,128)S(1)}, f32[64,128]{1,0:T(8,128)S(1)}, u32[]{:S(2)}, u32[]{:S(2)}) collective-permute-start(f32[64,128]{1,0:T(8,128)S(1)} %dynamic-slice_bitcast_fusion.2), channel_id=1, source_target_pairs={{0,1},{1,0},{2,3},{3,2},{4,5},{5,4},{6,7},{7,6},{8,9},{9,8},{10,11... | collective-permute-start | bytes 98312 | tf_op jit(solution)/shard_map/ppermute | solution.py:94
  11.8 10.6 %collective-permute-start.1 = (bf16[2,40960]{1,0:T(2,128)(2,1)S(1)}, bf16[2,40960]{1,0:T(2,128)(2,1)S(1)}, u32[]{:S(2)}, u32[]{:S(2)}) collective-permute-start(bf16[2,40960]{1,0:T(2,128)(2,1)S(1)} %broadcast_select_fusion), channel_id=1, source_target_pairs={{0,8},{4,12},{8,0},{12,4},{1,9},{5,13},{9,1},{13,5},{2,10},{6,14},... | collective-permute-start | bytes 491528 | tf_op jit(solution)/shard_map/ppermute | solution.py:139
  29.3 16.5 %all-to-all-start = ((bf16[1,1,16,4,256]{4,2,1,0,3:T(8,128)(2,1)}), bf16[1,1,16,4,256]{4,2,1,0,3:T(8,128)(2,1)S(1)}, u32[]{:S(2)}, u32[]{:S(2)}) async-start(bf16[1,1,16,4,256]{4,2,1,0,3:T(8,128)(2,1)} %copy.91), calls=%async_computation | async-start | bytes 65536 | tf_op jit(solution)/shard_map/all_to_all | solution.py:194
  33.3 4.3 %collective-permute-start.3 = (f32[2,2,32,64]{3,2,1,0:T(8,128)S(1)}, f32[2,2,32,64]{3,2,1,0:T(8,128)S(1)}, u32[]{:S(2)}, u32[]{:S(2)}) collective-permute-start(f32[2,2,32,64]{3,2,1,0:T(8,128)S(1)} %dynamic-slice_bitcast_fusion), channel_id=1, source_target_pairs={{0,2},{2,0},{1,3},{3,1},{4,6},{6,4},{5,7},{7,5},{8,10},{10,8},{9,1... | collective-permute-start | bytes 98312 | tf_op jit(solution)/shard_map/ppermute | solution.py:94
  35.4 11.7 %collective-permute-start.6 = (bf16[1,4,40960]{2,1,0:T(4,128)(2,1)S(1)}, bf16[1,4,40960]{2,1,0:T(4,128)(2,1)S(1)}, u32[]{:S(2)}, u32[]{:S(2)}) collective-permute-start(bf16[1,4,40960]{2,1,0:T(4,128)(2,1)S(1)} %maximum_select_fusion.1), channel_id=1, source_target_pairs={{0,2},{2,0},{1,3},{3,1},{4,6},{6,4},{5,7},{7,5},{8,10},{10,8},{9,1... | collective-permute-start | bytes 983048 | tf_op jit(solution)/shard_map/ppermute | solution.py:139
  37.6 4.2 %collective-permute-start.4 = (f32[2,32,64]{2,1,0:T(8,128)S(1)}, f32[2,32,64]{2,1,0:T(8,128)S(1)}, u32[]{:S(2)}, u32[]{:S(2)}) collective-permute-start(f32[2,32,64]{2,1,0:T(8,128)S(1)} %dynamic-slice_bitcast_fusion.1), channel_id=1, source_target_pairs={{0,4},{4,0},{8,12},{12,8},{1,5},{5,1},{9,13},{13,9},{2,6},{6,2},{1... | collective-permute-start | bytes 49160 | tf_op jit(solution)/shard_map/ppermute | solution.py:94
  41.8 4.7 %collective-permute-start.5 = (f32[32,64]{1,0:T(8,128)S(1)}, f32[32,64]{1,0:T(8,128)S(1)}, u32[]{:S(2)}, u32[]{:S(2)}) collective-permute-start(f32[32,64]{1,0:T(8,128)S(1)} %dynamic-slice_bitcast_fusion.3), channel_id=1, source_target_pairs={{0,8},{4,12},{8,0},{12,4},{1,9},{5,13},{9,1},{13,5},{2,10},{6,14},... | collective-permute-start | bytes 24584 | tf_op jit(solution)/shard_map/ppermute | solution.py:94

commit v5 on v3

--- a/solution.py
+++ b/solution.py
@@ -122,32 +122,18 @@
     return lax.dynamic_slice_in_dim(stacked, first - tap0 * chans, rows, 0)
 
 
-def group_index(names):
-    index = 0
-    for name in names:
-        index = index * lax.axis_size(name) + lax.axis_index(name)
-    return index
-
-
-def direct_gather(x, names):
+def exchange_gather(x, names):
     count = math.prod(lax.axis_size(n) for n in names)
-    pieces = [x]
-    for d in range(1, count):
-        pieces.append(lax.ppermute(x, names, [(k, k ^ d) for k in range(count)]))
-    return jnp.concatenate(pieces, axis=0)
-
-
-def direct_scatter(x, names):
+    copies = jnp.broadcast_to(x[None], (count,) + x.shape)
+    return lax.all_to_all(copies, names, 0, 0, tiled=True)
+
+
+def exchange_scatter(x, names):
     count = math.prod(lax.axis_size(n) for n in names)
     if count > 8:
         return halving_scatter(x, names)
-    index = group_index(names)
     blocks = x.reshape((count, x.shape[0] // count) + x.shape[1:])
-    total = lax.dynamic_index_in_dim(blocks, index, keepdims=False)
-    for d in range(1, count):
-        piece = lax.dynamic_index_in_dim(blocks, index ^ d, keepdims=False)
-        total = total + lax.ppermute(piece, names, [(k, k ^ d) for k in range(count)])
-    return total
+    return lax.all_to_all(blocks, names, 0, 0, tiled=True).sum(axis=0)
 
 
 def silu_slope(pre):
@@ -179,8 +165,8 @@
     shards = lax.axis_size("space") * lax.axis_size("sub")
     gather_second = shards * (width + half_o) * voxels * 2 <= 1 << 22
     if gather_second:
-        both = direct_gather(
-            jnp.concatenate([grid.reshape(width, voxels), cot], axis=0)[None], ("space", "sub")
+        both = exchange_gather(
+            jnp.concatenate([grid.reshape(width, voxels), cot], axis=0), ("space", "sub")
         )
         grad_second = (
             second_grad_rows(
@@ -219,7 +205,7 @@
         concat_axis=1,
         tiled=True,
     )
-    first_grad = direct_scatter(grad_first, ("space", "sub"))
+    first_grad = exchange_scatter(grad_first, ("space", "sub"))
     second_grad = (
         grad_second if gather_second else halving_scatter(grad_second, ("space", "sub"))
     )

time: 62.8 us -> 60.1 us (0.957)
  starting transfers between devices: 32.2 us -> 16.5 us
  waiting for transfers between devices: 9.91 us -> 21 us
  local copies, waits for them, and re-layouts: 8.32 us -> 9.56 us
  other arithmetic: 1.39 us -> 2.2 us
    ppermute x14 -> x0, starting transfers between devices: 22.5 us -> none  [the longest x7 11.3 us: direct_gather(): pieces.append(lax.ppermute(x, names, [(k, k ^ d) for k in range(count)]))]
    all_to_all x0 -> x2, waiting for transfers between devices: none -> 13.2 us  [the longest x1 6.69 us: exchange_scatter(): return lax.all_to_all(blocks, names, 0, 0, tiled=True).sum(axis=0)]
    all_to_all x0 -> x2, starting transfers between devices: none -> 6.8 us  [the longest x1 3.45 us: exchange_gather(): return lax.all_to_all(copies, names, 0, 0, tiled=True)]
    ppermute x14 -> x0, waiting for transfers between devices: 6.63 us -> none  [the longest x7 6.62 us: direct_gather(): pieces.append(lax.ppermute(x, names, [(k, k ^ d) for k in range(count)]))]
    all_to_all x1, waiting for transfers between devices: 0.01 us -> 4.43 us  [block(): lax.all_to_all(grad_sample.reshape(1, 1, half_c, depth, XY * XY), 'space'...]
    reshape x10 -> x0, local copies, waits for them, and re-layouts: 0.94 us -> none  [plane_stack(): windows.append(window.reshape(chans, depth * side * side))]
    all_to_all x0 -> x1, other arithmetic: none -> 0.8 us  [exchange_scatter(): return lax.all_to_all(blocks, names, 0, 0, tiled=True).sum(axis=0)]
    broadcast_in_dim x0 -> x1, local copies, waits for them, and re-layouts: none -> 0.79 us  [exchange_gather(): copies = jnp.broadcast_to(x[None], (count,) + x.shape)]
  transfers between devices with their start and end apart: 17 -> 5, of which waited for: 4 -> 4; matrix products, arithmetic and copies ran while one was open for 6% -> 9% of each run, Pallas kernels for 0% -> 0%
where the time goes in v5:
time: 60.1 us; the launch traced here: 59.6 us
  waiting for transfers between devices  21 us (35%)
  starting transfers between devices  16.5 us (27%)
  local copies, waits for them, and re-layouts  9.56 us (16%)
  blocking collectives  5.85 us (10%)
  matrix products  2.9 us (5%)
  other arithmetic  2.2 us (4%)
  between operations  1.58 us (3%)
    all_to_all x1, waiting for transfers between devices, exchange_scatter(): return lax.all_to_all(blocks, names, 0, 0, tiled=True).sum(axis=0)  6.69 us
    all_to_all x1, waiting for transfers between devices, exchange_gather(): return lax.all_to_all(copies, names, 0, 0, tiled=True)  6.54 us
    all_to_all x1, starting transfers between devices, block(): lax.all_to_all(volumes, 'space', split_axis=1, concat_axis=3, tiled=True)  5.88 us
    all_to_all x1, waiting for transfers between devices, block(): lax.all_to_all(grad_sample.reshape(1, 1, half_c, depth, XY * XY), 'space'...  4.43 us
    all_to_all x1, starting transfers between devices, exchange_gather(): return lax.all_to_all(copies, names, 0, 0, tiled=True)  3.45 us
    all_to_all x1, starting transfers between devices, exchange_scatter(): return lax.all_to_all(blocks, names, 0, 0, tiled=True).sum(axis=0)  3.35 us
    all_to_all x1, waiting for transfers between devices, block(): lax.all_to_all(volumes, 'space', split_axis=1, concat_axis=3, tiled=True)  3.34 us
    all_to_all x1, starting transfers between devices, block(): lax.all_to_all(grad_sample.reshape(1, 1, half_c, depth, XY * XY), 'space'...  3.26 us
  transfers between devices with their start and end apart: 5, of which 4 were waited for; matrix products, arithmetic and copies ran while one was open for 9% of the time, Pallas kernels for 0%

profile of v5, /device:TPU:0, one launch (start us, length us, event | category | flops | bytes accessed | tf_op | source)
XLA Modules:
  0.0 59.6 jit_solution(14651617577248143836)
XLA Ops:
  0.6 0.9 %copy.38 = bf16[1,1,64,2,64]{2,4,3,1,0:T(8,128)(2,1)S(1)} copy(bf16[1,1,64,2,64]{4,3,2,1,0:T(2,128)(2,1)} %param.5) | data formatting | bytes 32768 | tf_op args[1]
  2.4 0.3 fusion.21
  2.8 0.3 convolution_add_fusion.1
  3.2 0.3 convolution_add_fusion
  3.5 0.6 collective-permute-start
  4.1 5.9 %all-to-all-start = ((bf16[1,4,32,1,256]{4,2,3,0,1:T(8,128)(2,1)}), bf16[1,4,32,1,256]{4,2,3,0,1:T(8,128)(2,1)S(1)}, u32[]{:S(2)}, u32[]{:S(2)}) async-start(bf16[1,4,32,1,256]{4,2,3,0,1:T(8,128)(2,1)} %bitcast), calls=%async_computation | async-start | bytes 131072 | tf_op jit(solution)/shard_map/all_to_all | solution.py:149
  9.9 1.8 %all_gather.10 = bf16[256,128]{0,1:T(8,128)(2,1)S(1)} all-gather(bf16[256,64]{0,1:T(8,128)(2,1)S(1)} %copy-done.1), channel_id=1, replica_groups=mesh['groups'=2,'space'=4,'sub'=2,'ch'=2] {'ch'}, dimensions={1}, use_global_device_ids=true | all-gather | bytes 98304 | tf_op jit(solution)/shard_map/all_gather | solution.py:193
  12.3 3.3 %all-to-all-done = bf16[1,4,32,1,256]{4,2,3,0,1:T(8,128)(2,1)S(1)} async-done(((bf16[1,4,32,1,256]{4,2,3,0,1:T(8,128)(2,1)}), bf16[1,4,32,1,256]{4,2,3,0,1:T(8,128)(2,1)S(1)}, u32[]{:S(2)}, u32[]{:S(2)}) %all-to-all-start) | async-done | bytes 65568 | tf_op jit(solution)/shard_map/all_to_all | solution.py:149
  15.9 0.2 copy.32
  16.6 0.3 copy.34
  16.9 2.2 %all_gather.9 = bf16[128,2,8,8]{3,2,1,0:T(8,128)(2,1)S(1)} all-gather(bf16[64,2,8,8]{3,2,1,0:T(8,128)(2,1)S(1)} %copy.34), channel_id=1, replica_groups=mesh['groups'=2,'space'=4,'sub'=2,'ch'=2] {'ch'}, dimensions={0}, use_global_device_ids=true | all-gather | bytes 49152 | tf_op jit(solution)/shard_map/all_gather | solution.py:159
  19.0 0.4 copy.35
  19.6 1.8 %all_gather.11 = bf16[128,128]{1,0:T(8,128)(2,1)S(1)} all-gather(bf16[64,128]{1,0:T(8,128)(2,1)S(1)} %get-tuple-element.19), channel_id=1, replica_groups=mesh['groups'=2,'space'=4,'sub'=2,'ch'=2] {'ch'}, dimensions={0}, use_global_device_ids=true | all-gather | bytes 49152 | tf_op jit(solution)/shard_map/all_gather | solution.py:192
  21.8 0.3 fusion
  22.1 0.3 copy.44
  22.4 0.7 %copy.45 = bf16[1,1,16,4,256]{4,2,1,0,3:T(8,128)(2,1)} copy(bf16[1,1,16,4,256]{2,4,3,1,0:T(8,128)(2,1)S(1)} %bitcast.173) | data formatting | bytes 65536 | tf_op jit(solution)/shard_map/convert_element_type | solution.py:200
  23.1 3.3 %all-to-all-start.1 = ((bf16[1,1,16,4,256]{4,2,1,0,3:T(8,128)(2,1)}), bf16[1,1,16,4,256]{4,2,1,0,3:T(8,128)(2,1)S(1)}, u32[]{:S(2)}, u32[]{:S(2)}) async-start(bf16[1,1,16,4,256]{4,2,1,0,3:T(8,128)(2,1)} %copy.45), calls=%async_computation.1 | async-start | bytes 65536 | tf_op jit(solution)/shard_map/all_to_all | solution.py:201
  26.8 0.8 %reshape.318 = f32[8,1,2048]{2,1,0:T(1,128)} reshape(f32[8,32,64]{2,1,0:T(8,128)S(1)} %bitcast.183) | data formatting | bytes 131072
  27.6 4.4 %all-to-all-done.1 = bf16[1,1,16,4,256]{4,2,1,0,3:T(8,128)(2,1)S(1)} async-done(((bf16[1,1,16,4,256]{4,2,1,0,3:T(8,128)(2,1)}), bf16[1,1,16,4,256]{4,2,1,0,3:T(8,128)(2,1)S(1)}, u32[]{:S(2)}, u32[]{:S(2)}) %all-to-all-start.1) | async-done | bytes 32800 | tf_op jit(solution)/shard_map/all_to_all | solution.py:201
  32.0 3.4 %all-to-all-start.2 = ((f32[8,1,2048]{2,1,0:T(1,128)}), f32[8,1,2048]{2,1,0:T(1,128)S(1)}, u32[]{:S(2)}, u32[]{:S(2)}) async-start(f32[8,1,2048]{2,1,0:T(1,128)} %reshape.318), calls=%async_computation.2 | async-start | bytes 131072 | tf_op jit(solution)/shard_map/all_to_all | solution.py:136
  35.5 6.7 %all-to-all-done.2 = f32[8,1,2048]{2,1,0:T(1,128)S(1)} async-done(((f32[8,1,2048]{2,1,0:T(1,128)}), f32[8,1,2048]{2,1,0:T(1,128)S(1)}, u32[]{:S(2)}, u32[]{:S(2)}) %all-to-all-start.2) | async-done | bytes 65568 | tf_op jit(solution)/shard_map/all_to_all | solution.py:136
  42.2 0.8 %broadcast_in_dim.2 = bf16[8,192,128]{2,1,0:T(8,128)(2,1)} broadcast(bf16[192,128]{1,0:T(8,128)(2,1)S(1)} %copy.47), dimensions={1,2} | broadcast | bytes 442368 | tf_op jit(solution)/shard_map/broadcast_in_dim | solution.py:127
  43.0 3.5 %all-to-all-start.3 = ((bf16[8,192,128]{2,1,0:T(8,128)(2,1)}), bf16[8,192,128]{2,1,0:T(8,128)(2,1)S(1)}, u32[]{:S(2)}, u32[]{:S(2)}) async-start(bf16[8,192,128]{2,1,0:T(8,128)(2,1)} %broadcast_in_dim.2), calls=%async_computation.3 | async-start | bytes 786432 | tf_op jit(solution)/shard_map/all_to_all | solution.py:128
  46.9 0.2 fusion.8
  47.2 0.7 %reshape.271 = bf16[1,1,64,2,64]{4,3,2,1,0:T(2,128)(2,1)} reshape(bf16[64,128]{1,0:T(8,128)(2,1)S(1)} %fusion.8) | data formatting | bytes 32768 | tf_op jit(solution)/shard_map/reshape | solution.py:162
  47.9 0.5 broadcast.13
  48.4 0.8 %reduce = f32[8,2048]{1,0:T(8,128)S(1)} reduce(f32[8,1,2048]{2,1,0:T(1,128)S(1)} %all-to-all-done.2, f32[]{:T(128)} %broadcast.13), dimensions={1}, to_apply=%all_to_all.37.reduce_sub_computation | reduce | bytes 131076 | tf_op jit(solution)/shard_map/all_to_all | solution.py:136
  49.3 0.6 %reduce_sum.9 = f32[32,64]{1,0:T(8,128)} reduce(f32[8,32,64]{2,1,0:T(8,128)S(1)} %reshape.319, f32[]{:T(128)} %constant.112.clone.1), dimensions={0}, to_apply=%region_0.1 | reduce | flops 14336 | bytes 73732 | tf_op jit(solution)/shard_map/reduce_sum | solution.py:136
  49.9 6.5 %all-to-all-done.3 = bf16[8,192,128]{2,1,0:T(8,128)(2,1)S(1)} async-done(((bf16[8,192,128]{2,1,0:T(8,128)(2,1)}), bf16[8,192,128]{2,1,0:T(8,128)(2,1)S(1)}, u32[]{:S(2)}, u32[]{:S(2)}) %all-to-all-start.3) | async-done | bytes 393248 | tf_op jit(solution)/shard_map/all_to_all | solution.py:128
  56.8 0.5 pad_dynamic-slice_fusion
  58.2 0.8 %dynamic-slice_multiply_fusion = f32[432,64]{0,1:T(8,128)} fusion(f32[640,64]{0,1:T(8,128)S(1)} %fusion.2, s32[]{:T(128)S(6)} %select_n.174), kind=kLoop, calls=%fused_computation.77 | loop fusion | flops 27648 | bytes 221188 | tf_op jit(solution)/shard_map/mul | solution.py:172
  59.0 0.6 %copy.91 = bf16[1,4,16,1,256]{4,2,3,1,0:T(8,128)(2,1)} copy(bf16[1,4,16,1,256]{4,2,3,1,0:T(8,128)(2,1)S(1)} %bitcast.235) | data formatting | bytes 65536
  (69 shorter events, 4.4 us)
Async XLA Ops:
  0.6 1.1 %copy-start = (bf16[3456,64]{0,1:T(8,128)(2,1)S(1)}, bf16[3456,64]{0,1:T(8,128)(2,1)}, u32[]{:S(2)}) copy-start(bf16[3456,64]{0,1:T(8,128)(2,1)} %param.7) | copy-start | bytes 1327108
  3.0 6.9 %copy-start.1 = (bf16[256,64]{0,1:T(8,128)(2,1)S(1)}, bf16[256,64]{0,1:T(8,128)(2,1)}, u32[]{:S(2)}) copy-start(bf16[256,64]{0,1:T(8,128)(2,1)} %param.6) | copy-start | bytes 98308
  3.5 12.8 %collective-permute-start = (f32[64,128]{1,0:T(8,128)S(1)}, f32[64,128]{1,0:T(8,128)S(1)}, u32[]{:S(2)}, u32[]{:S(2)}) collective-permute-start(f32[64,128]{1,0:T(8,128)S(1)} %dynamic-slice_bitcast_fusion), channel_id=1, source_target_pairs={{0,1},{1,0},{2,3},{3,2},{4,5},{5,4},{6,7},{7,6},{8,9},{9,8},{10,11... | collective-permute-start | bytes 98312 | tf_op jit(solution)/shard_map/ppermute | solution.py:94
  4.1 11.6 %all-to-all-start = ((bf16[1,4,32,1,256]{4,2,3,0,1:T(8,128)(2,1)}), bf16[1,4,32,1,256]{4,2,3,0,1:T(8,128)(2,1)S(1)}, u32[]{:S(2)}, u32[]{:S(2)}) async-start(bf16[1,4,32,1,256]{4,2,3,0,1:T(8,128)(2,1)} %bitcast), calls=%async_computation | async-start | bytes 131072 | tf_op jit(solution)/shard_map/all_to_all | solution.py:149
  23.1 8.9 %all-to-all-start.1 = ((bf16[1,1,16,4,256]{4,2,1,0,3:T(8,128)(2,1)}), bf16[1,1,16,4,256]{4,2,1,0,3:T(8,128)(2,1)S(1)}, u32[]{:S(2)}, u32[]{:S(2)}) async-start(bf16[1,1,16,4,256]{4,2,1,0,3:T(8,128)(2,1)} %copy.45), calls=%async_computation.1 | async-start | bytes 65536 | tf_op jit(solution)/shard_map/all_to_all | solution.py:201
  32.0 10.2 %all-to-all-start.2 = ((f32[8,1,2048]{2,1,0:T(1,128)}), f32[8,1,2048]{2,1,0:T(1,128)S(1)}, u32[]{:S(2)}, u32[]{:S(2)}) async-start(f32[8,1,2048]{2,1,0:T(1,128)} %reshape.318), calls=%async_computation.2 | async-start | bytes 131072 | tf_op jit(solution)/shard_map/all_to_all | solution.py:136
  43.0 13.4 %all-to-all-start.3 = ((bf16[8,192,128]{2,1,0:T(8,128)(2,1)}), bf16[8,192,128]{2,1,0:T(8,128)(2,1)S(1)}, u32[]{:S(2)}, u32[]{:S(2)}) async-start(bf16[8,192,128]{2,1,0:T(8,128)(2,1)} %broadcast_in_dim.2), calls=%async_computation.3 | async-start | bytes 786432 | tf_op jit(solution)/shard_map/all_to_all | solution.py:128

commit v6 on v5

--- a/solution.py
+++ b/solution.py
@@ -93,6 +93,15 @@
             perm = [(i, i ^ (1 << j)) for i in range(size)]
             x = mine + lax.ppermute(other, name, perm)
             labels.pop(pos)
+    return x
+
+
+def doubling_gather(x, names):
+    for name in names:
+        size = lax.axis_size(name)
+        for j in reversed(range(size.bit_length() - 1)):
+            perm = [(i, i ^ (1 << j)) for i in range(size)]
+            x = jnp.concatenate([x, lax.ppermute(x, name, perm)], axis=0)
     return x
 
 
@@ -122,20 +131,6 @@
     return lax.dynamic_slice_in_dim(stacked, first - tap0 * chans, rows, 0)
 
 
-def exchange_gather(x, names):
-    count = math.prod(lax.axis_size(n) for n in names)
-    copies = jnp.broadcast_to(x[None], (count,) + x.shape)
-    return lax.all_to_all(copies, names, 0, 0, tiled=True)
-
-
-def exchange_scatter(x, names):
-    count = math.prod(lax.axis_size(n) for n in names)
-    if count > 8:
-        return halving_scatter(x, names)
-    blocks = x.reshape((count, x.shape[0] // count) + x.shape[1:])
-    return lax.all_to_all(blocks, names, 0, 0, tiled=True).sum(axis=0)
-
-
 def silu_slope(pre):
     sig = jax.nn.sigmoid(pre)
     return sig * (1.0 + pre * (1.0 - sig))
@@ -165,8 +160,8 @@
     shards = lax.axis_size("space") * lax.axis_size("sub")
     gather_second = shards * (width + half_o) * voxels * 2 <= 1 << 22
     if gather_second:
-        both = exchange_gather(
-            jnp.concatenate([grid.reshape(width, voxels), cot], axis=0), ("space", "sub")
+        both = doubling_gather(
+            jnp.concatenate([grid.reshape(width, voxels), cot], axis=0)[None], ("space", "sub")
         )
         grad_second = (
             second_grad_rows(
@@ -205,7 +200,7 @@
         concat_axis=1,
         tiled=True,
     )
-    first_grad = exchange_scatter(grad_first, ("space", "sub"))
+    first_grad = halving_scatter(grad_first, ("space", "sub"))
     second_grad = (
         grad_second if gather_second else halving_scatter(grad_second, ("space", "sub"))
     )

time: 60.1 us -> 52.2 us (0.87)
  waiting for transfers between devices: 21 us -> 12.8 us
  starting transfers between devices: 16.5 us -> 18.9 us
  local copies, waits for them, and re-layouts: 9.56 us -> 8.24 us
  other arithmetic: 2.2 us -> 1.46 us
    all_to_all x2 -> x0, waiting for transfers between devices: 13.2 us -> none  [the longest x1 6.69 us: exchange_scatter(): return lax.all_to_all(blocks, names, 0, 0, tiled=True).sum(axis=0)]
    ppermute x0 -> x3, waiting for transfers between devices: none -> 9.44 us  [doubling_gather(): x = jnp.concatenate([x, lax.ppermute(x, name, perm)], axis=0)]
    all_to_all x2 -> x0, starting transfers between devices: 6.8 us -> none  [the longest x1 3.45 us: exchange_gather(): return lax.all_to_all(copies, names, 0, 0, tiled=True)]
    ppermute x1 -> x4, starting transfers between devices: 0.56 us -> 6.69 us  [halving_scatter(): x = mine + lax.ppermute(other, name, perm)]
    all_to_all x1, waiting for transfers between devices: 4.43 us -> 0.01 us  [block(): lax.all_to_all(grad_sample.reshape(1, 1, half_c, depth, XY * XY), 'space'...]
    ppermute x0 -> x3, starting transfers between devices: none -> 3.11 us  [doubling_gather(): x = jnp.concatenate([x, lax.ppermute(x, name, perm)], axis=0)]
    reshape x0 -> x10, local copies, waits for them, and re-layouts: none -> 0.94 us  [plane_stack(): windows.append(window.reshape(chans, depth * side * side))]
    all_to_all x1 -> x0, other arithmetic: 0.8 us -> none  [exchange_scatter(): return lax.all_to_all(blocks, names, 0, 0, tiled=True).sum(axis=0)]
  transfers between devices with their start and end apart: 5 -> 9, of which waited for: 4 -> 4; matrix products, arithmetic and copies ran while one was open for 9% -> 8% of each run, Pallas kernels for 0% -> 0%
where the time goes in v6:
time: 52.2 us; the launch traced here: 51.9 us
  starting transfers between devices  18.9 us (36%)
  waiting for transfers between devices  12.8 us (25%)
  local copies, waits for them, and re-layouts  8.24 us (16%)
  blocking collectives  5.85 us (11%)
  matrix products  2.88 us (6%)
  between operations  1.71 us (3%)
  other arithmetic  1.46 us (3%)
    ppermute x3, waiting for transfers between devices, doubling_gather(): x = jnp.concatenate([x, lax.ppermute(x, name, perm)], axis=0)  9.44 us
    ppermute x4, starting transfers between devices, halving_scatter(): x = mine + lax.ppermute(other, name, perm)  6.69 us
    all_to_all x1, starting transfers between devices, block(): lax.all_to_all(volumes, 'space', split_axis=1, concat_axis=3, tiled=True)  5.88 us
    all_to_all x1, waiting for transfers between devices, block(): lax.all_to_all(volumes, 'space', split_axis=1, concat_axis=3, tiled=True)  3.33 us
    all_to_all x1, starting transfers between devices, block(): lax.all_to_all(grad_sample.reshape(1, 1, half_c, depth, XY * XY), 'space'...  3.26 us
    ppermute x3, starting transfers between devices, doubling_gather(): x = jnp.concatenate([x, lax.ppermute(x, name, perm)], axis=0)  3.11 us
    all_gather x1, blocking collectives, block(): lax.all_gather(hidden.reshape(half_o, half_z, half_s, half_s), 'ch', axis...  2.18 us
    unnamed x40, local copies, waits for them, and re-layouts  1.97 us
  transfers between devices with their start and end apart: 9, of which 4 were waited for; matrix products, arithmetic and copies ran while one was open for 8% of the time, Pallas kernels for 0%

profile of v6, /device:TPU:0, one launch (start us, length us, event | category | flops | bytes accessed | tf_op | source)
XLA Modules:
  0.0 51.9 jit_solution(17937538232933895312)
XLA Ops:
  0.7 0.9 %copy.47 = bf16[1,1,64,2,64]{2,4,3,1,0:T(8,128)(2,1)S(1)} copy(bf16[1,1,64,2,64]{4,3,2,1,0:T(2,128)(2,1)} %param.5) | data formatting | bytes 32768 | tf_op args[1]
  3.3 0.3 fusion.18
  3.7 0.3 fusion.17
  4.1 0.3 fusion.2
  4.4 0.6 %collective-permute-start = (f32[64,128]{1,0:T(8,128)S(1)}, f32[64,128]{1,0:T(8,128)S(1)}, u32[]{:S(2)}, u32[]{:S(2)}) collective-permute-start(f32[64,128]{1,0:T(8,128)S(1)} %dynamic-slice_bitcast_fusion.2), channel_id=1, source_target_pairs={{0,1},{1,0},{2,3},{3,2},{4,5},{5,4},{6,7},{7,6},{8,9},{9,8},{10,11... | collective-permute-start | bytes 98312 | tf_op jit(solution)/shard_map/ppermute | solution.py:94
  4.9 5.9 %all-to-all-start = ((bf16[1,4,32,1,256]{4,2,3,0,1:T(8,128)(2,1)}), bf16[1,4,32,1,256]{4,2,3,0,1:T(8,128)(2,1)S(1)}, u32[]{:S(2)}, u32[]{:S(2)}) async-start(bf16[1,4,32,1,256]{4,2,3,0,1:T(8,128)(2,1)} %bitcast), calls=%async_computation | async-start | bytes 131072 | tf_op jit(solution)/shard_map/all_to_all | solution.py:144
  10.8 1.8 %all_gather.10 = bf16[256,128]{0,1:T(8,128)(2,1)S(1)} all-gather(bf16[256,64]{0,1:T(8,128)(2,1)S(1)} %copy-done.2), channel_id=1, replica_groups=mesh['groups'=2,'space'=4,'sub'=2,'ch'=2] {'ch'}, dimensions={1}, use_global_device_ids=true | all-gather | bytes 98304 | tf_op jit(solution)/shard_map/all_gather | solution.py:188
  13.2 3.3 %all-to-all-done = bf16[1,4,32,1,256]{4,2,3,0,1:T(8,128)(2,1)S(1)} async-done(((bf16[1,4,32,1,256]{4,2,3,0,1:T(8,128)(2,1)}), bf16[1,4,32,1,256]{4,2,3,0,1:T(8,128)(2,1)S(1)}, u32[]{:S(2)}, u32[]{:S(2)}) %all-to-all-start) | async-done | bytes 65568 | tf_op jit(solution)/shard_map/all_to_all | solution.py:144
  16.7 0.2 copy.41
  17.5 0.3 copy.43
  17.8 2.2 %all_gather.9 = bf16[128,2,8,8]{3,2,1,0:T(8,128)(2,1)S(1)} all-gather(bf16[64,2,8,8]{3,2,1,0:T(8,128)(2,1)S(1)} %copy.43), channel_id=1, replica_groups=mesh['groups'=2,'space'=4,'sub'=2,'ch'=2] {'ch'}, dimensions={0}, use_global_device_ids=true | all-gather | bytes 49152 | tf_op jit(solution)/shard_map/all_gather | solution.py:154
  19.9 0.4 copy.44
  20.5 1.8 %all_gather.11 = bf16[128,128]{1,0:T(8,128)(2,1)S(1)} all-gather(bf16[64,128]{1,0:T(8,128)(2,1)S(1)} %get-tuple-element.19), channel_id=1, replica_groups=mesh['groups'=2,'space'=4,'sub'=2,'ch'=2] {'ch'}, dimensions={0}, use_global_device_ids=true | all-gather | bytes 49152 | tf_op jit(solution)/shard_map/all_gather | solution.py:187
  22.6 0.2 fusion.14
  23.2 1.6 %collective-permute-start.1 = (f32[2,2,32,64]{3,2,1,0:T(8,128)S(1)}, f32[2,2,32,64]{3,2,1,0:T(8,128)S(1)}, u32[]{:S(2)}, u32[]{:S(2)}) collective-permute-start(f32[2,2,32,64]{3,2,1,0:T(8,128)S(1)} %dynamic-slice_bitcast_fusion), channel_id=1, source_target_pairs={{0,2},{2,0},{1,3},{3,1},{4,6},{6,4},{5,7},{7,5},{8,10},{10,8},{9,1... | collective-permute-start | bytes 98312 | tf_op jit(solution)/shard_map/ppermute | solution.py:94
  25.2 0.2 fusion.9
  25.4 0.3 fusion
  25.8 0.7 %reshape.270 = bf16[1,1,64,2,64]{4,3,2,1,0:T(2,128)(2,1)} reshape(bf16[64,128]{1,0:T(8,128)(2,1)S(1)} %fusion.9) | data formatting | bytes 32768 | tf_op jit(solution)/shard_map/reshape | solution.py:157
  26.6 0.3 copy.60
  26.8 0.7 %copy.61 = bf16[1,1,16,4,256]{4,2,1,0,3:T(8,128)(2,1)} copy(bf16[1,1,16,4,256]{2,4,3,1,0:T(8,128)(2,1)S(1)} %bitcast.191) | data formatting | bytes 65536 | tf_op jit(solution)/shard_map/convert_element_type | solution.py:195
  27.6 3.3 %all-to-all-start.1 = ((bf16[1,1,16,4,256]{4,2,1,0,3:T(8,128)(2,1)}), bf16[1,1,16,4,256]{4,2,1,0,3:T(8,128)(2,1)S(1)}, u32[]{:S(2)}, u32[]{:S(2)}) async-start(bf16[1,1,16,4,256]{4,2,1,0,3:T(8,128)(2,1)} %copy.61), calls=%async_computation.1 | async-start | bytes 65536 | tf_op jit(solution)/shard_map/all_to_all | solution.py:196
  30.9 2.0 %collective-permute-start.2 = (f32[2,32,64]{2,1,0:T(8,128)S(1)}, f32[2,32,64]{2,1,0:T(8,128)S(1)}, u32[]{:S(2)}, u32[]{:S(2)}) collective-permute-start(f32[2,32,64]{2,1,0:T(8,128)S(1)} %dynamic-slice_bitcast_fusion.1), channel_id=1, source_target_pairs={{0,4},{4,0},{8,12},{12,8},{1,5},{5,1},{9,13},{13,9},{2,6},{6,2},{1... | collective-permute-start | bytes 49160 | tf_op jit(solution)/shard_map/ppermute | solution.py:94
  32.9 2.4 %collective-permute-start.4 = (bf16[1,192,128]{2,1,0:T(8,128)(2,1)S(1)}, bf16[1,192,128]{2,1,0:T(8,128)(2,1)S(1)}, u32[]{:S(2)}, u32[]{:S(2)}) collective-permute-start(bf16[1,192,128]{2,1,0:T(8,128)(2,1)S(1)} %maximum_bitcast_fusion), channel_id=1, source_target_pairs={{0,8},{4,12},{8,0},{12,4},{1,9},{5,13},{9,1},{13,5},{2,10},{6,14},... | collective-permute-start | bytes 147464 | tf_op jit(solution)/shard_map/ppermute | solution.py:104
  35.3 2.9 %collective-permute-done.4 = bf16[1,192,128]{2,1,0:T(8,128)(2,1)S(1)} collective-permute-done((bf16[1,192,128]{2,1,0:T(8,128)(2,1)S(1)}, bf16[1,192,128]{2,1,0:T(8,128)(2,1)S(1)}, u32[]{:S(2)}, u32[]{:S(2)}) %collective-permute-start.4) | collective-permute-done | bytes 49184 | tf_op jit(solution)/shard_map/ppermute | solution.py:104
  38.4 2.5 %collective-permute-start.3 = (f32[32,64]{1,0:T(8,128)S(1)}, f32[32,64]{1,0:T(8,128)S(1)}, u32[]{:S(2)}, u32[]{:S(2)}) collective-permute-start(f32[32,64]{1,0:T(8,128)S(1)} %dynamic-slice_bitcast_fusion.3), channel_id=1, source_target_pairs={{0,8},{4,12},{8,0},{12,4},{1,9},{5,13},{9,1},{13,5},{2,10},{6,14},... | collective-permute-start | bytes 24584 | tf_op jit(solution)/shard_map/ppermute | solution.py:94
  40.9 2.0 %collective-permute-done.5 = bf16[2,192,128]{2,1,0:T(8,128)(2,1)S(1)} collective-permute-done((bf16[2,192,128]{2,1,0:T(8,128)(2,1)S(1)}, bf16[2,192,128]{2,1,0:T(8,128)(2,1)S(1)}, u32[]{:S(2)}, u32[]{:S(2)}) %collective-permute-start.5) | collective-permute-done | bytes 98336 | tf_op jit(solution)/shard_map/ppermute | solution.py:104
  43.0 0.6 %collective-permute-start.6 = (bf16[4,192,128]{2,1,0:T(8,128)(2,1)S(1)}, bf16[4,192,128]{2,1,0:T(8,128)(2,1)S(1)}, u32[]{:S(2)}, u32[]{:S(2)}) collective-permute-start(bf16[4,192,128]{2,1,0:T(8,128)(2,1)S(1)} %pad_maximum_fusion.3), channel_id=1, source_target_pairs={{0,2},{2,0},{1,3},{3,1},{4,6},{6,4},{5,7},{7,5},{8,10},{10,8},{9,1... | collective-permute-start | bytes 589832 | tf_op jit(solution)/shard_map/ppermute | solution.py:104
  43.6 0.6 %bitcast_add_fusion.3 = f32[32,64]{1,0:T(8,128)} fusion(f32[32,64]{1,0:T(8,128)S(1)} %collective-permute-done.3, f32[2,32,64]{2,1,0:T(8,128)S(1)} %bitcast_add_fusion.1, s32[]{:T(128)S(6)} %select_n.163), kind=kLoop, calls=%fused_computation.131 | loop fusion | flops 2048 | bytes 24580 | tf_op jit(solution)/shard_map/add | solution.py:94
  44.2 4.5 %collective-permute-done.6 = bf16[4,192,128]{2,1,0:T(8,128)(2,1)S(1)} collective-permute-done((bf16[4,192,128]{2,1,0:T(8,128)(2,1)S(1)}, bf16[4,192,128]{2,1,0:T(8,128)(2,1)S(1)}, u32[]{:S(2)}, u32[]{:S(2)}) %collective-permute-start.6) | collective-permute-done | bytes 196640 | tf_op jit(solution)/shard_map/ppermute | solution.py:104
  49.2 0.5 pad_dynamic-slice_fusion
  50.5 0.8 %dynamic-slice_multiply_fusion = f32[432,64]{0,1:T(8,128)} fusion(f32[640,64]{0,1:T(8,128)S(1)} %fusion.3, s32[]{:T(128)S(6)} %select_n.201), kind=kLoop, calls=%fused_computation.82 | loop fusion | flops 27648 | bytes 221188 | tf_op jit(solution)/shard_map/mul | solution.py:167
  51.3 0.6 %copy.115 = bf16[1,4,16,1,256]{4,2,3,1,0:T(8,128)(2,1)} copy(bf16[1,4,16,1,256]{4,2,3,1,0:T(8,128)(2,1)S(1)} %bitcast.252) | data formatting | bytes 65536
  (99 shorter events, 5.2 us)
Async XLA Ops:
  0.6 1.1 %copy-start.1 = (bf16[1,1,64,2,64]{4,3,2,1,0:T(2,128)(2,1)S(1)}, bf16[1,1,64,2,64]{4,3,2,1,0:T(2,128)(2,1)}, u32[]{:S(2)}) copy-start(bf16[1,1,64,2,64]{4,3,2,1,0:T(2,128)(2,1)} %param.5) | copy-start | bytes 49156
  0.6 1.2 %copy-start = (bf16[3456,64]{0,1:T(8,128)(2,1)S(1)}, bf16[3456,64]{0,1:T(8,128)(2,1)}, u32[]{:S(2)}) copy-start(bf16[3456,64]{0,1:T(8,128)(2,1)} %param.7) | copy-start | bytes 1327108
  4.0 6.9 %copy-start.2 = (bf16[256,64]{0,1:T(8,128)(2,1)S(1)}, bf16[256,64]{0,1:T(8,128)(2,1)}, u32[]{:S(2)}) copy-start(bf16[256,64]{0,1:T(8,128)(2,1)} %param.6) | copy-start | bytes 98308
  4.4 12.8 %collective-permute-start = (f32[64,128]{1,0:T(8,128)S(1)}, f32[64,128]{1,0:T(8,128)S(1)}, u32[]{:S(2)}, u32[]{:S(2)}) collective-permute-start(f32[64,128]{1,0:T(8,128)S(1)} %dynamic-slice_bitcast_fusion.2), channel_id=1, source_target_pairs={{0,1},{1,0},{2,3},{3,2},{4,5},{5,4},{6,7},{7,6},{8,9},{9,8},{10,11... | collective-permute-start | bytes 98312 | tf_op jit(solution)/shard_map/ppermute | solution.py:94
  4.9 11.6 %all-to-all-start = ((bf16[1,4,32,1,256]{4,2,3,0,1:T(8,128)(2,1)}), bf16[1,4,32,1,256]{4,2,3,0,1:T(8,128)(2,1)S(1)}, u32[]{:S(2)}, u32[]{:S(2)}) async-start(bf16[1,4,32,1,256]{4,2,3,0,1:T(8,128)(2,1)} %bitcast), calls=%async_computation | async-start | bytes 131072 | tf_op jit(solution)/shard_map/all_to_all | solution.py:144
  23.2 7.7 %collective-permute-start.1 = (f32[2,2,32,64]{3,2,1,0:T(8,128)S(1)}, f32[2,2,32,64]{3,2,1,0:T(8,128)S(1)}, u32[]{:S(2)}, u32[]{:S(2)}) collective-permute-start(f32[2,2,32,64]{3,2,1,0:T(8,128)S(1)} %dynamic-slice_bitcast_fusion), channel_id=1, source_target_pairs={{0,2},{2,0},{1,3},{3,1},{4,6},{6,4},{5,7},{7,5},{8,10},{10,8},{9,1... | collective-permute-start | bytes 98312 | tf_op jit(solution)/shard_map/ppermute | solution.py:94
  27.6 13.4 %all-to-all-start.1 = ((bf16[1,1,16,4,256]{4,2,1,0,3:T(8,128)(2,1)}), bf16[1,1,16,4,256]{4,2,1,0,3:T(8,128)(2,1)S(1)}, u32[]{:S(2)}, u32[]{:S(2)}) async-start(bf16[1,1,16,4,256]{4,2,1,0,3:T(8,128)(2,1)} %copy.61), calls=%async_computation.1 | async-start | bytes 65536 | tf_op jit(solution)/shard_map/all_to_all | solution.py:196
  30.9 4.4 %collective-permute-start.2 = (f32[2,32,64]{2,1,0:T(8,128)S(1)}, f32[2,32,64]{2,1,0:T(8,128)S(1)}, u32[]{:S(2)}, u32[]{:S(2)}) collective-permute-start(f32[2,32,64]{2,1,0:T(8,128)S(1)} %dynamic-slice_bitcast_fusion.1), channel_id=1, source_target_pairs={{0,4},{4,0},{8,12},{12,8},{1,5},{5,1},{9,13},{13,9},{2,6},{6,2},{1... | collective-permute-start | bytes 49160 | tf_op jit(solution)/shard_map/ppermute | solution.py:94
  32.9 5.3 %collective-permute-start.4 = (bf16[1,192,128]{2,1,0:T(8,128)(2,1)S(1)}, bf16[1,192,128]{2,1,0:T(8,128)(2,1)S(1)}, u32[]{:S(2)}, u32[]{:S(2)}) collective-permute-start(bf16[1,192,128]{2,1,0:T(8,128)(2,1)S(1)} %maximum_bitcast_fusion), channel_id=1, source_target_pairs={{0,8},{4,12},{8,0},{12,4},{1,9},{5,13},{9,1},{13,5},{2,10},{6,14},... | collective-permute-start | bytes 147464 | tf_op jit(solution)/shard_map/ppermute | solution.py:104
  38.2 4.7 %collective-permute-start.5 = (bf16[2,192,128]{2,1,0:T(8,128)(2,1)S(1)}, bf16[2,192,128]{2,1,0:T(8,128)(2,1)S(1)}, u32[]{:S(2)}, u32[]{:S(2)}) collective-permute-start(bf16[2,192,128]{2,1,0:T(8,128)(2,1)S(1)} %pad_maximum_fusion.5), channel_id=1, source_target_pairs={{0,4},{4,0},{8,12},{12,8},{1,5},{5,1},{9,13},{13,9},{2,6},{6,2},{1... | collective-permute-start | bytes 294920 | tf_op jit(solution)/shard_map/ppermute | solution.py:104
  38.4 5.2 %collective-permute-start.3 = (f32[32,64]{1,0:T(8,128)S(1)}, f32[32,64]{1,0:T(8,128)S(1)}, u32[]{:S(2)}, u32[]{:S(2)}) collective-permute-start(f32[32,64]{1,0:T(8,128)S(1)} %dynamic-slice_bitcast_fusion.3), channel_id=1, source_target_pairs={{0,8},{4,12},{8,0},{12,4},{1,9},{5,13},{9,1},{13,5},{2,10},{6,14},... | collective-permute-start | bytes 24584 | tf_op jit(solution)/shard_map/ppermute | solution.py:94
  43.0 5.7 %collective-permute-start.6 = (bf16[4,192,128]{2,1,0:T(8,128)(2,1)S(1)}, bf16[4,192,128]{2,1,0:T(8,128)(2,1)S(1)}, u32[]{:S(2)}, u32[]{:S(2)}) collective-permute-start(bf16[4,192,128]{2,1,0:T(8,128)(2,1)S(1)} %pad_maximum_fusion.3), channel_id=1, source_target_pairs={{0,2},{2,0},{1,3},{3,1},{4,6},{6,4},{5,7},{7,5},{8,10},{10,8},{9,1... | collective-permute-start | bytes 589832 | tf_op jit(solution)/shard_map/ppermute | solution.py:104

commit v7 on v6

--- a/solution.py
+++ b/solution.py
@@ -93,15 +93,6 @@
             perm = [(i, i ^ (1 << j)) for i in range(size)]
             x = mine + lax.ppermute(other, name, perm)
             labels.pop(pos)
-    return x
-
-
-def doubling_gather(x, names):
-    for name in names:
-        size = lax.axis_size(name)
-        for j in reversed(range(size.bit_length() - 1)):
-            perm = [(i, i ^ (1 << j)) for i in range(size)]
-            x = jnp.concatenate([x, lax.ppermute(x, name, perm)], axis=0)
     return x
 
 
@@ -131,6 +122,39 @@
     return lax.dynamic_slice_in_dim(stacked, first - tap0 * chans, rows, 0)
 
 
+def fused_chain(x, y, names):
+    sizes = [lax.axis_size(n) for n in names]
+    labels = []
+    for name, size in zip(names, sizes):
+        labels += [(name, j) for j in reversed(range(size.bit_length() - 1))]
+    rows = y.shape[0] // math.prod(sizes)
+    y = y.reshape((2,) * len(labels) + (rows,) + y.shape[1:])
+    lanes = x.shape[-1]
+    x = x[None]
+    for name, size in zip(names, sizes):
+        for j in reversed(range(size.bit_length() - 1)):
+            pos = labels.index((name, j))
+            bit = (lax.axis_index(name) >> j) & 1
+            mine = lax.dynamic_index_in_dim(y, bit, axis=pos, keepdims=False)
+            other = lax.dynamic_index_in_dim(y, 1 - bit, axis=pos, keepdims=False)
+            high = other.astype(jnp.bfloat16)
+            low = (other - high.astype(jnp.float32)).astype(jnp.bfloat16)
+            message = jnp.concatenate(
+                [x.reshape(-1, lanes), high.reshape(-1, lanes), low.reshape(-1, lanes)], axis=0
+            )
+            perm = [(i, i ^ (1 << j)) for i in range(size)]
+            got = lax.ppermute(message, name, perm)
+            kept, part = x.size // lanes, high.size // lanes
+            x = jnp.concatenate([x, got[:kept].reshape(x.shape)], axis=0)
+            y = (
+                mine
+                + got[kept : kept + part].reshape(high.shape).astype(jnp.float32)
+                + got[kept + part :].reshape(high.shape).astype(jnp.float32)
+            )
+            labels.pop(pos)
+    return x, y
+
+
 def silu_slope(pre):
     sig = jax.nn.sigmoid(pre)
     return sig * (1.0 + pre * (1.0 - sig))
@@ -157,23 +181,6 @@
     block_out = out.astype(jnp.bfloat16).reshape(1, 1, half_o, half_z, half_s * half_s)
     cot = cotangent.reshape(half_o, voxels)
     factor = 1.0 / math.sqrt(lax.axis_size("space") * lax.axis_size("sub") * voxels)
-    shards = lax.axis_size("space") * lax.axis_size("sub")
-    gather_second = shards * (width + half_o) * voxels * 2 <= 1 << 22
-    if gather_second:
-        both = doubling_gather(
-            jnp.concatenate([grid.reshape(width, voxels), cot], axis=0)[None], ("space", "sub")
-        )
-        grad_second = (
-            second_grad_rows(
-                both[:, :width].reshape(both.shape[0], width, half_z, half_s, half_s),
-                both[:, width:],
-                ("space", "sub"),
-                second_weight.shape[0],
-            )
-            * factor
-        )
-    else:
-        grad_second = conv_weight_grad(grid, cot) * factor
     cot_grid = cot.reshape(half_o, half_z, half_s, half_s)
     local_rows = second_weight.reshape(27, width, half_o)
     hidden_grad = halving_scatter(conv_back(cot_grid, local_rows), ("ch",))
@@ -184,6 +191,28 @@
         )
         * factor
     )
+    shards = lax.axis_size("space") * lax.axis_size("sub")
+    gather_second = shards * (width + half_o) * voxels * 2 <= 1 << 22
+    gather_second = gather_second and (grad_first.size // shards) % voxels == 0
+    if gather_second:
+        both, first_grad = fused_chain(
+            jnp.concatenate([grid.reshape(width, voxels), cot], axis=0),
+            grad_first,
+            ("space", "sub"),
+        )
+        second_grad = (
+            second_grad_rows(
+                both[:, :width].reshape(both.shape[0], width, half_z, half_s, half_s),
+                both[:, width:],
+                ("space", "sub"),
+                second_weight.shape[0],
+            )
+            * factor
+        )
+    else:
+        grad_second = conv_weight_grad(grid, cot) * factor
+        first_grad = halving_scatter(grad_first, ("space", "sub"))
+        second_grad = halving_scatter(grad_second, ("space", "sub"))
     all_pre_grad = lax.all_gather(pre_grad, "ch", axis=0, tiled=True)
     all_first = lax.all_gather(first_weight, "ch", axis=1, tiled=True)
     first_rows = lax.dynamic_slice_in_dim(
@@ -199,10 +228,6 @@
         split_axis=3,
         concat_axis=1,
         tiled=True,
-    )
-    first_grad = halving_scatter(grad_first, ("space", "sub"))
-    second_grad = (
-        grad_second if gather_second else halving_scatter(grad_second, ("space", "sub"))
     )
     return (block_out, volume_grad, first_grad, second_grad)
 

time: 52.2 us -> 51.5 us (0.987)
  starting transfers between devices: 18.9 us -> 14.4 us
  waiting for transfers between devices: 12.8 us -> 15.7 us
  local copies, waits for them, and re-layouts: 8.24 us -> 8.95 us
    ppermute x4 -> x1, starting transfers between devices: 6.69 us -> 0.56 us  [halving_scatter(): x = mine + lax.ppermute(other, name, perm)]
    ppermute x3, waiting for transfers between devices: 9.44 us -> 12.4 us  [fused_chain(): got = lax.ppermute(message, name, perm)]
    ppermute x3, starting transfers between devices: 3.11 us -> 4.68 us  [fused_chain(): got = lax.ppermute(message, name, perm)]
  transfers between devices with their start and end apart: 9 -> 6, of which waited for: 4 -> 4; matrix products, arithmetic and copies ran while one was open for 8% -> 6% of each run, Pallas kernels for 0% -> 0%
where the time goes in v7:
time: 51.5 us; the launch traced here: 51.1 us
  waiting for transfers between devices  15.7 us (30%)
  starting transfers between devices  14.4 us (28%)
  local copies, waits for them, and re-layouts  8.95 us (17%)
  blocking collectives  5.85 us (11%)
  matrix products  2.85 us (6%)
  between operations  1.77 us (3%)
  other arithmetic  1.56 us (3%)
    ppermute x3, waiting for transfers between devices, fused_chain(): got = lax.ppermute(message, name, perm)  12.4 us
    all_to_all x1, starting transfers between devices, block(): lax.all_to_all(volumes, 'space', split_axis=1, concat_axis=3, tiled=True)  5.88 us
    ppermute x3, starting transfers between devices, fused_chain(): got = lax.ppermute(message, name, perm)  4.68 us
    all_to_all x1, waiting for transfers between devices, block(): lax.all_to_all(volumes, 'space', split_axis=1, concat_axis=3, tiled=True)  3.33 us
    all_to_all x1, starting transfers between devices, block(): lax.all_to_all(grad_sample.reshape(1, 1, half_c, depth, XY * XY), 'space'...  3.26 us
    all_gather x1, blocking collectives, block(): lax.all_gather(hidden.reshape(half_o, half_z, half_s, half_s), 'ch', axis...  2.18 us
    unnamed x40, local copies, waits for them, and re-layouts  1.97 us
    all_gather x1, blocking collectives, block(): all_first = lax.all_gather(first_weight, 'ch', axis=1, tiled=True)  1.84 us
  transfers between devices with their start and end apart: 6, of which 4 were waited for; matrix products, arithmetic and copies ran while one was open for 6% of the time, Pallas kernels for 0%

profile of v7, /device:TPU:0, one launch (start us, length us, event | category | flops | bytes accessed | tf_op | source)
XLA Modules:
  0.0 51.1 jit_solution(16519335166436339067)
XLA Ops:
  0.7 0.9 %copy.47 = bf16[1,1,64,2,64]{2,4,3,1,0:T(8,128)(2,1)S(1)} copy(bf16[1,1,64,2,64]{4,3,2,1,0:T(2,128)(2,1)} %param.5) | data formatting | bytes 32768 | tf_op args[1]
  3.3 0.3 fusion.21
  3.7 0.3 fusion.20
  4.1 0.3 fusion.2
  4.4 0.6 %collective-permute-start = (f32[64,128]{1,0:T(8,128)S(1)}, f32[64,128]{1,0:T(8,128)S(1)}, u32[]{:S(2)}, u32[]{:S(2)}) collective-permute-start(f32[64,128]{1,0:T(8,128)S(1)} %dynamic-slice_bitcast_fusion), channel_id=1, source_target_pairs={{0,1},{1,0},{2,3},{3,2},{4,5},{5,4},{6,7},{7,6},{8,9},{9,8},{10,11... | collective-permute-start | bytes 98312 | tf_op jit(solution)/shard_map/ppermute | solution.py:94
  4.9 5.9 %all-to-all-start = ((bf16[1,4,32,1,256]{4,2,3,0,1:T(8,128)(2,1)}), bf16[1,4,32,1,256]{4,2,3,0,1:T(8,128)(2,1)S(1)}, u32[]{:S(2)}, u32[]{:S(2)}) async-start(bf16[1,4,32,1,256]{4,2,3,0,1:T(8,128)(2,1)} %bitcast), calls=%async_computation | async-start | bytes 131072 | tf_op jit(solution)/shard_map/all_to_all | solution.py:168
  10.8 1.8 %all_gather.10 = bf16[256,128]{0,1:T(8,128)(2,1)S(1)} all-gather(bf16[256,64]{0,1:T(8,128)(2,1)S(1)} %copy-done.2), channel_id=1, replica_groups=mesh['groups'=2,'space'=4,'sub'=2,'ch'=2] {'ch'}, dimensions={1}, use_global_device_ids=true | all-gather | bytes 98304 | tf_op jit(solution)/shard_map/all_gather | solution.py:217
  13.2 3.3 %all-to-all-done = bf16[1,4,32,1,256]{4,2,3,0,1:T(8,128)(2,1)S(1)} async-done(((bf16[1,4,32,1,256]{4,2,3,0,1:T(8,128)(2,1)}), bf16[1,4,32,1,256]{4,2,3,0,1:T(8,128)(2,1)S(1)}, u32[]{:S(2)}, u32[]{:S(2)}) %all-to-all-start) | async-done | bytes 65568 | tf_op jit(solution)/shard_map/all_to_all | solution.py:168
  16.7 0.2 copy.41
  17.5 0.3 copy.43
  17.8 2.2 %all_gather.9 = bf16[128,2,8,8]{3,2,1,0:T(8,128)(2,1)S(1)} all-gather(bf16[64,2,8,8]{3,2,1,0:T(8,128)(2,1)S(1)} %copy.43), channel_id=1, replica_groups=mesh['groups'=2,'space'=4,'sub'=2,'ch'=2] {'ch'}, dimensions={0}, use_global_device_ids=true | all-gather | bytes 49152 | tf_op jit(solution)/shard_map/all_gather | solution.py:178
  19.9 0.4 copy.44
  20.5 1.8 %all_gather.11 = bf16[128,128]{1,0:T(8,128)(2,1)S(1)} all-gather(bf16[64,128]{1,0:T(8,128)(2,1)S(1)} %get-tuple-element.31), channel_id=1, replica_groups=mesh['groups'=2,'space'=4,'sub'=2,'ch'=2] {'ch'}, dimensions={0}, use_global_device_ids=true | all-gather | bytes 49152 | tf_op jit(solution)/shard_map/all_gather | solution.py:216
  22.6 0.2 fusion.17
  23.2 0.3 fusion
  23.5 0.3 copy.60
  23.8 0.7 %copy.61 = bf16[1,1,16,4,256]{4,2,1,0,3:T(8,128)(2,1)} copy(bf16[1,1,16,4,256]{2,4,3,1,0:T(8,128)(2,1)S(1)} %bitcast.206) | data formatting | bytes 65536 | tf_op jit(solution)/shard_map/convert_element_type | solution.py:224
  24.5 3.3 %all-to-all-start.1 = ((bf16[1,1,16,4,256]{4,2,1,0,3:T(8,128)(2,1)}), bf16[1,1,16,4,256]{4,2,1,0,3:T(8,128)(2,1)S(1)}, u32[]{:S(2)}, u32[]{:S(2)}) async-start(bf16[1,1,16,4,256]{4,2,1,0,3:T(8,128)(2,1)} %copy.61), calls=%async_computation.1 | async-start | bytes 65536 | tf_op jit(solution)/shard_map/all_to_all | solution.py:225
  28.0 3.0 %collective-permute-start.1 = (bf16[320,128]{1,0:T(8,128)(2,1)S(1)}, bf16[320,128]{1,0:T(8,128)(2,1)S(1)}, u32[]{:S(2)}, u32[]{:S(2)}) collective-permute-start(bf16[320,128]{1,0:T(8,128)(2,1)S(1)} %pad_maximum_fusion.8), channel_id=1, source_target_pairs={{0,8},{4,12},{8,0},{12,4},{1,9},{5,13},{9,1},{13,5},{2,10},{6,14},... | collective-permute-start | bytes 245768 | tf_op jit(solution)/shard_map/ppermute | solution.py:146
  31.0 0.2 convolution_add_fusion.2
  31.4 4.4 %collective-permute-done.1 = bf16[320,128]{1,0:T(8,128)(2,1)S(1)} collective-permute-done((bf16[320,128]{1,0:T(8,128)(2,1)S(1)}, bf16[320,128]{1,0:T(8,128)(2,1)S(1)}, u32[]{:S(2)}, u32[]{:S(2)}) %collective-permute-start.1) | collective-permute-done | bytes 81952 | tf_op jit(solution)/shard_map/ppermute | solution.py:146
  36.3 4.6 %collective-permute-done.2 = bf16[448,128]{1,0:T(8,128)(2,1)S(1)} collective-permute-done((bf16[448,128]{1,0:T(8,128)(2,1)S(1)}, bf16[448,128]{1,0:T(8,128)(2,1)S(1)}, u32[]{:S(2)}, u32[]{:S(2)}) %collective-permute-start.2) | collective-permute-done | bytes 114720 | tf_op jit(solution)/shard_map/ppermute | solution.py:146
  41.3 1.6 %collective-permute-start.3 = (bf16[800,128]{1,0:T(8,128)(2,1)S(1)}, bf16[800,128]{1,0:T(8,128)(2,1)S(1)}, u32[]{:S(2)}, u32[]{:S(2)}) collective-permute-start(bf16[800,128]{1,0:T(8,128)(2,1)S(1)} %pad_maximum_fusion.3), channel_id=1, source_target_pairs={{0,2},{2,0},{1,3},{3,1},{4,6},{6,4},{5,7},{7,5},{8,10},{10,8},{9,1... | collective-permute-start | bytes 614408 | tf_op jit(solution)/shard_map/ppermute | solution.py:146
  42.9 0.2 fusion.9
  43.1 0.7 %reshape.315 = bf16[1,1,64,2,64]{4,3,2,1,0:T(2,128)(2,1)} reshape(bf16[64,128]{1,0:T(8,128)(2,1)S(1)} %fusion.9) | data formatting | bytes 32768 | tf_op jit(solution)/shard_map/reshape | solution.py:181
  43.8 3.3 %collective-permute-done.3 = bf16[800,128]{1,0:T(8,128)(2,1)S(1)} collective-permute-done((bf16[800,128]{1,0:T(8,128)(2,1)S(1)}, bf16[800,128]{1,0:T(8,128)(2,1)S(1)}, u32[]{:S(2)}, u32[]{:S(2)}) %collective-permute-start.3) | collective-permute-done | bytes 204832 | tf_op jit(solution)/shard_map/ppermute | solution.py:146
  47.4 0.2 copy.65
  47.7 0.2 fusion.7
  47.9 0.5 %pad_dynamic-slice_fusion = (bf16[8,128,2,8,8]{1,4,3,2,0:T(8,128)(2,1)S(1)}, bf16[8,128,2,8,8]{1,4,3,2,0:T(8,128)(2,1)S(1)}, bf16[8,128,2,8,8]{1,4,3,2,0:T(8,128)(2,1)S(1)}, bf16[8,128,2,8,8]{1,4,3,2,0:T(8,128)(2,1)S(1)}) fusion(s32[]{:T(128)S(6)} %select_n.195, s32[]{:T(128)S(6)} %select_n.198, s32[]{:T(128)S(6)} %select_n.200, ...), kind=kLoop, calls=%fused_computation | loop fusion | bytes 1310768 | tf_op jit(solution)/shard_map/dynamic_slice | solution.py:113
  49.1 0.8 %dynamic-slice_multiply_fusion = f32[432,64]{0,1:T(8,128)} fusion(f32[640,64]{0,1:T(8,128)S(1)} %fusion.3, s32[]{:T(128)S(6)} %select_n.201), kind=kLoop, calls=%fused_computation.83 | loop fusion | flops 27648 | bytes 221188 | tf_op jit(solution)/shard_map/mul | solution.py:204
  49.9 0.6 %fusion.14 = f32[32,64]{1,0:T(8,128)} fusion(f32[32,64]{1,0:T(8,128)S(1)} %reshape.365, f32[32,64]{1,0:T(8,128)S(1)} %reshape.364, f32[2,32,64]{2,1,0:T(8,128)S(1)} %fusion.11, s32[]{:T(128)S(6)} %select_n.163), kind=kLoop, calls=%fused_computation.139 | loop fusion | flops 4096 | bytes 32772 | tf_op jit(solution)/shard_map/add | solution.py:150
  50.5 0.6 %copy.116 = bf16[1,4,16,1,256]{4,2,3,1,0:T(8,128)(2,1)} copy(bf16[1,4,16,1,256]{4,2,3,1,0:T(8,128)(2,1)S(1)} %bitcast.269) | data formatting | bytes 65536
  (114 shorter events, 5.4 us)
Async XLA Ops:
  0.6 1.1 %copy-start.1 = (bf16[1,1,64,2,64]{4,3,2,1,0:T(2,128)(2,1)S(1)}, bf16[1,1,64,2,64]{4,3,2,1,0:T(2,128)(2,1)}, u32[]{:S(2)}) copy-start(bf16[1,1,64,2,64]{4,3,2,1,0:T(2,128)(2,1)} %param.5) | copy-start | bytes 49156
  0.6 1.2 %copy-start = (bf16[3456,64]{0,1:T(8,128)(2,1)S(1)}, bf16[3456,64]{0,1:T(8,128)(2,1)}, u32[]{:S(2)}) copy-start(bf16[3456,64]{0,1:T(8,128)(2,1)} %param.7) | copy-start | bytes 1327108
  4.0 6.9 %copy-start.2 = (bf16[256,64]{0,1:T(8,128)(2,1)S(1)}, bf16[256,64]{0,1:T(8,128)(2,1)}, u32[]{:S(2)}) copy-start(bf16[256,64]{0,1:T(8,128)(2,1)} %param.6) | copy-start | bytes 98308
  4.4 12.8 %collective-permute-start = (f32[64,128]{1,0:T(8,128)S(1)}, f32[64,128]{1,0:T(8,128)S(1)}, u32[]{:S(2)}, u32[]{:S(2)}) collective-permute-start(f32[64,128]{1,0:T(8,128)S(1)} %dynamic-slice_bitcast_fusion), channel_id=1, source_target_pairs={{0,1},{1,0},{2,3},{3,2},{4,5},{5,4},{6,7},{7,6},{8,9},{9,8},{10,11... | collective-permute-start | bytes 98312 | tf_op jit(solution)/shard_map/ppermute | solution.py:94
  4.9 11.6 %all-to-all-start = ((bf16[1,4,32,1,256]{4,2,3,0,1:T(8,128)(2,1)}), bf16[1,4,32,1,256]{4,2,3,0,1:T(8,128)(2,1)S(1)}, u32[]{:S(2)}, u32[]{:S(2)}) async-start(bf16[1,4,32,1,256]{4,2,3,0,1:T(8,128)(2,1)} %bitcast), calls=%async_computation | async-start | bytes 131072 | tf_op jit(solution)/shard_map/all_to_all | solution.py:168
  24.5 19.3 %all-to-all-start.1 = ((bf16[1,1,16,4,256]{4,2,1,0,3:T(8,128)(2,1)}), bf16[1,1,16,4,256]{4,2,1,0,3:T(8,128)(2,1)S(1)}, u32[]{:S(2)}, u32[]{:S(2)}) async-start(bf16[1,1,16,4,256]{4,2,1,0,3:T(8,128)(2,1)} %copy.61), calls=%async_computation.1 | async-start | bytes 65536 | tf_op jit(solution)/shard_map/all_to_all | solution.py:225
  28.0 7.8 %collective-permute-start.1 = (bf16[320,128]{1,0:T(8,128)(2,1)S(1)}, bf16[320,128]{1,0:T(8,128)(2,1)S(1)}, u32[]{:S(2)}, u32[]{:S(2)}) collective-permute-start(bf16[320,128]{1,0:T(8,128)(2,1)S(1)} %pad_maximum_fusion.8), channel_id=1, source_target_pairs={{0,8},{4,12},{8,0},{12,4},{1,9},{5,13},{9,1},{13,5},{2,10},{6,14},... | collective-permute-start | bytes 245768 | tf_op jit(solution)/shard_map/ppermute | solution.py:146
  36.1 4.9 %collective-permute-start.2 = (bf16[448,128]{1,0:T(8,128)(2,1)S(1)}, bf16[448,128]{1,0:T(8,128)(2,1)S(1)}, u32[]{:S(2)}, u32[]{:S(2)}) collective-permute-start(bf16[448,128]{1,0:T(8,128)(2,1)S(1)} %pad_maximum_fusion.6), channel_id=1, source_target_pairs={{0,4},{4,0},{8,12},{12,8},{1,5},{5,1},{9,13},{13,9},{2,6},{6,2},{1... | collective-permute-start | bytes 344072 | tf_op jit(solution)/shard_map/ppermute | solution.py:146
  41.3 5.8 %collective-permute-start.3 = (bf16[800,128]{1,0:T(8,128)(2,1)S(1)}, bf16[800,128]{1,0:T(8,128)(2,1)S(1)}, u32[]{:S(2)}, u32[]{:S(2)}) collective-permute-start(bf16[800,128]{1,0:T(8,128)(2,1)S(1)} %pad_maximum_fusion.3), channel_id=1, source_target_pairs={{0,2},{2,0},{1,3},{3,1},{4,6},{6,4},{5,7},{7,5},{8,10},{10,8},{9,1... | collective-permute-start | bytes 614408 | tf_op jit(solution)/shard_map/ppermute | solution.py:146

commit v8 on v7

--- a/solution.py
+++ b/solution.py
@@ -137,8 +137,9 @@
             bit = (lax.axis_index(name) >> j) & 1
             mine = lax.dynamic_index_in_dim(y, bit, axis=pos, keepdims=False)
             other = lax.dynamic_index_in_dim(y, 1 - bit, axis=pos, keepdims=False)
-            high = other.astype(jnp.bfloat16)
-            low = (other - high.astype(jnp.float32)).astype(jnp.bfloat16)
+            rounded = lax.reduce_precision(other, exponent_bits=8, mantissa_bits=7)
+            high = rounded.astype(jnp.bfloat16)
+            low = (other - rounded).astype(jnp.bfloat16)
             message = jnp.concatenate(
                 [x.reshape(-1, lanes), high.reshape(-1, lanes), low.reshape(-1, lanes)], axis=0
             )

time: 51.5 us -> 51.5 us (level)
  no operation moved by 1% of the time
where the time goes in v8:
time: 51.5 us; the launch traced here: 51.1 us
  waiting for transfers between devices  15.7 us (30%)
  starting transfers between devices  14.4 us (28%)
  local copies, waits for them, and re-layouts  8.95 us (17%)
  blocking collectives  5.85 us (11%)
  matrix products  2.85 us (6%)
  between operations  1.77 us (3%)
  other arithmetic  1.56 us (3%)
    ppermute x3, waiting for transfers between devices, fused_chain(): got = lax.ppermute(message, name, perm)  12.4 us
    all_to_all x1, starting transfers between devices, block(): lax.all_to_all(volumes, 'space', split_axis=1, concat_axis=3, tiled=True)  5.88 us
    ppermute x3, starting transfers between devices, fused_chain(): got = lax.ppermute(message, name, perm)  4.69 us
    all_to_all x1, waiting for transfers between devices, block(): lax.all_to_all(volumes, 'space', split_axis=1, concat_axis=3, tiled=True)  3.33 us
    all_to_all x1, starting transfers between devices, block(): lax.all_to_all(grad_sample.reshape(1, 1, half_c, depth, XY * XY), 'space'...  3.26 us
    all_gather x1, blocking collectives, block(): lax.all_gather(hidden.reshape(half_o, half_z, half_s, half_s), 'ch', axis...  2.18 us
    unnamed x40, local copies, waits for them, and re-layouts  1.97 us
    all_gather x1, blocking collectives, block(): all_first = lax.all_gather(first_weight, 'ch', axis=1, tiled=True)  1.84 us
  transfers between devices with their start and end apart: 6, of which 4 were waited for; matrix products, arithmetic and copies ran while one was open for 6% of the time, Pallas kernels for 0%

profile of v8, /device:TPU:0, one launch (start us, length us, event | category | flops | bytes accessed | tf_op | source)
XLA Modules:
  0.0 51.1 jit_solution(485518705394855053)
XLA Ops:
  0.7 0.9 %copy.47 = bf16[1,1,64,2,64]{2,4,3,1,0:T(8,128)(2,1)S(1)} copy(bf16[1,1,64,2,64]{4,3,2,1,0:T(2,128)(2,1)} %param.5) | data formatting | bytes 32768 | tf_op args[1]
  3.3 0.3 fusion.24
  3.7 0.3 fusion.23
  4.1 0.3 fusion.2
  4.4 0.6 %collective-permute-start = (f32[64,128]{1,0:T(8,128)S(1)}, f32[64,128]{1,0:T(8,128)S(1)}, u32[]{:S(2)}, u32[]{:S(2)}) collective-permute-start(f32[64,128]{1,0:T(8,128)S(1)} %dynamic-slice_bitcast_fusion), channel_id=1, source_target_pairs={{0,1},{1,0},{2,3},{3,2},{4,5},{5,4},{6,7},{7,6},{8,9},{9,8},{10,11... | collective-permute-start | bytes 98312 | tf_op jit(solution)/shard_map/ppermute | solution.py:94
  4.9 5.9 %all-to-all-start = ((bf16[1,4,32,1,256]{4,2,3,0,1:T(8,128)(2,1)}), bf16[1,4,32,1,256]{4,2,3,0,1:T(8,128)(2,1)S(1)}, u32[]{:S(2)}, u32[]{:S(2)}) async-start(bf16[1,4,32,1,256]{4,2,3,0,1:T(8,128)(2,1)} %bitcast), calls=%async_computation | async-start | bytes 131072 | tf_op jit(solution)/shard_map/all_to_all | solution.py:169
  10.8 1.8 %all_gather.10 = bf16[256,128]{0,1:T(8,128)(2,1)S(1)} all-gather(bf16[256,64]{0,1:T(8,128)(2,1)S(1)} %copy-done.2), channel_id=1, replica_groups=mesh['groups'=2,'space'=4,'sub'=2,'ch'=2] {'ch'}, dimensions={1}, use_global_device_ids=true | all-gather | bytes 98304 | tf_op jit(solution)/shard_map/all_gather | solution.py:218
  13.2 3.3 %all-to-all-done = bf16[1,4,32,1,256]{4,2,3,0,1:T(8,128)(2,1)S(1)} async-done(((bf16[1,4,32,1,256]{4,2,3,0,1:T(8,128)(2,1)}), bf16[1,4,32,1,256]{4,2,3,0,1:T(8,128)(2,1)S(1)}, u32[]{:S(2)}, u32[]{:S(2)}) %all-to-all-start) | async-done | bytes 65568 | tf_op jit(solution)/shard_map/all_to_all | solution.py:169
  16.7 0.2 copy.41
  17.5 0.3 copy.43
  17.8 2.2 %all_gather.9 = bf16[128,2,8,8]{3,2,1,0:T(8,128)(2,1)S(1)} all-gather(bf16[64,2,8,8]{3,2,1,0:T(8,128)(2,1)S(1)} %copy.43), channel_id=1, replica_groups=mesh['groups'=2,'space'=4,'sub'=2,'ch'=2] {'ch'}, dimensions={0}, use_global_device_ids=true | all-gather | bytes 49152 | tf_op jit(solution)/shard_map/all_gather | solution.py:179
  19.9 0.4 copy.44
  20.5 1.8 %all_gather.11 = bf16[128,128]{1,0:T(8,128)(2,1)S(1)} all-gather(bf16[64,128]{1,0:T(8,128)(2,1)S(1)} %get-tuple-element.27), channel_id=1, replica_groups=mesh['groups'=2,'space'=4,'sub'=2,'ch'=2] {'ch'}, dimensions={0}, use_global_device_ids=true | all-gather | bytes 49152 | tf_op jit(solution)/shard_map/all_gather | solution.py:217
  22.6 0.2 fusion.20
  23.2 0.3 fusion
  23.5 0.3 copy.60
  23.8 0.7 %copy.61 = bf16[1,1,16,4,256]{4,2,1,0,3:T(8,128)(2,1)} copy(bf16[1,1,16,4,256]{2,4,3,1,0:T(8,128)(2,1)S(1)} %bitcast.206) | data formatting | bytes 65536 | tf_op jit(solution)/shard_map/convert_element_type | solution.py:225
  24.5 3.3 %all-to-all-start.1 = ((bf16[1,1,16,4,256]{4,2,1,0,3:T(8,128)(2,1)}), bf16[1,1,16,4,256]{4,2,1,0,3:T(8,128)(2,1)S(1)}, u32[]{:S(2)}, u32[]{:S(2)}) async-start(bf16[1,1,16,4,256]{4,2,1,0,3:T(8,128)(2,1)} %copy.61), calls=%async_computation.1 | async-start | bytes 65536 | tf_op jit(solution)/shard_map/all_to_all | solution.py:226
  28.0 3.0 %collective-permute-start.1 = (bf16[320,128]{1,0:T(8,128)(2,1)S(1)}, bf16[320,128]{1,0:T(8,128)(2,1)S(1)}, u32[]{:S(2)}, u32[]{:S(2)}) collective-permute-start(bf16[320,128]{1,0:T(8,128)(2,1)S(1)} %pad_maximum_fusion.8), channel_id=1, source_target_pairs={{0,8},{4,12},{8,0},{12,4},{1,9},{5,13},{9,1},{13,5},{2,10},{6,14},... | collective-permute-start | bytes 245768 | tf_op jit(solution)/shard_map/ppermute | solution.py:147
  31.0 0.2 convolution_add_fusion.2
  31.4 4.4 %collective-permute-done.1 = bf16[320,128]{1,0:T(8,128)(2,1)S(1)} collective-permute-done((bf16[320,128]{1,0:T(8,128)(2,1)S(1)}, bf16[320,128]{1,0:T(8,128)(2,1)S(1)}, u32[]{:S(2)}, u32[]{:S(2)}) %collective-permute-start.1) | collective-permute-done | bytes 81952 | tf_op jit(solution)/shard_map/ppermute | solution.py:147
  36.1 0.2 collective-permute-start.2
  36.4 4.6 %collective-permute-done.2 = bf16[448,128]{1,0:T(8,128)(2,1)S(1)} collective-permute-done((bf16[448,128]{1,0:T(8,128)(2,1)S(1)}, bf16[448,128]{1,0:T(8,128)(2,1)S(1)}, u32[]{:S(2)}, u32[]{:S(2)}) %collective-permute-start.2) | collective-permute-done | bytes 114720 | tf_op jit(solution)/shard_map/ppermute | solution.py:147
  41.3 1.6 %collective-permute-start.3 = (bf16[800,128]{1,0:T(8,128)(2,1)S(1)}, bf16[800,128]{1,0:T(8,128)(2,1)S(1)}, u32[]{:S(2)}, u32[]{:S(2)}) collective-permute-start(bf16[800,128]{1,0:T(8,128)(2,1)S(1)} %pad_maximum_fusion.3), channel_id=1, source_target_pairs={{0,2},{2,0},{1,3},{3,1},{4,6},{6,4},{5,7},{7,5},{8,10},{10,8},{9,1... | collective-permute-start | bytes 614408 | tf_op jit(solution)/shard_map/ppermute | solution.py:147
  42.9 0.2 fusion.9
  43.1 0.7 %reshape.315 = bf16[1,1,64,2,64]{4,3,2,1,0:T(2,128)(2,1)} reshape(bf16[64,128]{1,0:T(8,128)(2,1)S(1)} %fusion.9) | data formatting | bytes 32768 | tf_op jit(solution)/shard_map/reshape | solution.py:182
  43.8 3.3 %collective-permute-done.3 = bf16[800,128]{1,0:T(8,128)(2,1)S(1)} collective-permute-done((bf16[800,128]{1,0:T(8,128)(2,1)S(1)}, bf16[800,128]{1,0:T(8,128)(2,1)S(1)}, u32[]{:S(2)}, u32[]{:S(2)}) %collective-permute-start.3) | collective-permute-done | bytes 204832 | tf_op jit(solution)/shard_map/ppermute | solution.py:147
  47.7 0.2 fusion.7
  47.9 0.5 %pad_dynamic-slice_fusion = (bf16[8,128,2,8,8]{1,4,3,2,0:T(8,128)(2,1)S(1)}, bf16[8,128,2,8,8]{1,4,3,2,0:T(8,128)(2,1)S(1)}, bf16[8,128,2,8,8]{1,4,3,2,0:T(8,128)(2,1)S(1)}, bf16[8,128,2,8,8]{1,4,3,2,0:T(8,128)(2,1)S(1)}) fusion(s32[]{:T(128)S(6)} %select_n.195, s32[]{:T(128)S(6)} %select_n.198, s32[]{:T(128)S(6)} %select_n.200, ...), kind=kLoop, calls=%fused_computation | loop fusion | bytes 1310768 | tf_op jit(solution)/shard_map/dynamic_slice | solution.py:113
  49.1 0.8 %dynamic-slice_multiply_fusion = f32[432,64]{0,1:T(8,128)} fusion(f32[640,64]{0,1:T(8,128)S(1)} %fusion.3, s32[]{:T(128)S(6)} %select_n.201), kind=kLoop, calls=%fused_computation.83 | loop fusion | flops 27648 | bytes 221188 | tf_op jit(solution)/shard_map/mul | solution.py:205
  49.9 0.6 %fusion.16 = f32[32,64]{1,0:T(8,128)} fusion(f32[32,64]{1,0:T(8,128)S(1)} %reshape.365, f32[32,64]{1,0:T(8,128)S(1)} %reshape.364, f32[2,32,64]{2,1,0:T(8,128)S(1)} %fusion.12, s32[]{:T(128)S(6)} %select_n.163), kind=kLoop, calls=%fused_computation.144 | loop fusion | flops 4096 | bytes 32772 | tf_op jit(solution)/shard_map/add | solution.py:151
  50.5 0.6 %copy.116 = bf16[1,4,16,1,256]{4,2,3,1,0:T(8,128)(2,1)} copy(bf16[1,4,16,1,256]{4,2,3,1,0:T(8,128)(2,1)S(1)} %bitcast.269) | data formatting | bytes 65536
  (114 shorter events, 5.4 us)
Async XLA Ops:
  0.6 1.1 %copy-start.1 = (bf16[1,1,64,2,64]{4,3,2,1,0:T(2,128)(2,1)S(1)}, bf16[1,1,64,2,64]{4,3,2,1,0:T(2,128)(2,1)}, u32[]{:S(2)}) copy-start(bf16[1,1,64,2,64]{4,3,2,1,0:T(2,128)(2,1)} %param.5) | copy-start | bytes 49156
  0.6 1.2 %copy-start = (bf16[3456,64]{0,1:T(8,128)(2,1)S(1)}, bf16[3456,64]{0,1:T(8,128)(2,1)}, u32[]{:S(2)}) copy-start(bf16[3456,64]{0,1:T(8,128)(2,1)} %param.7) | copy-start | bytes 1327108
  4.0 6.9 %copy-start.2 = (bf16[256,64]{0,1:T(8,128)(2,1)S(1)}, bf16[256,64]{0,1:T(8,128)(2,1)}, u32[]{:S(2)}) copy-start(bf16[256,64]{0,1:T(8,128)(2,1)} %param.6) | copy-start | bytes 98308
  4.4 12.8 %collective-permute-start = (f32[64,128]{1,0:T(8,128)S(1)}, f32[64,128]{1,0:T(8,128)S(1)}, u32[]{:S(2)}, u32[]{:S(2)}) collective-permute-start(f32[64,128]{1,0:T(8,128)S(1)} %dynamic-slice_bitcast_fusion), channel_id=1, source_target_pairs={{0,1},{1,0},{2,3},{3,2},{4,5},{5,4},{6,7},{7,6},{8,9},{9,8},{10,11... | collective-permute-start | bytes 98312 | tf_op jit(solution)/shard_map/ppermute | solution.py:94
  4.9 11.6 %all-to-all-start = ((bf16[1,4,32,1,256]{4,2,3,0,1:T(8,128)(2,1)}), bf16[1,4,32,1,256]{4,2,3,0,1:T(8,128)(2,1)S(1)}, u32[]{:S(2)}, u32[]{:S(2)}) async-start(bf16[1,4,32,1,256]{4,2,3,0,1:T(8,128)(2,1)} %bitcast), calls=%async_computation | async-start | bytes 131072 | tf_op jit(solution)/shard_map/all_to_all | solution.py:169
  24.5 19.3 %all-to-all-start.1 = ((bf16[1,1,16,4,256]{4,2,1,0,3:T(8,128)(2,1)}), bf16[1,1,16,4,256]{4,2,1,0,3:T(8,128)(2,1)S(1)}, u32[]{:S(2)}, u32[]{:S(2)}) async-start(bf16[1,1,16,4,256]{4,2,1,0,3:T(8,128)(2,1)} %copy.61), calls=%async_computation.1 | async-start | bytes 65536 | tf_op jit(solution)/shard_map/all_to_all | solution.py:226
  28.0 7.8 %collective-permute-start.1 = (bf16[320,128]{1,0:T(8,128)(2,1)S(1)}, bf16[320,128]{1,0:T(8,128)(2,1)S(1)}, u32[]{:S(2)}, u32[]{:S(2)}) collective-permute-start(bf16[320,128]{1,0:T(8,128)(2,1)S(1)} %pad_maximum_fusion.8), channel_id=1, source_target_pairs={{0,8},{4,12},{8,0},{12,4},{1,9},{5,13},{9,1},{13,5},{2,10},{6,14},... | collective-permute-start | bytes 245768 | tf_op jit(solution)/shard_map/ppermute | solution.py:147
  36.1 4.9 %collective-permute-start.2 = (bf16[448,128]{1,0:T(8,128)(2,1)S(1)}, bf16[448,128]{1,0:T(8,128)(2,1)S(1)}, u32[]{:S(2)}, u32[]{:S(2)}) collective-permute-start(bf16[448,128]{1,0:T(8,128)(2,1)S(1)} %pad_maximum_fusion.6), channel_id=1, source_target_pairs={{0,4},{4,0},{8,12},{12,8},{1,5},{5,1},{9,13},{13,9},{2,6},{6,2},{1... | collective-permute-start | bytes 344072 | tf_op jit(solution)/shard_map/ppermute | solution.py:147
  41.3 5.8 %collective-permute-start.3 = (bf16[800,128]{1,0:T(8,128)(2,1)S(1)}, bf16[800,128]{1,0:T(8,128)(2,1)S(1)}, u32[]{:S(2)}, u32[]{:S(2)}) collective-permute-start(bf16[800,128]{1,0:T(8,128)(2,1)S(1)} %pad_maximum_fusion.3), channel_id=1, source_target_pairs={{0,2},{2,0},{1,3},{3,1},{4,6},{6,4},{5,7},{7,5},{8,10},{10,8},{9,1... | collective-permute-start | bytes 614408 | tf_op jit(solution)/shard_map/ppermute | solution.py:147

commit v9 on v8

--- a/solution.py
+++ b/solution.py
@@ -156,6 +156,22 @@
     return x, y
 
 
+def regroup(volumes, name):
+    size = lax.axis_size(name)
+    bits = size.bit_length() - 1
+    index = lax.axis_index(name)
+    per, chans, planes, area = volumes.shape[1:]
+    x = volumes.reshape((2,) * bits + (per // size, chans, planes, area))
+    for j in reversed(range(bits)):
+        bit = (index >> j) & 1
+        mine = lax.dynamic_index_in_dim(x, bit, axis=0, keepdims=False)
+        other = lax.dynamic_index_in_dim(x, 1 - bit, axis=0, keepdims=False)
+        got = lax.ppermute(other, name, [(i, i ^ (1 << j)) for i in range(size)])
+        axis = mine.ndim - 2
+        x = jnp.where(bit == 0, jnp.stack([mine, got], axis), jnp.stack([got, mine], axis))
+    return x.reshape(per // size, chans, size * planes, area)
+
+
 def silu_slope(pre):
     sig = jax.nn.sigmoid(pre)
     return sig * (1.0 + pre * (1.0 - sig))
@@ -166,8 +182,8 @@
     half_c = chans // lax.axis_size("ch")
     pair_index = lax.axis_index("ch")
     half_o = first_weight.shape[1]
-    sample = lax.all_to_all(volumes, "space", split_axis=1, concat_axis=3, tiled=True)
-    depth = sample.shape[3]
+    sample = regroup(volumes, "space")
+    depth = sample.shape[2]
     sample = sample.reshape(chans, depth, XY * XY)
     half_z, half_s = (depth // 2, XY // 2)
     voxels = half_z * half_s * half_s

time: 51.5 us -> 53 us (1.029)
  local copies, waits for them, and re-layouts: 8.95 us -> 9.87 us
  waiting for transfers between devices: 15.7 us -> 16.6 us
  starting transfers between devices: 14.4 us -> 13.8 us
    all_to_all x1 -> x0, starting transfers between devices: 5.88 us -> none  [block(): lax.all_to_all(volumes, 'space', split_axis=1, concat_axis=3, tiled=True)]
    ppermute x0 -> x2, starting transfers between devices: none -> 5.77 us  [regroup(): got = lax.ppermute(other, name, [(i, i ^ 1 << j) for i in range(size)])]
    ppermute x0 -> x2, waiting for transfers between devices: none -> 4.18 us  [regroup(): got = lax.ppermute(other, name, [(i, i ^ 1 << j) for i in range(size)])]
    all_to_all x1 -> x0, waiting for transfers between devices: 3.33 us -> none  [block(): lax.all_to_all(volumes, 'space', split_axis=1, concat_axis=3, tiled=True)]
    another operation x0 -> x3, local copies, waits for them, and re-layouts: none -> 1.13 us  [the longest x2 0.96 us: regroup(): jnp.stack([mine, got], axis)]
  transfers between devices with their start and end apart: 6 -> 7, of which waited for: 4 -> 4; matrix products, arithmetic and copies ran while one was open for 6% -> 13% of each run, Pallas kernels for 0% -> 0%
where the time goes in v9:
time: 53 us; the launch traced here: 52.6 us
  waiting for transfers between devices  16.6 us (31%)
  starting transfers between devices  13.8 us (26%)
  local copies, waits for them, and re-layouts  9.87 us (19%)
  blocking collectives  5.98 us (11%)
  matrix products  2.86 us (5%)
  other arithmetic  2.07 us (4%)
  between operations  1.39 us (3%)
    ppermute x3, waiting for transfers between devices, fused_chain(): got = lax.ppermute(message, name, perm)  12.4 us
    ppermute x2, starting transfers between devices, regroup(): got = lax.ppermute(other, name, [(i, i ^ 1 << j) for i in range(size)])  5.77 us
    ppermute x3, starting transfers between devices, fused_chain(): got = lax.ppermute(message, name, perm)  4.69 us
    ppermute x2, waiting for transfers between devices, regroup(): got = lax.ppermute(other, name, [(i, i ^ 1 << j) for i in range(size)])  4.18 us
    all_to_all x1, starting transfers between devices, block(): lax.all_to_all(grad_sample.reshape(1, 1, half_c, depth, XY * XY), 'space'...  3.26 us
    all_gather x1, blocking collectives, block(): lax.all_gather(hidden.reshape(half_o, half_z, half_s, half_s), 'ch', axis...  2.18 us
    all_gather x1, blocking collectives, block(): all_first = lax.all_gather(first_weight, 'ch', axis=1, tiled=True)  1.97 us
    unnamed x40, local copies, waits for them, and re-layouts  1.91 us
  transfers between devices with their start and end apart: 7, of which 4 were waited for; matrix products, arithmetic and copies ran while one was open for 13% of the time, Pallas kernels for 0%

profile of v9, /device:TPU:0, one launch (start us, length us, event | category | flops | bytes accessed | tf_op | source)
XLA Modules:
  0.0 52.6 jit_solution(10950359911126821371)
XLA Ops:
  0.6 0.8 %dynamic-slice_bitcast_fusion.3 = (bf16[2,1,32,1,1,256]{5,2,4,3,1,0:T(8,128)(2,1)S(1)}, bf16[2,1,32,1,256]{4,2,0,3,1:T(8,128)(2,1)S(1)}) fusion(bf16[2,2,1,32,1,256]{5,3,1,4,2,0:T(8,128)(2,1)} %bitcast.286, s32[]{:T(128)S(6)} %select_n.191, s32[]{:T(128)S(6)} %select_n.192), kind=kLoop, calls=%fused_computation.145 | loop fusion | bytes 131080 | tf_op jit(solution)/shard_map/stack | solution.py:171
  1.4 4.1 %collective-permute-start = (bf16[2,1,32,1,256]{4,2,0,3,1:T(8,128)(2,1)S(1)}, bf16[2,1,32,1,256]{4,2,0,3,1:T(8,128)(2,1)S(1)}, u32[]{:S(2)}, u32[]{:S(2)}) collective-permute-start(bf16[2,1,32,1,256]{4,2,0,3,1:T(8,128)(2,1)S(1)} %get-tuple-element.30), channel_id=1, source_target_pairs={{0,8},{4,12},{8,0},{12,4},{1,9},{5,13},{9,1},{13,5},{2,10},{6,14},... | collective-permute-start | bytes 98312 | tf_op jit(solution)/shard_map/ppermute | solution.py:169
  5.6 0.9 %copy.50 = bf16[1,1,64,2,64]{2,4,3,1,0:T(8,128)(2,1)S(1)} copy(bf16[1,1,64,2,64]{4,3,2,1,0:T(2,128)(2,1)} %param.5) | data formatting | bytes 32768 | tf_op args[1]
  8.1 0.3 fusion.24
  8.6 0.3 fusion.23
  8.9 0.3 fusion.1
  9.3 2.0 %all_gather.10 = bf16[256,128]{0,1:T(8,128)(2,1)S(1)} all-gather(bf16[256,64]{0,1:T(8,128)(2,1)S(1)} %copy-done.2), channel_id=1, replica_groups=mesh['groups'=2,'space'=4,'sub'=2,'ch'=2] {'ch'}, dimensions={1}, use_global_device_ids=true | all-gather | bytes 98304 | tf_op jit(solution)/shard_map/all_gather | solution.py:234
  11.9 1.6 %collective-permute-start.1 = (bf16[1,32,2,1,256]{1,4,2,3,0:T(8,128)(2,1)S(1)}, bf16[1,32,2,1,256]{1,4,2,3,0:T(8,128)(2,1)S(1)}, u32[]{:S(2)}, u32[]{:S(2)}) collective-permute-start(bf16[1,32,2,1,256]{1,4,2,3,0:T(8,128)(2,1)S(1)} %get-tuple-element.20), channel_id=1, source_target_pairs={{0,4},{4,0},{8,12},{12,8},{1,5},{5,1},{9,13},{13,9},{2,6},{6,2},{1... | collective-permute-start | bytes 98312 | tf_op jit(solution)/shard_map/ppermute | solution.py:169
  13.5 4.2 %collective-permute-done.1 = bf16[1,32,2,1,256]{1,4,2,3,0:T(8,128)(2,1)S(1)} collective-permute-done((bf16[1,32,2,1,256]{1,4,2,3,0:T(8,128)(2,1)S(1)}, bf16[1,32,2,1,256]{1,4,2,3,0:T(8,128)(2,1)S(1)}, u32[]{:S(2)}, u32[]{:S(2)}) %collective-permute-start.1) | collective-permute-done | bytes 32800 | tf_op jit(solution)/shard_map/ppermute | solution.py:169
  17.7 0.5 fusion.9
  18.2 0.2 copy.44
  18.9 0.3 copy.46
  19.2 2.2 %all_gather.9 = bf16[128,2,8,8]{3,2,1,0:T(8,128)(2,1)S(1)} all-gather(bf16[64,2,8,8]{3,2,1,0:T(8,128)(2,1)S(1)} %copy.46), channel_id=1, replica_groups=mesh['groups'=2,'space'=4,'sub'=2,'ch'=2] {'ch'}, dimensions={0}, use_global_device_ids=true | all-gather | bytes 49152 | tf_op jit(solution)/shard_map/all_gather | solution.py:195
  21.4 0.4 copy.47
  21.9 1.8 %all_gather.11 = bf16[128,128]{1,0:T(8,128)(2,1)S(1)} all-gather(bf16[64,128]{1,0:T(8,128)(2,1)S(1)} %get-tuple-element.33), channel_id=1, replica_groups=mesh['groups'=2,'space'=4,'sub'=2,'ch'=2] {'ch'}, dimensions={0}, use_global_device_ids=true | all-gather | bytes 49152 | tf_op jit(solution)/shard_map/all_gather | solution.py:233
  24.1 0.2 fusion.20
  24.7 0.3 fusion
  24.9 0.3 copy.63
  25.2 0.7 %copy.64 = bf16[1,1,16,4,256]{4,2,1,0,3:T(8,128)(2,1)} copy(bf16[1,1,16,4,256]{2,4,3,1,0:T(8,128)(2,1)S(1)} %bitcast.212) | data formatting | bytes 65536 | tf_op jit(solution)/shard_map/convert_element_type | solution.py:241
  25.9 3.3 %all-to-all-start = ((bf16[1,1,16,4,256]{4,2,1,0,3:T(8,128)(2,1)}), bf16[1,1,16,4,256]{4,2,1,0,3:T(8,128)(2,1)S(1)}, u32[]{:S(2)}, u32[]{:S(2)}) async-start(bf16[1,1,16,4,256]{4,2,1,0,3:T(8,128)(2,1)} %copy.64), calls=%async_computation | async-start | bytes 65536 | tf_op jit(solution)/shard_map/all_to_all | solution.py:242
  29.4 3.0 %collective-permute-start.3 = (bf16[320,128]{1,0:T(8,128)(2,1)S(1)}, bf16[320,128]{1,0:T(8,128)(2,1)S(1)}, u32[]{:S(2)}, u32[]{:S(2)}) collective-permute-start(bf16[320,128]{1,0:T(8,128)(2,1)S(1)} %pad_maximum_fusion.8), channel_id=1, source_target_pairs={{0,8},{4,12},{8,0},{12,4},{1,9},{5,13},{9,1},{13,5},{2,10},{6,14},... | collective-permute-start | bytes 245768 | tf_op jit(solution)/shard_map/ppermute | solution.py:147
  32.5 0.2 convolution_add_fusion.2
  32.8 4.4 %collective-permute-done.3 = bf16[320,128]{1,0:T(8,128)(2,1)S(1)} collective-permute-done((bf16[320,128]{1,0:T(8,128)(2,1)S(1)}, bf16[320,128]{1,0:T(8,128)(2,1)S(1)}, u32[]{:S(2)}, u32[]{:S(2)}) %collective-permute-start.3) | collective-permute-done | bytes 81952 | tf_op jit(solution)/shard_map/ppermute | solution.py:147
  37.8 4.6 %collective-permute-done.4 = bf16[448,128]{1,0:T(8,128)(2,1)S(1)} collective-permute-done((bf16[448,128]{1,0:T(8,128)(2,1)S(1)}, bf16[448,128]{1,0:T(8,128)(2,1)S(1)}, u32[]{:S(2)}, u32[]{:S(2)}) %collective-permute-start.4) | collective-permute-done | bytes 114720 | tf_op jit(solution)/shard_map/ppermute | solution.py:147
  42.8 1.6 %collective-permute-start.5 = (bf16[800,128]{1,0:T(8,128)(2,1)S(1)}, bf16[800,128]{1,0:T(8,128)(2,1)S(1)}, u32[]{:S(2)}, u32[]{:S(2)}) collective-permute-start(bf16[800,128]{1,0:T(8,128)(2,1)S(1)} %pad_maximum_fusion.3), channel_id=1, source_target_pairs={{0,2},{2,0},{1,3},{3,1},{4,6},{6,4},{5,7},{7,5},{8,10},{10,8},{9,1... | collective-permute-start | bytes 614408 | tf_op jit(solution)/shard_map/ppermute | solution.py:147
  44.3 0.2 fusion.8
  44.5 0.7 %reshape.413 = bf16[1,1,64,2,64]{4,3,2,1,0:T(2,128)(2,1)} reshape(bf16[64,128]{1,0:T(8,128)(2,1)S(1)} %fusion.8) | data formatting | bytes 32768 | tf_op jit(solution)/shard_map/reshape | solution.py:198
  45.3 3.3 %collective-permute-done.5 = bf16[800,128]{1,0:T(8,128)(2,1)S(1)} collective-permute-done((bf16[800,128]{1,0:T(8,128)(2,1)S(1)}, bf16[800,128]{1,0:T(8,128)(2,1)S(1)}, u32[]{:S(2)}, u32[]{:S(2)}) %collective-permute-start.5) | collective-permute-done | bytes 204832 | tf_op jit(solution)/shard_map/ppermute | solution.py:147
  49.3 0.5 pad_dynamic-slice_fusion
  50.6 0.8 %dynamic-slice_multiply_fusion = f32[432,64]{0,1:T(8,128)} fusion(f32[640,64]{0,1:T(8,128)S(1)} %fusion.2, s32[]{:T(128)S(6)} %select_n.238), kind=kLoop, calls=%fused_computation.86 | loop fusion | flops 27648 | bytes 221188 | tf_op jit(solution)/shard_map/mul | solution.py:221
  51.3 0.6 %fusion.16 = f32[32,64]{1,0:T(8,128)} fusion(f32[32,64]{1,0:T(8,128)S(1)} %reshape.463, f32[32,64]{1,0:T(8,128)S(1)} %reshape.462, f32[2,32,64]{2,1,0:T(8,128)S(1)} %fusion.12, s32[]{:T(128)S(6)} %select_n.200), kind=kLoop, calls=%fused_computation.152 | loop fusion | flops 4096 | bytes 32772 | tf_op jit(solution)/shard_map/add | solution.py:151
  51.9 0.6 %copy.119 = bf16[1,4,16,1,256]{4,2,3,1,0:T(8,128)(2,1)} copy(bf16[1,4,16,1,256]{4,2,3,1,0:T(8,128)(2,1)S(1)} %bitcast.277) | data formatting | bytes 65536
  (122 shorter events, 6.1 us)
Async XLA Ops:
  1.4 5.2 %copy-start.1 = (bf16[1,1,64,2,64]{4,3,2,1,0:T(2,128)(2,1)S(1)}, bf16[1,1,64,2,64]{4,3,2,1,0:T(2,128)(2,1)}, u32[]{:S(2)}) copy-start(bf16[1,1,64,2,64]{4,3,2,1,0:T(2,128)(2,1)} %param.5) | copy-start | bytes 49156
  1.4 5.3 %copy-start = (bf16[3456,64]{0,1:T(8,128)(2,1)S(1)}, bf16[3456,64]{0,1:T(8,128)(2,1)}, u32[]{:S(2)}) copy-start(bf16[3456,64]{0,1:T(8,128)(2,1)} %param.7) | copy-start | bytes 1327108
  1.4 10.0 %collective-permute-start = (bf16[2,1,32,1,256]{4,2,0,3,1:T(8,128)(2,1)S(1)}, bf16[2,1,32,1,256]{4,2,0,3,1:T(8,128)(2,1)S(1)}, u32[]{:S(2)}, u32[]{:S(2)}) collective-permute-start(bf16[2,1,32,1,256]{4,2,0,3,1:T(8,128)(2,1)S(1)} %get-tuple-element.30), channel_id=1, source_target_pairs={{0,8},{4,12},{8,0},{12,4},{1,9},{5,13},{9,1},{13,5},{2,10},{6,14},... | collective-permute-start | bytes 98312 | tf_op jit(solution)/shard_map/ppermute | solution.py:169
  8.6 0.8 %copy-start.2 = (bf16[256,64]{0,1:T(8,128)(2,1)S(1)}, bf16[256,64]{0,1:T(8,128)(2,1)}, u32[]{:S(2)}) copy-start(bf16[256,64]{0,1:T(8,128)(2,1)} %param.6) | copy-start | bytes 98308
  9.2 9.4 %collective-permute-start.2 = (f32[64,128]{1,0:T(8,128)S(1)}, f32[64,128]{1,0:T(8,128)S(1)}, u32[]{:S(2)}, u32[]{:S(2)}) collective-permute-start(f32[64,128]{1,0:T(8,128)S(1)} %dynamic-slice_bitcast_fusion.1), channel_id=1, source_target_pairs={{0,1},{1,0},{2,3},{3,2},{4,5},{5,4},{6,7},{7,6},{8,9},{9,8},{10,11... | collective-permute-start | bytes 98312 | tf_op jit(solution)/shard_map/ppermute | solution.py:94
  11.9 5.8 %collective-permute-start.1 = (bf16[1,32,2,1,256]{1,4,2,3,0:T(8,128)(2,1)S(1)}, bf16[1,32,2,1,256]{1,4,2,3,0:T(8,128)(2,1)S(1)}, u32[]{:S(2)}, u32[]{:S(2)}) collective-permute-start(bf16[1,32,2,1,256]{1,4,2,3,0:T(8,128)(2,1)S(1)} %get-tuple-element.20), channel_id=1, source_target_pairs={{0,4},{4,0},{8,12},{12,8},{1,5},{5,1},{9,13},{13,9},{2,6},{6,2},{1... | collective-permute-start | bytes 98312 | tf_op jit(solution)/shard_map/ppermute | solution.py:169
  25.9 19.3 %all-to-all-start = ((bf16[1,1,16,4,256]{4,2,1,0,3:T(8,128)(2,1)}), bf16[1,1,16,4,256]{4,2,1,0,3:T(8,128)(2,1)S(1)}, u32[]{:S(2)}, u32[]{:S(2)}) async-start(bf16[1,1,16,4,256]{4,2,1,0,3:T(8,128)(2,1)} %copy.64), calls=%async_computation | async-start | bytes 65536 | tf_op jit(solution)/shard_map/all_to_all | solution.py:242
  29.4 7.8 %collective-permute-start.3 = (bf16[320,128]{1,0:T(8,128)(2,1)S(1)}, bf16[320,128]{1,0:T(8,128)(2,1)S(1)}, u32[]{:S(2)}, u32[]{:S(2)}) collective-permute-start(bf16[320,128]{1,0:T(8,128)(2,1)S(1)} %pad_maximum_fusion.8), channel_id=1, source_target_pairs={{0,8},{4,12},{8,0},{12,4},{1,9},{5,13},{9,1},{13,5},{2,10},{6,14},... | collective-permute-start | bytes 245768 | tf_op jit(solution)/shard_map/ppermute | solution.py:147
  37.6 4.9 %collective-permute-start.4 = (bf16[448,128]{1,0:T(8,128)(2,1)S(1)}, bf16[448,128]{1,0:T(8,128)(2,1)S(1)}, u32[]{:S(2)}, u32[]{:S(2)}) collective-permute-start(bf16[448,128]{1,0:T(8,128)(2,1)S(1)} %pad_maximum_fusion.6), channel_id=1, source_target_pairs={{0,4},{4,0},{8,12},{12,8},{1,5},{5,1},{9,13},{13,9},{2,6},{6,2},{1... | collective-permute-start | bytes 344072 | tf_op jit(solution)/shard_map/ppermute | solution.py:147
  42.8 5.8 %collective-permute-start.5 = (bf16[800,128]{1,0:T(8,128)(2,1)S(1)}, bf16[800,128]{1,0:T(8,128)(2,1)S(1)}, u32[]{:S(2)}, u32[]{:S(2)}) collective-permute-start(bf16[800,128]{1,0:T(8,128)(2,1)S(1)} %pad_maximum_fusion.3), channel_id=1, source_target_pairs={{0,2},{2,0},{1,3},{3,1},{4,6},{6,4},{5,7},{7,5},{8,10},{10,8},{9,1... | collective-permute-start | bytes 614408 | tf_op jit(solution)/shard_map/ppermute | solution.py:147

commit v10 on v8

--- a/solution.py
+++ b/solution.py
@@ -172,12 +172,13 @@
     half_z, half_s = (depth // 2, XY // 2)
     voxels = half_z * half_s * half_s
     cols = to_depth(sample, XY)
-    pre = lax.dot_general(
-        first_weight, cols, (((0,), (0,)), ((), ())), preferred_element_type=jnp.float32
-    )
-    hidden = jax.nn.silu(pre).astype(jnp.bfloat16)
-    grid = lax.all_gather(hidden.reshape(half_o, half_z, half_s, half_s), "ch", axis=0, tiled=True)
-    width = grid.shape[0]
+    all_first = lax.all_gather(first_weight, "ch", axis=1, tiled=True)
+    width = all_first.shape[1]
+    pre_all = lax.dot_general(
+        all_first, cols, (((0,), (0,)), ((), ())), preferred_element_type=jnp.float32
+    )
+    grid = jax.nn.silu(pre_all).astype(jnp.bfloat16).reshape(width, half_z, half_s, half_s)
+    pre = lax.dynamic_slice_in_dim(pre_all, pair_index * half_o, half_o, 0)
     out = conv_forward(grid, second_weight)
     block_out = out.astype(jnp.bfloat16).reshape(1, 1, half_o, half_z, half_s * half_s)
     cot = cotangent.reshape(half_o, voxels)
@@ -215,7 +216,6 @@
         first_grad = halving_scatter(grad_first, ("space", "sub"))
         second_grad = halving_scatter(grad_second, ("space", "sub"))
     all_pre_grad = lax.all_gather(pre_grad, "ch", axis=0, tiled=True)
-    all_first = lax.all_gather(first_weight, "ch", axis=1, tiled=True)
     first_rows = lax.dynamic_slice_in_dim(
         all_first.reshape(8, chans, width), pair_index * half_c, half_c, 1
     )

time: 51.5 us -> 48.9 us (0.950)
  waiting for transfers between devices: 15.7 us -> 12.5 us
  blocking collectives: 5.85 us -> 3.68 us
  starting transfers between devices: 14.4 us -> 16.2 us
  local copies, waits for them, and re-layouts: 8.95 us -> 9.72 us
    all_to_all x1, waiting for transfers between devices: 3.33 us -> 0.01 us  [block(): lax.all_to_all(volumes, 'space', split_axis=1, concat_axis=3, tiled=True)]
    all_gather x1 -> x0, blocking collectives: 2.18 us -> none  [block(): lax.all_gather(hidden.reshape(half_o, half_z, half_s, half_s), 'ch', axis...]
    all_to_all x1, starting transfers between devices: 3.26 us -> 5.09 us  [block(): lax.all_to_all(grad_sample.reshape(1, 1, half_c, depth, XY * XY), 'space'...]
    reshape x10 -> x17, local copies, waits for them, and re-layouts: 0.94 us -> 1.79 us  [plane_stack(): windows.append(window.reshape(chans, depth * side * side))]
    unnamed x40, local copies, waits for them, and re-layouts: 1.97 us -> 2.61 us
  transfers between devices with their start and end apart: 6 -> 6, of which waited for: 4 -> 3; matrix products, arithmetic and copies ran while one was open for 6% -> 13% of each run, Pallas kernels for 0% -> 0%
where the time goes in v10:
time: 48.9 us; the launch traced here: 48.4 us
  starting transfers between devices  16.2 us (33%)
  waiting for transfers between devices  12.5 us (26%)
  local copies, waits for them, and re-layouts  9.72 us (20%)
  blocking collectives  3.68 us (8%)
  matrix products  2.84 us (6%)
  between operations  1.86 us (4%)
  other arithmetic  1.6 us (3%)
    ppermute x3, waiting for transfers between devices, fused_chain(): got = lax.ppermute(message, name, perm)  12.5 us
    all_to_all x1, starting transfers between devices, block(): lax.all_to_all(volumes, 'space', split_axis=1, concat_axis=3, tiled=True)  6.36 us
    all_to_all x1, starting transfers between devices, block(): lax.all_to_all(grad_sample.reshape(1, 1, half_c, depth, XY * XY), 'space'...  5.09 us
    ppermute x3, starting transfers between devices, fused_chain(): got = lax.ppermute(message, name, perm)  4.71 us
    unnamed x40, local copies, waits for them, and re-layouts  2.61 us
    all_gather x1, blocking collectives, block(): all_first = lax.all_gather(first_weight, 'ch', axis=1, tiled=True)  1.85 us
    all_gather x1, blocking collectives, block(): all_pre_grad = lax.all_gather(pre_grad, 'ch', axis=0, tiled=True)  1.83 us
    reshape x17, local copies, waits for them, and re-layouts, plane_stack(): windows.append(window.reshape(chans, depth * side * side))  1.79 us
  transfers between devices with their start and end apart: 6, of which 3 were waited for; matrix products, arithmetic and copies ran while one was open for 13% of the time, Pallas kernels for 0%

profile of v10, /device:TPU:0, one launch (start us, length us, event | category | flops | bytes accessed | tf_op | source)
XLA Modules:
  0.0 48.4 jit_solution(13623458430768350993)
XLA Ops:
  0.6 6.4 %all-to-all-start = ((bf16[1,4,32,1,256]{4,2,3,0,1:T(8,128)(2,1)}), bf16[1,4,32,1,256]{4,2,3,0,1:T(8,128)(2,1)S(1)}, u32[]{:S(2)}, u32[]{:S(2)}) async-start(bf16[1,4,32,1,256]{4,2,3,0,1:T(8,128)(2,1)} %bitcast.276), calls=%async_computation | async-start | bytes 131072 | tf_op jit(solution)/shard_map/all_to_all | solution.py:169
  7.0 0.9 %copy.59 = bf16[1,1,64,2,64]{2,4,3,1,0:T(8,128)(2,1)S(1)} copy(bf16[1,1,64,2,64]{4,3,2,1,0:T(2,128)(2,1)} %param.5) | data formatting | bytes 32768 | tf_op args[1]
  8.0 0.6 %copy-done.1 = bf16[1,1,64,2,64]{4,3,2,1,0:T(2,128)(2,1)S(1)} copy-done((bf16[1,1,64,2,64]{4,3,2,1,0:T(2,128)(2,1)S(1)}, bf16[1,1,64,2,64]{4,3,2,1,0:T(2,128)(2,1)}, u32[]{:S(2)}) %copy-start.1) | copy-done | bytes 16408
  8.7 0.2 copy-done
  10.3 0.3 fusion.26
  10.7 0.3 fusion.25
  11.1 0.3 fusion.2
  11.9 1.9 %all_gather.6 = bf16[256,128]{0,1:T(8,128)(2,1)S(1)} all-gather(bf16[256,64]{0,1:T(8,128)(2,1)S(1)} %copy-done.2), channel_id=1, replica_groups=mesh['groups'=2,'space'=4,'sub'=2,'ch'=2] {'ch'}, dimensions={1}, use_global_device_ids=true | all-gather | bytes 98304 | tf_op jit(solution)/shard_map/all_gather | solution.py:175
  14.2 0.2 copy.48
  14.4 0.2 reshape.284
  14.6 0.2 multiply_convert_fusion
  15.1 1.8 %all_gather.7 = bf16[128,128]{1,0:T(8,128)(2,1)S(1)} all-gather(bf16[64,128]{1,0:T(8,128)(2,1)S(1)} %fusion.15), channel_id=1, replica_groups=mesh['groups'=2,'space'=4,'sub'=2,'ch'=2] {'ch'}, dimensions={0}, use_global_device_ids=true | all-gather | bytes 49152 | tf_op jit(solution)/shard_map/all_gather | solution.py:218
  17.3 0.2 fusion.19
  17.7 0.2 fusion.22
  19.0 0.3 fusion
  19.2 0.3 copy.72
  19.5 0.7 %copy.73 = bf16[1,1,16,4,256]{4,2,1,0,3:T(8,128)(2,1)} copy(bf16[1,1,16,4,256]{2,4,3,1,0:T(8,128)(2,1)S(1)} %bitcast.205) | data formatting | bytes 65536 | tf_op jit(solution)/shard_map/convert_element_type | solution.py:225
  20.2 5.1 %all-to-all-start.1 = ((bf16[1,1,16,4,256]{4,2,1,0,3:T(8,128)(2,1)}), bf16[1,1,16,4,256]{4,2,1,0,3:T(8,128)(2,1)S(1)}, u32[]{:S(2)}, u32[]{:S(2)}) async-start(bf16[1,1,16,4,256]{4,2,1,0,3:T(8,128)(2,1)} %copy.73), calls=%async_computation.1 | async-start | bytes 65536 | tf_op jit(solution)/shard_map/all_to_all | solution.py:226
  25.6 3.0 %collective-permute-start.1 = (bf16[320,128]{1,0:T(8,128)(2,1)S(1)}, bf16[320,128]{1,0:T(8,128)(2,1)S(1)}, u32[]{:S(2)}, u32[]{:S(2)}) collective-permute-start(bf16[320,128]{1,0:T(8,128)(2,1)S(1)} %pad_maximum_fusion.8), channel_id=1, source_target_pairs={{0,8},{4,12},{8,0},{12,4},{1,9},{5,13},{9,1},{13,5},{2,10},{6,14},... | collective-permute-start | bytes 245768 | tf_op jit(solution)/shard_map/ppermute | solution.py:147
  28.6 4.6 %collective-permute-done.1 = bf16[320,128]{1,0:T(8,128)(2,1)S(1)} collective-permute-done((bf16[320,128]{1,0:T(8,128)(2,1)S(1)}, bf16[320,128]{1,0:T(8,128)(2,1)S(1)}, u32[]{:S(2)}, u32[]{:S(2)}) %collective-permute-start.1) | collective-permute-done | bytes 81952 | tf_op jit(solution)/shard_map/ppermute | solution.py:147
  33.8 4.5 %collective-permute-done.2 = bf16[448,128]{1,0:T(8,128)(2,1)S(1)} collective-permute-done((bf16[448,128]{1,0:T(8,128)(2,1)S(1)}, bf16[448,128]{1,0:T(8,128)(2,1)S(1)}, u32[]{:S(2)}, u32[]{:S(2)}) %collective-permute-start.2) | collective-permute-done | bytes 114720 | tf_op jit(solution)/shard_map/ppermute | solution.py:147
  38.6 1.6 %collective-permute-start.3 = (bf16[800,128]{1,0:T(8,128)(2,1)S(1)}, bf16[800,128]{1,0:T(8,128)(2,1)S(1)}, u32[]{:S(2)}, u32[]{:S(2)}) collective-permute-start(bf16[800,128]{1,0:T(8,128)(2,1)S(1)} %pad_maximum_fusion.3), channel_id=1, source_target_pairs={{0,2},{2,0},{1,3},{3,1},{4,6},{6,4},{5,7},{7,5},{8,10},{10,8},{9,1... | collective-permute-start | bytes 614408 | tf_op jit(solution)/shard_map/ppermute | solution.py:147
  40.2 0.2 fusion.10
  40.4 0.7 %reshape.312 = bf16[1,1,64,2,64]{4,3,2,1,0:T(2,128)(2,1)} reshape(bf16[64,128]{1,0:T(8,128)(2,1)S(1)} %fusion.10) | data formatting | bytes 32768 | tf_op jit(solution)/shard_map/reshape | solution.py:183
  41.1 3.4 %collective-permute-done.3 = bf16[800,128]{1,0:T(8,128)(2,1)S(1)} collective-permute-done((bf16[800,128]{1,0:T(8,128)(2,1)S(1)}, bf16[800,128]{1,0:T(8,128)(2,1)S(1)}, u32[]{:S(2)}, u32[]{:S(2)}) %collective-permute-start.3) | collective-permute-done | bytes 204832 | tf_op jit(solution)/shard_map/ppermute | solution.py:147
  44.7 0.2 copy.75
  45.2 0.5 %pad_dynamic-slice_fusion = (bf16[8,128,2,8,8]{1,4,3,2,0:T(8,128)(2,1)S(1)}, bf16[8,128,2,8,8]{1,4,3,2,0:T(8,128)(2,1)S(1)}, bf16[8,128,2,8,8]{1,4,3,2,0:T(8,128)(2,1)S(1)}, bf16[8,128,2,8,8]{1,4,3,2,0:T(8,128)(2,1)S(1)}) fusion(s32[]{:T(128)S(6)} %select_n.199, s32[]{:T(128)S(6)} %select_n.202, s32[]{:T(128)S(6)} %select_n.204, ...), kind=kLoop, calls=%fused_computation | loop fusion | bytes 1310768 | tf_op jit(solution)/shard_map/dynamic_slice | solution.py:113
  45.7 0.2 fusion.6
  46.1 0.2 fusion.4
  46.4 0.8 %dynamic-slice_multiply_fusion = f32[432,64]{0,1:T(8,128)} fusion(f32[640,64]{0,1:T(8,128)S(1)} %fusion.3, s32[]{:T(128)S(6)} %select_n.205), kind=kLoop, calls=%fused_computation.83 | loop fusion | flops 27648 | bytes 221188 | tf_op jit(solution)/shard_map/mul | solution.py:206
  47.2 0.6 %fusion.17 = f32[32,64]{1,0:T(8,128)} fusion(f32[32,64]{1,0:T(8,128)S(1)} %reshape.362, f32[32,64]{1,0:T(8,128)S(1)} %reshape.361, f32[2,32,64]{2,1,0:T(8,128)S(1)} %fusion.13, s32[]{:T(128)S(6)} %select_n.167), kind=kLoop, calls=%fused_computation.143 | loop fusion | flops 4096 | bytes 32772 | tf_op jit(solution)/shard_map/add | solution.py:151
  47.8 0.6 %copy.126 = bf16[1,4,16,1,256]{4,2,3,1,0:T(8,128)(2,1)} copy(bf16[1,4,16,1,256]{4,2,3,1,0:T(8,128)(2,1)S(1)} %bitcast.267) | data formatting | bytes 65536
  (119 shorter events, 5.8 us)
Async XLA Ops:
  0.6 13.4 %all-to-all-start = ((bf16[1,4,32,1,256]{4,2,3,0,1:T(8,128)(2,1)}), bf16[1,4,32,1,256]{4,2,3,0,1:T(8,128)(2,1)S(1)}, u32[]{:S(2)}, u32[]{:S(2)}) async-start(bf16[1,4,32,1,256]{4,2,3,0,1:T(8,128)(2,1)} %bitcast.276), calls=%async_computation | async-start | bytes 131072 | tf_op jit(solution)/shard_map/all_to_all | solution.py:169
  7.8 0.8 %copy-start.1 = (bf16[1,1,64,2,64]{4,3,2,1,0:T(2,128)(2,1)S(1)}, bf16[1,1,64,2,64]{4,3,2,1,0:T(2,128)(2,1)}, u32[]{:S(2)}) copy-start(bf16[1,1,64,2,64]{4,3,2,1,0:T(2,128)(2,1)} %param.5) | copy-start | bytes 49156
  7.9 1.0 %copy-start = (bf16[3456,64]{0,1:T(8,128)(2,1)S(1)}, bf16[3456,64]{0,1:T(8,128)(2,1)}, u32[]{:S(2)}) copy-start(bf16[3456,64]{0,1:T(8,128)(2,1)} %param.7) | copy-start | bytes 1327108
  11.1 0.8 %copy-start.2 = (bf16[256,64]{0,1:T(8,128)(2,1)S(1)}, bf16[256,64]{0,1:T(8,128)(2,1)}, u32[]{:S(2)}) copy-start(bf16[256,64]{0,1:T(8,128)(2,1)} %param.6) | copy-start | bytes 98308
  11.4 3.6 %collective-permute-start = (f32[64,128]{1,0:T(8,128)S(1)}, f32[64,128]{1,0:T(8,128)S(1)}, u32[]{:S(2)}, u32[]{:S(2)}) collective-permute-start(f32[64,128]{1,0:T(8,128)S(1)} %dynamic-slice_bitcast_fusion), channel_id=1, source_target_pairs={{0,1},{1,0},{2,3},{3,2},{4,5},{5,4},{6,7},{7,6},{8,9},{9,8},{10,11... | collective-permute-start | bytes 98312 | tf_op jit(solution)/shard_map/ppermute | solution.py:94
  20.2 20.9 %all-to-all-start.1 = ((bf16[1,1,16,4,256]{4,2,1,0,3:T(8,128)(2,1)}), bf16[1,1,16,4,256]{4,2,1,0,3:T(8,128)(2,1)S(1)}, u32[]{:S(2)}, u32[]{:S(2)}) async-start(bf16[1,1,16,4,256]{4,2,1,0,3:T(8,128)(2,1)} %copy.73), calls=%async_computation.1 | async-start | bytes 65536 | tf_op jit(solution)/shard_map/all_to_all | solution.py:226
  25.6 7.6 %collective-permute-start.1 = (bf16[320,128]{1,0:T(8,128)(2,1)S(1)}, bf16[320,128]{1,0:T(8,128)(2,1)S(1)}, u32[]{:S(2)}, u32[]{:S(2)}) collective-permute-start(bf16[320,128]{1,0:T(8,128)(2,1)S(1)} %pad_maximum_fusion.8), channel_id=1, source_target_pairs={{0,8},{4,12},{8,0},{12,4},{1,9},{5,13},{9,1},{13,5},{2,10},{6,14},... | collective-permute-start | bytes 245768 | tf_op jit(solution)/shard_map/ppermute | solution.py:147
  33.5 4.9 %collective-permute-start.2 = (bf16[448,128]{1,0:T(8,128)(2,1)S(1)}, bf16[448,128]{1,0:T(8,128)(2,1)S(1)}, u32[]{:S(2)}, u32[]{:S(2)}) collective-permute-start(bf16[448,128]{1,0:T(8,128)(2,1)S(1)} %pad_maximum_fusion.6), channel_id=1, source_target_pairs={{0,4},{4,0},{8,12},{12,8},{1,5},{5,1},{9,13},{13,9},{2,6},{6,2},{1... | collective-permute-start | bytes 344072 | tf_op jit(solution)/shard_map/ppermute | solution.py:147
  38.6 5.8 %collective-permute-start.3 = (bf16[800,128]{1,0:T(8,128)(2,1)S(1)}, bf16[800,128]{1,0:T(8,128)(2,1)S(1)}, u32[]{:S(2)}, u32[]{:S(2)}) collective-permute-start(bf16[800,128]{1,0:T(8,128)(2,1)S(1)} %pad_maximum_fusion.3), channel_id=1, source_target_pairs={{0,2},{2,0},{1,3},{3,1},{4,6},{6,4},{5,7},{7,5},{8,10},{10,8},{9,1... | collective-permute-start | bytes 614408 | tf_op jit(solution)/shard_map/ppermute | solution.py:147

commit v11 on v10

--- a/solution.py
+++ b/solution.py
@@ -96,7 +96,7 @@
     return x
 
 
-def second_grad_rows(hidden_all, cot_all, names, total_rows):
+def second_grad_rows(hidden_all, cot_all, names, total_rows, fence=False):
     count, chans, depth, side = hidden_all.shape[0], hidden_all.shape[1], hidden_all.shape[2], hidden_all.shape[3]
     shards = math.prod(lax.axis_size(n) for n in names)
     rows = total_rows // shards
@@ -104,6 +104,8 @@
     for name in names:
         index = index * lax.axis_size(name) + lax.axis_index(name)
     first = index * rows
+    if fence:
+        first, hidden_all = lax.optimization_barrier((first, hidden_all))
     tap0 = first // chans
     taps = min(27, (rows + 2 * chans - 2) // chans)
     padded = jnp.pad(hidden_all, ((0, 0), (0, 0), (1, 1), (1, 1), (1, 1)))
@@ -146,14 +148,15 @@
             perm = [(i, i ^ (1 << j)) for i in range(size)]
             got = lax.ppermute(message, name, perm)
             kept, part = x.size // lanes, high.size // lanes
-            x = jnp.concatenate([x, got[:kept].reshape(x.shape)], axis=0)
+            pieces = (x, got[:kept].reshape(x.shape))
+            x = jnp.concatenate(pieces, axis=0)
             y = (
                 mine
                 + got[kept : kept + part].reshape(high.shape).astype(jnp.float32)
                 + got[kept + part :].reshape(high.shape).astype(jnp.float32)
             )
             labels.pop(pos)
-    return x, y
+    return pieces, y
 
 
 def silu_slope(pre):
@@ -197,20 +200,22 @@
     gather_second = shards * (width + half_o) * voxels * 2 <= 1 << 22
     gather_second = gather_second and (grad_first.size // shards) % voxels == 0
     if gather_second:
-        both, first_grad = fused_chain(
+        pieces, first_grad = fused_chain(
             jnp.concatenate([grid.reshape(width, voxels), cot], axis=0),
             grad_first,
             ("space", "sub"),
         )
-        second_grad = (
-            second_grad_rows(
-                both[:, :width].reshape(both.shape[0], width, half_z, half_s, half_s),
-                both[:, width:],
+        half = pieces[0].shape[0]
+        terms = []
+        for k, part in enumerate(pieces):
+            terms.append(second_grad_rows(
+                part[:, :width].reshape(half, width, half_z, half_s, half_s),
+                part[:, width:],
                 ("space", "sub"),
                 second_weight.shape[0],
-            )
-            * factor
-        )
+                fence=k == 0,
+            ))
+        second_grad = (lax.optimization_barrier(terms[0]) + terms[1]) * factor
     else:
         grad_second = conv_weight_grad(grid, cot) * factor
         first_grad = halving_scatter(grad_first, ("space", "sub"))

time: 48.9 us -> 44.5 us (0.910)
  waiting for transfers between devices: 12.5 us -> 7.85 us
  starting transfers between devices: 16.2 us -> 14.7 us
  local copies, waits for them, and re-layouts: 9.72 us -> 10.8 us
  matrix products: 2.84 us -> 3.54 us
    ppermute x3, waiting for transfers between devices: 12.5 us -> 4.41 us  [fused_chain(): got = lax.ppermute(message, name, perm)]
    all_to_all x1, waiting for transfers between devices: 0.01 us -> 2.91 us  [block(): lax.all_to_all(volumes, 'space', split_axis=1, concat_axis=3, tiled=True)]
    all_to_all x1, starting transfers between devices: 5.09 us -> 3.8 us  [block(): lax.all_to_all(grad_sample.reshape(1, 1, half_c, depth, XY * XY), 'space'...]
    unnamed x40, local copies, waits for them, and re-layouts: 2.61 us -> 3.35 us
    dot_general x5 -> x10, matrix products: 0.87 us -> 1.58 us  [second_grad_rows(): lax.dot_general(window, cot_all, (((0, 2), (0, 2)), ((), ())), preferred_...]
    all_to_all x1, waiting for transfers between devices: 0.01 us -> 0.53 us  [block(): lax.all_to_all(grad_sample.reshape(1, 1, half_c, depth, XY * XY), 'space'...]
  transfers between devices with their start and end apart: 6 -> 6, of which waited for: 3 -> 4; matrix products, arithmetic and copies ran while one was open for 13% -> 15% of each run, Pallas kernels for 0% -> 0%
where the time goes in v11:
time: 44.5 us; the launch traced here: 44 us
  starting transfers between devices  14.7 us (33%)
  local copies, waits for them, and re-layouts  10.8 us (24%)
  waiting for transfers between devices  7.85 us (18%)
  blocking collectives  3.67 us (8%)
  matrix products  3.54 us (8%)
  between operations  1.92 us (4%)
  other arithmetic  1.56 us (4%)
    all_to_all x1, starting transfers between devices, block(): lax.all_to_all(volumes, 'space', split_axis=1, concat_axis=3, tiled=True)  5.88 us
    ppermute x3, starting transfers between devices, fused_chain(): got = lax.ppermute(message, name, perm)  4.45 us
    ppermute x3, waiting for transfers between devices, fused_chain(): got = lax.ppermute(message, name, perm)  4.41 us
    all_to_all x1, starting transfers between devices, block(): lax.all_to_all(grad_sample.reshape(1, 1, half_c, depth, XY * XY), 'space'...  3.8 us
    unnamed x40, local copies, waits for them, and re-layouts  3.35 us
    all_to_all x1, waiting for transfers between devices, block(): lax.all_to_all(volumes, 'space', split_axis=1, concat_axis=3, tiled=True)  2.91 us
    all_gather x1, blocking collectives, block(): all_first = lax.all_gather(first_weight, 'ch', axis=1, tiled=True)  1.84 us
    all_gather x1, blocking collectives, block(): all_pre_grad = lax.all_gather(pre_grad, 'ch', axis=0, tiled=True)  1.83 us
  transfers between devices with their start and end apart: 6, of which 4 were waited for; matrix products, arithmetic and copies ran while one was open for 15% of the time, Pallas kernels for 0%

profile of v11, /device:TPU:0, one launch (start us, length us, event | category | flops | bytes accessed | tf_op | source)
XLA Modules:
  0.0 44.0 jit_solution(7699481074204578671)
XLA Ops:
  0.6 0.9 %copy.65 = bf16[1,1,64,2,64]{2,4,3,1,0:T(8,128)(2,1)S(1)} copy(bf16[1,1,64,2,64]{4,3,2,1,0:T(2,128)(2,1)} %param.5) | data formatting | bytes 32768 | tf_op args[1]
  1.7 0.7 %copy-done.1 = bf16[1,1,64,2,64]{4,3,2,1,0:T(2,128)(2,1)S(1)} copy-done((bf16[1,1,64,2,64]{4,3,2,1,0:T(2,128)(2,1)S(1)}, bf16[1,1,64,2,64]{4,3,2,1,0:T(2,128)(2,1)}, u32[]{:S(2)}) %copy-start.1) | copy-done | bytes 16408
  4.0 0.3 fusion.40
  4.5 0.3 fusion.41
  4.8 0.3 fusion.2
  5.1 0.6 %collective-permute-start = (f32[64,128]{1,0:T(8,128)S(1)}, f32[64,128]{1,0:T(8,128)S(1)}, u32[]{:S(2)}, u32[]{:S(2)}) collective-permute-start(f32[64,128]{1,0:T(8,128)S(1)} %dynamic-slice_bitcast_fusion), channel_id=1, source_target_pairs={{0,1},{1,0},{2,3},{3,2},{4,5},{5,4},{6,7},{7,6},{8,9},{9,8},{10,11... | collective-permute-start | bytes 98312 | tf_op jit(solution)/shard_map/ppermute | solution.py:94
  5.6 5.9 %all-to-all-start = ((bf16[1,4,32,1,256]{4,2,3,0,1:T(8,128)(2,1)}), bf16[1,4,32,1,256]{4,2,3,0,1:T(8,128)(2,1)S(1)}, u32[]{:S(2)}, u32[]{:S(2)}) async-start(bf16[1,4,32,1,256]{4,2,3,0,1:T(8,128)(2,1)} %bitcast), calls=%async_computation | async-start | bytes 131072 | tf_op jit(solution)/shard_map/all_to_all | solution.py:172
  11.5 0.8 %copy-done.2 = bf16[256,64]{0,1:T(8,128)(2,1)S(1)} copy-done((bf16[256,64]{0,1:T(8,128)(2,1)S(1)}, bf16[256,64]{0,1:T(8,128)(2,1)}, u32[]{:S(2)}) %copy-start.2) | copy-done | bytes 32792
  12.2 1.8 %all_gather.6 = bf16[256,128]{0,1:T(8,128)(2,1)S(1)} all-gather(bf16[256,64]{0,1:T(8,128)(2,1)S(1)} %copy-done.2), channel_id=1, replica_groups=mesh['groups'=2,'space'=4,'sub'=2,'ch'=2] {'ch'}, dimensions={1}, use_global_device_ids=true | all-gather | bytes 98304 | tf_op jit(solution)/shard_map/all_gather | solution.py:178
  14.3 2.9 %all-to-all-done = bf16[1,4,32,1,256]{4,2,3,0,1:T(8,128)(2,1)S(1)} async-done(((bf16[1,4,32,1,256]{4,2,3,0,1:T(8,128)(2,1)}), bf16[1,4,32,1,256]{4,2,3,0,1:T(8,128)(2,1)S(1)}, u32[]{:S(2)}, u32[]{:S(2)}) %all-to-all-start) | async-done | bytes 65568 | tf_op jit(solution)/shard_map/all_to_all | solution.py:172
  17.4 0.2 copy.54
  17.8 0.2 multiply_convert_fusion
  18.2 1.8 %all_gather.7 = bf16[128,128]{1,0:T(8,128)(2,1)S(1)} all-gather(bf16[64,128]{1,0:T(8,128)(2,1)S(1)} %fusion.30), channel_id=1, replica_groups=mesh['groups'=2,'space'=4,'sub'=2,'ch'=2] {'ch'}, dimensions={0}, use_global_device_ids=true | all-gather | bytes 49152 | tf_op jit(solution)/shard_map/all_gather | solution.py:223
  20.5 0.8 %collective-permute-start.1 = (bf16[320,128]{1,0:T(8,128)(2,1)S(1)}, bf16[320,128]{1,0:T(8,128)(2,1)S(1)}, u32[]{:S(2)}, u32[]{:S(2)}) collective-permute-start(bf16[320,128]{1,0:T(8,128)(2,1)S(1)} %pad_maximum_fusion.4), channel_id=1, source_target_pairs={{0,8},{4,12},{8,0},{12,4},{1,9},{5,13},{9,1},{13,5},{2,10},{6,14},... | collective-permute-start | bytes 245768 | tf_op jit(solution)/shard_map/ppermute | solution.py:149
  21.5 0.3 fusion
  21.7 0.3 copy.78
  22.0 0.7 %copy.79 = bf16[1,1,16,4,256]{4,2,1,0,3:T(8,128)(2,1)} copy(bf16[1,1,16,4,256]{2,4,3,1,0:T(8,128)(2,1)S(1)} %bitcast.230) | data formatting | bytes 65536 | tf_op jit(solution)/shard_map/convert_element_type | solution.py:230
  22.7 3.8 %all-to-all-start.1 = ((bf16[1,1,16,4,256]{4,2,1,0,3:T(8,128)(2,1)}), bf16[1,1,16,4,256]{4,2,1,0,3:T(8,128)(2,1)S(1)}, u32[]{:S(2)}, u32[]{:S(2)}) async-start(bf16[1,1,16,4,256]{4,2,1,0,3:T(8,128)(2,1)} %copy.79), calls=%async_computation.1 | async-start | bytes 65536 | tf_op jit(solution)/shard_map/all_to_all | solution.py:231
  26.7 0.2 fusion.37
  28.2 0.2 fusion.34
  28.8 2.1 %collective-permute-start.2 = (bf16[448,128]{1,0:T(8,128)(2,1)S(1)}, bf16[448,128]{1,0:T(8,128)(2,1)S(1)}, u32[]{:S(2)}, u32[]{:S(2)}) collective-permute-start(bf16[448,128]{1,0:T(8,128)(2,1)S(1)} %pad_maximum_fusion.2), channel_id=1, source_target_pairs={{0,4},{4,0},{8,12},{12,8},{1,5},{5,1},{9,13},{13,9},{2,6},{6,2},{1... | collective-permute-start | bytes 344072 | tf_op jit(solution)/shard_map/ppermute | solution.py:149
  30.9 0.2 fusion.15
  31.1 0.7 %reshape.330 = bf16[1,1,64,2,64]{4,3,2,1,0:T(2,128)(2,1)} reshape(bf16[64,128]{1,0:T(8,128)(2,1)S(1)} %fusion.15) | data formatting | bytes 32768 | tf_op jit(solution)/shard_map/reshape | solution.py:186
  31.8 0.5 %all-to-all-done.1 = bf16[1,1,16,4,256]{4,2,1,0,3:T(8,128)(2,1)S(1)} async-done(((bf16[1,1,16,4,256]{4,2,1,0,3:T(8,128)(2,1)}), bf16[1,1,16,4,256]{4,2,1,0,3:T(8,128)(2,1)S(1)}, u32[]{:S(2)}, u32[]{:S(2)}) %all-to-all-start.1) | async-done | bytes 32800 | tf_op jit(solution)/shard_map/all_to_all | solution.py:231
  32.3 1.4 %collective-permute-done.2 = bf16[448,128]{1,0:T(8,128)(2,1)S(1)} collective-permute-done((bf16[448,128]{1,0:T(8,128)(2,1)S(1)}, bf16[448,128]{1,0:T(8,128)(2,1)S(1)}, u32[]{:S(2)}, u32[]{:S(2)}) %collective-permute-start.2) | collective-permute-done | bytes 114720 | tf_op jit(solution)/shard_map/ppermute | solution.py:149
  34.6 1.6 %collective-permute-start.3 = (bf16[800,128]{1,0:T(8,128)(2,1)S(1)}, bf16[800,128]{1,0:T(8,128)(2,1)S(1)}, u32[]{:S(2)}, u32[]{:S(2)}) collective-permute-start(bf16[800,128]{1,0:T(8,128)(2,1)S(1)} %pad_maximum_fusion), channel_id=1, source_target_pairs={{0,2},{2,0},{1,3},{3,1},{4,6},{6,4},{5,7},{7,5},{8,10},{10,8},{9,1... | collective-permute-start | bytes 614408 | tf_op jit(solution)/shard_map/ppermute | solution.py:149
  36.4 0.3 pad_dynamic-slice_fusion.5
  37.5 3.0 %collective-permute-done.3 = bf16[800,128]{1,0:T(8,128)(2,1)S(1)} collective-permute-done((bf16[800,128]{1,0:T(8,128)(2,1)S(1)}, bf16[800,128]{1,0:T(8,128)(2,1)S(1)}, u32[]{:S(2)}, u32[]{:S(2)}) %collective-permute-start.3) | collective-permute-done | bytes 204832 | tf_op jit(solution)/shard_map/ppermute | solution.py:149
  41.1 0.3 pad_dynamic-slice_fusion
  42.0 0.8 %add_multiply_fusion = f32[432,64]{0,1:T(8,128)} fusion(f32[432,64]{0,1:T(8,128)S(1)} %constant_dynamic-slice_fusion, f32[640,64]{0,1:T(8,128)S(1)} %fusion.3, s32[]{:T(128)S(6)} %select_n.363), kind=kLoop, calls=%fused_computation.94 | loop fusion | flops 55296 | bytes 331780 | tf_op jit(solution)/shard_map/mul | solution.py:218
  42.8 0.6 %fusion.32 = f32[32,64]{1,0:T(8,128)} fusion(f32[32,64]{1,0:T(8,128)S(1)} %reshape.386, f32[32,64]{1,0:T(8,128)S(1)} %reshape.385, f32[2,32,64]{2,1,0:T(8,128)S(1)} %fusion.28, s32[]{:T(128)S(6)} %select_n.288), kind=kLoop, calls=%fused_computation.164 | loop fusion | flops 4096 | bytes 32772 | tf_op jit(solution)/shard_map/add | solution.py:154
  43.4 0.6 %copy.147 = bf16[1,4,16,1,256]{4,2,3,1,0:T(8,128)(2,1)} copy(bf16[1,4,16,1,256]{4,2,3,1,0:T(8,128)(2,1)S(1)} %bitcast.302) | data formatting | bytes 65536
  (128 shorter events, 7.2 us)
Async XLA Ops:
  1.5 1.0 %copy-start = (bf16[3456,64]{0,1:T(8,128)(2,1)S(1)}, bf16[3456,64]{0,1:T(8,128)(2,1)}, u32[]{:S(2)}) copy-start(bf16[3456,64]{0,1:T(8,128)(2,1)} %param.7) | copy-start | bytes 1327108
  1.6 0.8 %copy-start.1 = (bf16[1,1,64,2,64]{4,3,2,1,0:T(2,128)(2,1)S(1)}, bf16[1,1,64,2,64]{4,3,2,1,0:T(2,128)(2,1)}, u32[]{:S(2)}) copy-start(bf16[1,1,64,2,64]{4,3,2,1,0:T(2,128)(2,1)} %param.5) | copy-start | bytes 49156
  5.1 13.0 %collective-permute-start = (f32[64,128]{1,0:T(8,128)S(1)}, f32[64,128]{1,0:T(8,128)S(1)}, u32[]{:S(2)}, u32[]{:S(2)}) collective-permute-start(f32[64,128]{1,0:T(8,128)S(1)} %dynamic-slice_bitcast_fusion), channel_id=1, source_target_pairs={{0,1},{1,0},{2,3},{3,2},{4,5},{5,4},{6,7},{7,6},{8,9},{9,8},{10,11... | collective-permute-start | bytes 98312 | tf_op jit(solution)/shard_map/ppermute | solution.py:94
  5.6 11.6 %all-to-all-start = ((bf16[1,4,32,1,256]{4,2,3,0,1:T(8,128)(2,1)}), bf16[1,4,32,1,256]{4,2,3,0,1:T(8,128)(2,1)S(1)}, u32[]{:S(2)}, u32[]{:S(2)}) async-start(bf16[1,4,32,1,256]{4,2,3,0,1:T(8,128)(2,1)} %bitcast), calls=%async_computation | async-start | bytes 131072 | tf_op jit(solution)/shard_map/all_to_all | solution.py:172
  11.5 0.8 %copy-start.2 = (bf16[256,64]{0,1:T(8,128)(2,1)S(1)}, bf16[256,64]{0,1:T(8,128)(2,1)}, u32[]{:S(2)}) copy-start(bf16[256,64]{0,1:T(8,128)(2,1)} %param.6) | copy-start | bytes 98308
  20.5 7.9 %collective-permute-start.1 = (bf16[320,128]{1,0:T(8,128)(2,1)S(1)}, bf16[320,128]{1,0:T(8,128)(2,1)S(1)}, u32[]{:S(2)}, u32[]{:S(2)}) collective-permute-start(bf16[320,128]{1,0:T(8,128)(2,1)S(1)} %pad_maximum_fusion.4), channel_id=1, source_target_pairs={{0,8},{4,12},{8,0},{12,4},{1,9},{5,13},{9,1},{13,5},{2,10},{6,14},... | collective-permute-start | bytes 245768 | tf_op jit(solution)/shard_map/ppermute | solution.py:149
  22.7 9.6 %all-to-all-start.1 = ((bf16[1,1,16,4,256]{4,2,1,0,3:T(8,128)(2,1)}), bf16[1,1,16,4,256]{4,2,1,0,3:T(8,128)(2,1)S(1)}, u32[]{:S(2)}, u32[]{:S(2)}) async-start(bf16[1,1,16,4,256]{4,2,1,0,3:T(8,128)(2,1)} %copy.79), calls=%async_computation.1 | async-start | bytes 65536 | tf_op jit(solution)/shard_map/all_to_all | solution.py:231
  28.8 4.9 %collective-permute-start.2 = (bf16[448,128]{1,0:T(8,128)(2,1)S(1)}, bf16[448,128]{1,0:T(8,128)(2,1)S(1)}, u32[]{:S(2)}, u32[]{:S(2)}) collective-permute-start(bf16[448,128]{1,0:T(8,128)(2,1)S(1)} %pad_maximum_fusion.2), channel_id=1, source_target_pairs={{0,4},{4,0},{8,12},{12,8},{1,5},{5,1},{9,13},{13,9},{2,6},{6,2},{1... | collective-permute-start | bytes 344072 | tf_op jit(solution)/shard_map/ppermute | solution.py:149
  34.6 6.0 %collective-permute-start.3 = (bf16[800,128]{1,0:T(8,128)(2,1)S(1)}, bf16[800,128]{1,0:T(8,128)(2,1)S(1)}, u32[]{:S(2)}, u32[]{:S(2)}) collective-permute-start(bf16[800,128]{1,0:T(8,128)(2,1)S(1)} %pad_maximum_fusion), channel_id=1, source_target_pairs={{0,2},{2,0},{1,3},{3,1},{4,6},{6,4},{5,7},{7,5},{8,10},{10,8},{9,1... | collective-permute-start | bytes 614408 | tf_op jit(solution)/shard_map/ppermute | solution.py:149

commit v12 on v10

--- a/solution.py
+++ b/solution.py
@@ -156,6 +156,21 @@
     return x, y
 
 
+def regroup_back(x, name):
+    size = lax.axis_size(name)
+    bits = size.bit_length() - 1
+    index = lax.axis_index(name)
+    count, chans, depth, area = x.shape
+    x = x.reshape((count, chans) + (2,) * bits + (depth // size, area))
+    for j in range(bits):
+        bit = (index >> j) & 1
+        mine = lax.dynamic_index_in_dim(x, bit, axis=x.ndim - 3, keepdims=False)
+        other = lax.dynamic_index_in_dim(x, 1 - bit, axis=x.ndim - 3, keepdims=False)
+        got = lax.ppermute(other, name, [(i, i ^ (1 << j)) for i in range(size)])
+        x = jnp.where(bit == 0, jnp.stack([mine, got], 0), jnp.stack([got, mine], 0))
+    return x.reshape((count * size, chans, depth // size, area))
+
+
 def silu_slope(pre):
     sig = jax.nn.sigmoid(pre)
     return sig * (1.0 + pre * (1.0 - sig))
@@ -197,15 +212,23 @@
     gather_second = shards * (width + half_o) * voxels * 2 <= 1 << 22
     gather_second = gather_second and (grad_first.size // shards) % voxels == 0
     if gather_second:
+        own_half = lax.dynamic_slice_in_dim(
+            grid.reshape(width, voxels), pair_index * half_o, half_o, 0
+        )
         both, first_grad = fused_chain(
-            jnp.concatenate([grid.reshape(width, voxels), cot], axis=0),
-            grad_first,
-            ("space", "sub"),
+            jnp.concatenate([own_half, cot], axis=0), grad_first, ("space", "sub")
+        )
+        mine = both[:, :half_o]
+        other = lax.ppermute(mine, "ch", [(0, 1), (1, 0)])
+        hidden_all = jnp.where(
+            pair_index == 0,
+            jnp.concatenate([mine, other], axis=1),
+            jnp.concatenate([other, mine], axis=1),
         )
         second_grad = (
             second_grad_rows(
-                both[:, :width].reshape(both.shape[0], width, half_z, half_s, half_s),
-                both[:, width:],
+                hidden_all.reshape(both.shape[0], width, half_z, half_s, half_s),
+                both[:, half_o:],
                 ("space", "sub"),
                 second_weight.shape[0],
             )
@@ -223,13 +246,7 @@
         first_rows.reshape(8 * half_c, width), all_pre_grad, preferred_element_type=jnp.float32
     )
     grad_sample = from_depth(grad_cols, half_c, depth, XY).astype(jnp.bfloat16)
-    volume_grad = lax.all_to_all(
-        grad_sample.reshape(1, 1, half_c, depth, XY * XY),
-        "space",
-        split_axis=3,
-        concat_axis=1,
-        tiled=True,
-    )
+    volume_grad = regroup_back(grad_sample.reshape(1, half_c, depth, XY * XY), "space")[None]
     return (block_out, volume_grad, first_grad, second_grad)
 
 

time: 48.9 us -> 43.1 us (0.88)
  waiting for transfers between devices: 12.5 us -> 7 us
  local copies, waits for them, and re-layouts: 9.72 us -> 8.76 us
  other arithmetic: 1.6 us -> 2.51 us
    ppermute x3, waiting for transfers between devices: 12.5 us -> 6.61 us  [fused_chain(): got = lax.ppermute(message, name, perm)]
    ppermute x0 -> x3, starting transfers between devices: none -> 5.49 us  [the longest x2 5.41 us: regroup_back(): got = lax.ppermute(other, name, [(i, i ^ 1 << j) for i in range(size)])]
    all_to_all x1 -> x0, starting transfers between devices: 5.09 us -> none  [block(): lax.all_to_all(grad_sample.reshape(1, 1, half_c, depth, XY * XY), 'space'...]
    select_n x0 -> x3, other arithmetic: none -> 0.93 us  [the longest x2 0.64 us: regroup_back(): jnp.where(bit == 0, jnp.stack([mine, got], 0), jnp.stack([got, mine], 0))]
    convert_element_type x2 -> x1, local copies, waits for them, and re-layouts: 1 us -> 0.27 us  [block(): grad_sample = from_depth(grad_cols, half_c, depth, XY).astype(jnp.bfloat16)]
    unnamed x40 -> x39, local copies, waits for them, and re-layouts: 2.61 us -> 2 us
    ppermute x3, starting transfers between devices: 4.71 us -> 4.1 us  [fused_chain(): got = lax.ppermute(message, name, perm)]
  transfers between devices with their start and end apart: 6 -> 8, of which waited for: 3 -> 4; matrix products, arithmetic and copies ran while one was open for 13% -> 18% of each run, Pallas kernels for 0% -> 0%
where the time goes in v12:
time: 43.1 us; the launch traced here: 42.7 us
  starting transfers between devices  16 us (37%)
  local copies, waits for them, and re-layouts  8.76 us (20%)
  waiting for transfers between devices  7 us (16%)
  blocking collectives  3.68 us (9%)
  matrix products  2.85 us (7%)
  other arithmetic  2.51 us (6%)
  between operations  1.91 us (4%)
    ppermute x3, waiting for transfers between devices, fused_chain(): got = lax.ppermute(message, name, perm)  6.61 us
    all_to_all x1, starting transfers between devices, block(): lax.all_to_all(volumes, 'space', split_axis=1, concat_axis=3, tiled=True)  6.36 us
    ppermute x2, starting transfers between devices, regroup_back(): got = lax.ppermute(other, name, [(i, i ^ 1 << j) for i in range(size)])  5.41 us
    ppermute x3, starting transfers between devices, fused_chain(): got = lax.ppermute(message, name, perm)  4.1 us
    unnamed x39, local copies, waits for them, and re-layouts  2 us
    all_gather x1, blocking collectives, block(): all_first = lax.all_gather(first_weight, 'ch', axis=1, tiled=True)  1.85 us
    all_gather x1, blocking collectives, block(): all_pre_grad = lax.all_gather(pre_grad, 'ch', axis=0, tiled=True)  1.83 us
    reshape x17, local copies, waits for them, and re-layouts, plane_stack(): windows.append(window.reshape(chans, depth * side * side))  1.8 us
  transfers between devices with their start and end apart: 8, of which 4 were waited for; matrix products, arithmetic and copies ran while one was open for 18% of the time, Pallas kernels for 0%

profile of v12, /device:TPU:0, one launch (start us, length us, event | category | flops | bytes accessed | tf_op | source)
XLA Modules:
  0.0 42.7 jit_solution(9834153440410884745)
XLA Ops:
  0.6 6.4 %all-to-all-start = ((bf16[1,4,32,1,256]{4,2,3,0,1:T(8,128)(2,1)}), bf16[1,4,32,1,256]{4,2,3,0,1:T(8,128)(2,1)S(1)}, u32[]{:S(2)}, u32[]{:S(2)}) async-start(bf16[1,4,32,1,256]{4,2,3,0,1:T(8,128)(2,1)} %bitcast.274), calls=%async_computation | async-start | bytes 131072 | tf_op jit(solution)/shard_map/all_to_all | solution.py:184
  7.0 0.9 %copy.132 = bf16[1,1,64,2,64]{2,4,3,1,0:T(8,128)(2,1)S(1)} copy(bf16[1,1,64,2,64]{4,3,2,1,0:T(2,128)(2,1)} %param.5) | data formatting | bytes 32768 | tf_op args[1]
  8.0 0.6 %copy-done.1 = bf16[1,1,64,2,64]{4,3,2,1,0:T(2,128)(2,1)S(1)} copy-done((bf16[1,1,64,2,64]{4,3,2,1,0:T(2,128)(2,1)S(1)}, bf16[1,1,64,2,64]{4,3,2,1,0:T(2,128)(2,1)}, u32[]{:S(2)}) %copy-start.1) | copy-done | bytes 16408
  8.7 0.2 copy-done
  10.3 0.3 fusion.31
  10.7 0.3 fusion.30
  11.1 0.3 fusion.2
  11.9 1.9 %all_gather.6 = bf16[256,128]{0,1:T(8,128)(2,1)S(1)} all-gather(bf16[256,64]{0,1:T(8,128)(2,1)S(1)} %copy-done.2), channel_id=1, replica_groups=mesh['groups'=2,'space'=4,'sub'=2,'ch'=2] {'ch'}, dimensions={1}, use_global_device_ids=true | all-gather | bytes 98304 | tf_op jit(solution)/shard_map/all_gather | solution.py:190
  14.2 0.2 copy.121
  14.4 0.2 reshape.391
  14.6 0.2 multiply_convert_fusion
  15.1 1.8 %all_gather.7 = bf16[128,128]{1,0:T(8,128)(2,1)S(1)} all-gather(bf16[64,128]{1,0:T(8,128)(2,1)S(1)} %fusion.20), channel_id=1, replica_groups=mesh['groups'=2,'space'=4,'sub'=2,'ch'=2] {'ch'}, dimensions={0}, use_global_device_ids=true | all-gather | bytes 49152 | tf_op jit(solution)/shard_map/all_gather | solution.py:241
  17.3 0.2 fusion.24
  17.7 0.2 fusion.27
  19.1 0.3 fusion
  19.4 0.3 copy.145
  19.7 2.1 %collective-permute-start.1 = (bf16[1,16,2,1,256]{4,1,2,3,0:T(8,128)(2,1)S(1)}, bf16[1,16,2,1,256]{4,1,2,3,0:T(8,128)(2,1)S(1)}, u32[]{:S(2)}, u32[]{:S(2)}) collective-permute-start(bf16[1,16,2,1,256]{4,1,2,3,0:T(8,128)(2,1)S(1)} %copy.148), channel_id=1, source_target_pairs={{0,4},{4,0},{8,12},{12,8},{1,5},{5,1},{9,13},{13,9},{2,6},{6,2},{1... | collective-permute-start | bytes 49160 | tf_op jit(solution)/shard_map/ppermute | solution.py:169
  22.0 2.4 %collective-permute-start.3 = (bf16[256,128]{1,0:T(8,128)(2,1)S(1)}, bf16[256,128]{1,0:T(8,128)(2,1)S(1)}, u32[]{:S(2)}, u32[]{:S(2)}) collective-permute-start(bf16[256,128]{1,0:T(8,128)(2,1)S(1)} %pad_maximum_fusion.4), channel_id=1, source_target_pairs={{0,8},{4,12},{8,0},{12,4},{1,9},{5,13},{9,1},{13,5},{2,10},{6,14},... | collective-permute-start | bytes 196616 | tf_op jit(solution)/shard_map/ppermute | solution.py:147
  24.6 3.4 %collective-permute-done.3 = bf16[256,128]{1,0:T(8,128)(2,1)S(1)} collective-permute-done((bf16[256,128]{1,0:T(8,128)(2,1)S(1)}, bf16[256,128]{1,0:T(8,128)(2,1)S(1)}, u32[]{:S(2)}, u32[]{:S(2)}) %collective-permute-start.3) | collective-permute-done | bytes 65568 | tf_op jit(solution)/shard_map/ppermute | solution.py:147
  28.5 3.3 %collective-permute-start.2 = (bf16[2,1,16,1,256]{4,2,0,3,1:T(8,128)(2,1)S(1)}, bf16[2,1,16,1,256]{4,2,0,3,1:T(8,128)(2,1)S(1)}, u32[]{:S(2)}, u32[]{:S(2)}) collective-permute-start(bf16[2,1,16,1,256]{4,2,0,3,1:T(8,128)(2,1)S(1)} %get-tuple-element.34), channel_id=1, source_target_pairs={{0,8},{4,12},{8,0},{12,4},{1,9},{5,13},{9,1},{13,5},{2,10},{6,14},... | collective-permute-start | bytes 49160 | tf_op jit(solution)/shard_map/ppermute | solution.py:169
  31.8 1.2 %collective-permute-done.4 = bf16[320,128]{1,0:T(8,128)(2,1)S(1)} collective-permute-done((bf16[320,128]{1,0:T(8,128)(2,1)S(1)}, bf16[320,128]{1,0:T(8,128)(2,1)S(1)}, u32[]{:S(2)}, u32[]{:S(2)}) %collective-permute-start.4) | collective-permute-done | bytes 81952 | tf_op jit(solution)/shard_map/ppermute | solution.py:147
  33.3 1.6 %collective-permute-start.5 = (bf16[544,128]{1,0:T(8,128)(2,1)S(1)}, bf16[544,128]{1,0:T(8,128)(2,1)S(1)}, u32[]{:S(2)}, u32[]{:S(2)}) collective-permute-start(bf16[544,128]{1,0:T(8,128)(2,1)S(1)} %pad_maximum_fusion.1), channel_id=1, source_target_pairs={{0,2},{2,0},{1,3},{3,1},{4,6},{6,4},{5,7},{7,5},{8,10},{10,8},{9,1... | collective-permute-start | bytes 417800 | tf_op jit(solution)/shard_map/ppermute | solution.py:147
  34.9 0.2 fusion.10
  35.1 0.7 %reshape.419 = bf16[1,1,64,2,64]{4,3,2,1,0:T(2,128)(2,1)} reshape(bf16[64,128]{1,0:T(8,128)(2,1)S(1)} %fusion.10) | data formatting | bytes 32768 | tf_op jit(solution)/shard_map/reshape | solution.py:198
  35.8 0.6 %maximum_select_fusion.2 = bf16[2,2,1,16,1,256]{5,3,1,4,2,0:T(8,128)(2,1)} fusion(bf16[1,2,1,16,1,256]{5,3,1,4,2,0:T(8,128)(2,1)S(1)} %bitcast.277, bf16[1,2,1,16,1,256]{5,3,1,4,2,0:T(8,128)(2,1)S(1)} %get-tuple-element.33, pred[]{:T(512)S(6)} %eq.20), kind=kLoop, calls=%fused_computation.135 | loop fusion | flops 49152 | bytes 65537 | tf_op jit(solution)/shard_map/jit(_where)/select_n | solution.py:170
  36.4 2.0 %collective-permute-done.5 = bf16[544,128]{1,0:T(8,128)(2,1)S(1)} collective-permute-done((bf16[544,128]{1,0:T(8,128)(2,1)S(1)}, bf16[544,128]{1,0:T(8,128)(2,1)S(1)}, u32[]{:S(2)}, u32[]{:S(2)}) %collective-permute-start.5) | collective-permute-done | bytes 139296 | tf_op jit(solution)/shard_map/ppermute | solution.py:147
  38.9 0.6 %fusion.22 = f32[32,64]{1,0:T(8,128)} fusion(f32[32,64]{1,0:T(8,128)S(1)} %reshape.468, f32[32,64]{1,0:T(8,128)S(1)} %reshape.467, f32[2,32,64]{2,1,0:T(8,128)S(1)} %fusion.18, s32[]{:T(128)S(6)} %select_n.224), kind=kLoop, calls=%fused_computation.149 | loop fusion | flops 4096 | bytes 32772 | tf_op jit(solution)/shard_map/add | solution.py:151
  39.5 0.4 collective-permute-done.6
  40.1 0.3 maximum_select_fusion
  40.5 0.2 fusion.7
  40.7 0.5 %pad_dynamic-slice_fusion = (bf16[8,128,2,8,8]{1,4,3,2,0:T(8,128)(2,1)S(1)}, bf16[8,128,2,8,8]{1,4,3,2,0:T(8,128)(2,1)S(1)}, bf16[8,128,2,8,8]{1,4,3,2,0:T(8,128)(2,1)S(1)}, bf16[8,128,2,8,8]{1,4,3,2,0:T(8,128)(2,1)S(1)}) fusion(s32[]{:T(128)S(6)} %select_n.258, s32[]{:T(128)S(6)} %select_n.261, s32[]{:T(128)S(6)} %select_n.263, ...), kind=kLoop, calls=%fused_computation | loop fusion | bytes 1310768 | tf_op jit(solution)/shard_map/dynamic_slice | solution.py:113
  42.0 0.8 %dynamic-slice_multiply_fusion = f32[432,64]{0,1:T(8,128)} fusion(f32[640,64]{0,1:T(8,128)S(1)} %fusion.3, s32[]{:T(128)S(6)} %select_n.264), kind=kLoop, calls=%fused_computation.81 | loop fusion | flops 27648 | bytes 221188 | tf_op jit(solution)/shard_map/mul | solution.py:229
  (130 shorter events, 6.5 us)
Async XLA Ops:
  0.6 13.4 %all-to-all-start = ((bf16[1,4,32,1,256]{4,2,3,0,1:T(8,128)(2,1)}), bf16[1,4,32,1,256]{4,2,3,0,1:T(8,128)(2,1)S(1)}, u32[]{:S(2)}, u32[]{:S(2)}) async-start(bf16[1,4,32,1,256]{4,2,3,0,1:T(8,128)(2,1)} %bitcast.274), calls=%async_computation | async-start | bytes 131072 | tf_op jit(solution)/shard_map/all_to_all | solution.py:184
  7.8 0.8 %copy-start.1 = (bf16[1,1,64,2,64]{4,3,2,1,0:T(2,128)(2,1)S(1)}, bf16[1,1,64,2,64]{4,3,2,1,0:T(2,128)(2,1)}, u32[]{:S(2)}) copy-start(bf16[1,1,64,2,64]{4,3,2,1,0:T(2,128)(2,1)} %param.5) | copy-start | bytes 49156
  7.9 1.0 %copy-start = (bf16[3456,64]{0,1:T(8,128)(2,1)S(1)}, bf16[3456,64]{0,1:T(8,128)(2,1)}, u32[]{:S(2)}) copy-start(bf16[3456,64]{0,1:T(8,128)(2,1)} %param.7) | copy-start | bytes 1327108
  11.1 0.8 %copy-start.2 = (bf16[256,64]{0,1:T(8,128)(2,1)S(1)}, bf16[256,64]{0,1:T(8,128)(2,1)}, u32[]{:S(2)}) copy-start(bf16[256,64]{0,1:T(8,128)(2,1)} %param.6) | copy-start | bytes 98308
  11.4 3.7 %collective-permute-start = (f32[64,128]{1,0:T(8,128)S(1)}, f32[64,128]{1,0:T(8,128)S(1)}, u32[]{:S(2)}, u32[]{:S(2)}) collective-permute-start(f32[64,128]{1,0:T(8,128)S(1)} %dynamic-slice_bitcast_fusion.1), channel_id=1, source_target_pairs={{0,1},{1,0},{2,3},{3,2},{4,5},{5,4},{6,7},{7,6},{8,9},{9,8},{10,11... | collective-permute-start | bytes 98312 | tf_op jit(solution)/shard_map/ppermute | solution.py:94
  19.7 4.9 %collective-permute-start.1 = (bf16[1,16,2,1,256]{4,1,2,3,0:T(8,128)(2,1)S(1)}, bf16[1,16,2,1,256]{4,1,2,3,0:T(8,128)(2,1)S(1)}, u32[]{:S(2)}, u32[]{:S(2)}) collective-permute-start(bf16[1,16,2,1,256]{4,1,2,3,0:T(8,128)(2,1)S(1)} %copy.148), channel_id=1, source_target_pairs={{0,4},{4,0},{8,12},{12,8},{1,5},{5,1},{9,13},{13,9},{2,6},{6,2},{1... | collective-permute-start | bytes 49160 | tf_op jit(solution)/shard_map/ppermute | solution.py:169
  22.0 6.0 %collective-permute-start.3 = (bf16[256,128]{1,0:T(8,128)(2,1)S(1)}, bf16[256,128]{1,0:T(8,128)(2,1)S(1)}, u32[]{:S(2)}, u32[]{:S(2)}) collective-permute-start(bf16[256,128]{1,0:T(8,128)(2,1)S(1)} %pad_maximum_fusion.4), channel_id=1, source_target_pairs={{0,8},{4,12},{8,0},{12,4},{1,9},{5,13},{9,1},{13,5},{2,10},{6,14},... | collective-permute-start | bytes 196616 | tf_op jit(solution)/shard_map/ppermute | solution.py:147
  28.3 4.7 %collective-permute-start.4 = (bf16[320,128]{1,0:T(8,128)(2,1)S(1)}, bf16[320,128]{1,0:T(8,128)(2,1)S(1)}, u32[]{:S(2)}, u32[]{:S(2)}) collective-permute-start(bf16[320,128]{1,0:T(8,128)(2,1)S(1)} %pad_maximum_fusion.3), channel_id=1, source_target_pairs={{0,4},{4,0},{8,12},{12,8},{1,5},{5,1},{9,13},{13,9},{2,6},{6,2},{1... | collective-permute-start | bytes 245768 | tf_op jit(solution)/shard_map/ppermute | solution.py:147
  28.5 7.3 %collective-permute-start.2 = (bf16[2,1,16,1,256]{4,2,0,3,1:T(8,128)(2,1)S(1)}, bf16[2,1,16,1,256]{4,2,0,3,1:T(8,128)(2,1)S(1)}, u32[]{:S(2)}, u32[]{:S(2)}) collective-permute-start(bf16[2,1,16,1,256]{4,2,0,3,1:T(8,128)(2,1)S(1)} %get-tuple-element.34), channel_id=1, source_target_pairs={{0,8},{4,12},{8,0},{12,4},{1,9},{5,13},{9,1},{13,5},{2,10},{6,14},... | collective-permute-start | bytes 49160 | tf_op jit(solution)/shard_map/ppermute | solution.py:169
  33.3 5.1 %collective-permute-start.5 = (bf16[544,128]{1,0:T(8,128)(2,1)S(1)}, bf16[544,128]{1,0:T(8,128)(2,1)S(1)}, u32[]{:S(2)}, u32[]{:S(2)}) collective-permute-start(bf16[544,128]{1,0:T(8,128)(2,1)S(1)} %pad_maximum_fusion.1), channel_id=1, source_target_pairs={{0,2},{2,0},{1,3},{3,1},{4,6},{6,4},{5,7},{7,5},{8,10},{10,8},{9,1... | collective-permute-start | bytes 417800 | tf_op jit(solution)/shard_map/ppermute | solution.py:147
  38.5 1.4 %collective-permute-start.6 = (bf16[8,64,128]{2,1,0:T(8,128)(2,1)S(1)}, bf16[8,64,128]{2,1,0:T(8,128)(2,1)S(1)}, u32[]{:S(2)}, u32[]{:S(2)}) collective-permute-start(bf16[8,64,128]{2,1,0:T(8,128)(2,1)S(1)} %slice.291), channel_id=1, source_target_pairs={{0,1},{1,0},{2,3},{3,2},{4,5},{5,4},{6,7},{7,6},{8,9},{9,8},{10,11... | collective-permute-start | bytes 393224 | tf_op jit(solution)/shard_map/ppermute | solution.py:222

commit v13 on v11

--- a/solution.py
+++ b/solution.py
@@ -200,21 +200,33 @@
     gather_second = shards * (width + half_o) * voxels * 2 <= 1 << 22
     gather_second = gather_second and (grad_first.size // shards) % voxels == 0
     if gather_second:
+        own_half = lax.dynamic_slice_in_dim(
+            grid.reshape(width, voxels), pair_index * half_o, half_o, 0
+        )
         pieces, first_grad = fused_chain(
-            jnp.concatenate([grid.reshape(width, voxels), cot], axis=0),
-            grad_first,
-            ("space", "sub"),
-        )
-        half = pieces[0].shape[0]
+            jnp.concatenate([own_half, cot], axis=0), grad_first, ("space", "sub")
+        )
         terms = []
         for k, part in enumerate(pieces):
-            terms.append(second_grad_rows(
-                part[:, :width].reshape(half, width, half_z, half_s, half_s),
-                part[:, width:],
-                ("space", "sub"),
-                second_weight.shape[0],
-                fence=k == 0,
-            ))
+            mine = part[:, :half_o]
+            other = lax.ppermute(mine, "ch", [(0, 1), (1, 0)])
+            low = pair_index == 0
+            if k == 0:
+                low, mine, other = lax.optimization_barrier((low, mine, other))
+            hidden_part = jnp.where(
+                low,
+                jnp.concatenate([mine, other], axis=1),
+                jnp.concatenate([other, mine], axis=1),
+            )
+            terms.append(
+                second_grad_rows(
+                    hidden_part.reshape(part.shape[0], width, half_z, half_s, half_s),
+                    part[:, half_o:],
+                    ("space", "sub"),
+                    second_weight.shape[0],
+                    fence=k == 0,
+                )
+            )
         second_grad = (lax.optimization_barrier(terms[0]) + terms[1]) * factor
     else:
         grad_second = conv_weight_grad(grid, cot) * factor

time: 44.5 us -> 44.5 us (level)
  waiting for transfers between devices: 7.85 us -> 7.13 us
    ppermute x3, waiting for transfers between devices: 4.41 us -> 3.44 us  [fused_chain(): got = lax.ppermute(message, name, perm)]
  transfers between devices with their start and end apart: 6 -> 8, of which waited for: 4 -> 5; matrix products, arithmetic and copies ran while one was open for 15% -> 18% of each run, Pallas kernels for 0% -> 0%
where the time goes in v13:
time: 44.5 us; the launch traced here: 44.1 us
  starting transfers between devices  14.8 us (33%)
  local copies, waits for them, and re-layouts  11.1 us (25%)
  waiting for transfers between devices  7.13 us (16%)
  blocking collectives  3.67 us (8%)
  matrix products  3.55 us (8%)
  between operations  1.96 us (4%)
  other arithmetic  1.85 us (4%)
    all_to_all x1, starting transfers between devices, block(): lax.all_to_all(volumes, 'space', split_axis=1, concat_axis=3, tiled=True)  5.88 us
    ppermute x3, starting transfers between devices, fused_chain(): got = lax.ppermute(message, name, perm)  4.44 us
    all_to_all x1, starting transfers between devices, block(): lax.all_to_all(grad_sample.reshape(1, 1, half_c, depth, XY * XY), 'space'...  3.8 us
    ppermute x3, waiting for transfers between devices, fused_chain(): got = lax.ppermute(message, name, perm)  3.44 us
    unnamed x40, local copies, waits for them, and re-layouts  3.35 us
    all_to_all x1, waiting for transfers between devices, block(): lax.all_to_all(volumes, 'space', split_axis=1, concat_axis=3, tiled=True)  2.91 us
    all_gather x1, blocking collectives, block(): all_first = lax.all_gather(first_weight, 'ch', axis=1, tiled=True)  1.84 us
    all_gather x1, blocking collectives, block(): all_pre_grad = lax.all_gather(pre_grad, 'ch', axis=0, tiled=True)  1.83 us
  transfers between devices with their start and end apart: 8, of which 5 were waited for; matrix products, arithmetic and copies ran while one was open for 18% of the time, Pallas kernels for 0%

profile of v13, /device:TPU:0, one launch (start us, length us, event | category | flops | bytes accessed | tf_op | source)
XLA Modules:
  0.0 44.1 jit_solution(6143444572647698862)
XLA Ops:
  0.6 0.9 %copy.67 = bf16[1,1,64,2,64]{2,4,3,1,0:T(8,128)(2,1)S(1)} copy(bf16[1,1,64,2,64]{4,3,2,1,0:T(2,128)(2,1)} %param.5) | data formatting | bytes 32768 | tf_op args[1]
  1.7 0.7 %copy-done.1 = bf16[1,1,64,2,64]{4,3,2,1,0:T(2,128)(2,1)S(1)} copy-done((bf16[1,1,64,2,64]{4,3,2,1,0:T(2,128)(2,1)S(1)}, bf16[1,1,64,2,64]{4,3,2,1,0:T(2,128)(2,1)}, u32[]{:S(2)}) %copy-start.1) | copy-done | bytes 16408
  4.0 0.3 fusion.40
  4.5 0.3 fusion.41
  4.8 0.3 fusion.2
  5.1 0.6 %collective-permute-start = (f32[64,128]{1,0:T(8,128)S(1)}, f32[64,128]{1,0:T(8,128)S(1)}, u32[]{:S(2)}, u32[]{:S(2)}) collective-permute-start(f32[64,128]{1,0:T(8,128)S(1)} %dynamic-slice_bitcast_fusion), channel_id=1, source_target_pairs={{0,1},{1,0},{2,3},{3,2},{4,5},{5,4},{6,7},{7,6},{8,9},{9,8},{10,11... | collective-permute-start | bytes 98312 | tf_op jit(solution)/shard_map/ppermute | solution.py:94
  5.6 5.9 %all-to-all-start = ((bf16[1,4,32,1,256]{4,2,3,0,1:T(8,128)(2,1)}), bf16[1,4,32,1,256]{4,2,3,0,1:T(8,128)(2,1)S(1)}, u32[]{:S(2)}, u32[]{:S(2)}) async-start(bf16[1,4,32,1,256]{4,2,3,0,1:T(8,128)(2,1)} %bitcast), calls=%async_computation | async-start | bytes 131072 | tf_op jit(solution)/shard_map/all_to_all | solution.py:172
  11.5 0.8 %copy-done.2 = bf16[256,64]{0,1:T(8,128)(2,1)S(1)} copy-done((bf16[256,64]{0,1:T(8,128)(2,1)S(1)}, bf16[256,64]{0,1:T(8,128)(2,1)}, u32[]{:S(2)}) %copy-start.2) | copy-done | bytes 32792
  12.2 1.8 %all_gather.6 = bf16[256,128]{0,1:T(8,128)(2,1)S(1)} all-gather(bf16[256,64]{0,1:T(8,128)(2,1)S(1)} %copy-done.2), channel_id=1, replica_groups=mesh['groups'=2,'space'=4,'sub'=2,'ch'=2] {'ch'}, dimensions={1}, use_global_device_ids=true | all-gather | bytes 98304 | tf_op jit(solution)/shard_map/all_gather | solution.py:178
  14.3 2.9 %all-to-all-done = bf16[1,4,32,1,256]{4,2,3,0,1:T(8,128)(2,1)S(1)} async-done(((bf16[1,4,32,1,256]{4,2,3,0,1:T(8,128)(2,1)}), bf16[1,4,32,1,256]{4,2,3,0,1:T(8,128)(2,1)S(1)}, u32[]{:S(2)}, u32[]{:S(2)}) %all-to-all-start) | async-done | bytes 65568 | tf_op jit(solution)/shard_map/all_to_all | solution.py:172
  17.4 0.2 copy.56
  18.2 1.8 %all_gather.7 = bf16[128,128]{1,0:T(8,128)(2,1)S(1)} all-gather(bf16[64,128]{1,0:T(8,128)(2,1)S(1)} %fusion.30), channel_id=1, replica_groups=mesh['groups'=2,'space'=4,'sub'=2,'ch'=2] {'ch'}, dimensions={0}, use_global_device_ids=true | all-gather | bytes 49152 | tf_op jit(solution)/shard_map/all_gather | solution.py:235
  20.5 0.8 %collective-permute-start.1 = (bf16[256,128]{1,0:T(8,128)(2,1)S(1)}, bf16[256,128]{1,0:T(8,128)(2,1)S(1)}, u32[]{:S(2)}, u32[]{:S(2)}) collective-permute-start(bf16[256,128]{1,0:T(8,128)(2,1)S(1)} %pad_maximum_fusion.3), channel_id=1, source_target_pairs={{0,8},{4,12},{8,0},{12,4},{1,9},{5,13},{9,1},{13,5},{2,10},{6,14},... | collective-permute-start | bytes 196616 | tf_op jit(solution)/shard_map/ppermute | solution.py:149
  21.5 0.3 fusion
  21.7 0.3 copy.80
  22.0 0.7 %copy.81 = bf16[1,1,16,4,256]{4,2,1,0,3:T(8,128)(2,1)} copy(bf16[1,1,16,4,256]{2,4,3,1,0:T(8,128)(2,1)S(1)} %bitcast.228) | data formatting | bytes 65536 | tf_op jit(solution)/shard_map/convert_element_type | solution.py:242
  22.7 3.8 %all-to-all-start.1 = ((bf16[1,1,16,4,256]{4,2,1,0,3:T(8,128)(2,1)}), bf16[1,1,16,4,256]{4,2,1,0,3:T(8,128)(2,1)S(1)}, u32[]{:S(2)}, u32[]{:S(2)}) async-start(bf16[1,1,16,4,256]{4,2,1,0,3:T(8,128)(2,1)} %copy.81), calls=%async_computation.1 | async-start | bytes 65536 | tf_op jit(solution)/shard_map/all_to_all | solution.py:243
  26.7 0.2 fusion.37
  28.2 0.2 fusion.34
  28.8 2.1 %collective-permute-start.2 = (bf16[320,128]{1,0:T(8,128)(2,1)S(1)}, bf16[320,128]{1,0:T(8,128)(2,1)S(1)}, u32[]{:S(2)}, u32[]{:S(2)}) collective-permute-start(bf16[320,128]{1,0:T(8,128)(2,1)S(1)} %pad_maximum_fusion.2), channel_id=1, source_target_pairs={{0,4},{4,0},{8,12},{12,8},{1,5},{5,1},{9,13},{13,9},{2,6},{6,2},{1... | collective-permute-start | bytes 245768 | tf_op jit(solution)/shard_map/ppermute | solution.py:149
  30.9 0.2 fusion.15
  31.1 0.7 %reshape.334 = bf16[1,1,64,2,64]{4,3,2,1,0:T(2,128)(2,1)} reshape(bf16[64,128]{1,0:T(8,128)(2,1)S(1)} %fusion.15) | data formatting | bytes 32768 | tf_op jit(solution)/shard_map/reshape | solution.py:186
  31.8 0.4 all-to-all-done.1
  32.2 1.1 %collective-permute-done.2 = bf16[320,128]{1,0:T(8,128)(2,1)S(1)} collective-permute-done((bf16[320,128]{1,0:T(8,128)(2,1)S(1)}, bf16[320,128]{1,0:T(8,128)(2,1)S(1)}, u32[]{:S(2)}, u32[]{:S(2)}) %collective-permute-start.2) | collective-permute-done | bytes 81952 | tf_op jit(solution)/shard_map/ppermute | solution.py:149
  33.7 1.6 %collective-permute-start.3 = (bf16[544,128]{1,0:T(8,128)(2,1)S(1)}, bf16[544,128]{1,0:T(8,128)(2,1)S(1)}, u32[]{:S(2)}, u32[]{:S(2)}) collective-permute-start(bf16[544,128]{1,0:T(8,128)(2,1)S(1)} %pad_maximum_fusion), channel_id=1, source_target_pairs={{0,2},{2,0},{1,3},{3,1},{4,6},{6,4},{5,7},{7,5},{8,10},{10,8},{9,1... | collective-permute-start | bytes 417800 | tf_op jit(solution)/shard_map/ppermute | solution.py:149
  36.4 0.3 pad_dynamic-slice_fusion.5
  37.5 2.3 %collective-permute-done.3 = bf16[544,128]{1,0:T(8,128)(2,1)S(1)} collective-permute-done((bf16[544,128]{1,0:T(8,128)(2,1)S(1)}, bf16[544,128]{1,0:T(8,128)(2,1)S(1)}, u32[]{:S(2)}, u32[]{:S(2)}) %collective-permute-start.3) | collective-permute-done | bytes 139296 | tf_op jit(solution)/shard_map/ppermute | solution.py:149
  40.1 0.6 %fusion.32 = f32[32,64]{1,0:T(8,128)} fusion(f32[32,64]{1,0:T(8,128)S(1)} %reshape.388, f32[32,64]{1,0:T(8,128)S(1)} %reshape.387, f32[2,32,64]{2,1,0:T(8,128)S(1)} %fusion.28, s32[]{:T(128)S(6)} %select_n.305), kind=kLoop, calls=%fused_computation.166 | loop fusion | flops 4096 | bytes 32772 | tf_op jit(solution)/shard_map/add | solution.py:154
  40.9 0.3 collective-permute-done.5
  41.7 0.3 pad_dynamic-slice_fusion
  42.7 0.8 %add_multiply_fusion = f32[432,64]{0,1:T(8,128)} fusion(f32[432,64]{0,1:T(8,128)S(1)} %constant_dynamic-slice_fusion, f32[640,64]{0,1:T(8,128)S(1)} %fusion.3, s32[]{:T(128)S(6)} %select_n.384), kind=kLoop, calls=%fused_computation.96 | loop fusion | flops 55296 | bytes 331780 | tf_op jit(solution)/shard_map/mul | solution.py:230
  43.5 0.6 %copy.151 = bf16[1,4,16,1,256]{4,2,3,1,0:T(8,128)(2,1)} copy(bf16[1,4,16,1,256]{4,2,3,1,0:T(8,128)(2,1)S(1)} %bitcast.304) | data formatting | bytes 65536
  (137 shorter events, 8.0 us)
Async XLA Ops:
  1.5 1.0 %copy-start = (bf16[3456,64]{0,1:T(8,128)(2,1)S(1)}, bf16[3456,64]{0,1:T(8,128)(2,1)}, u32[]{:S(2)}) copy-start(bf16[3456,64]{0,1:T(8,128)(2,1)} %param.7) | copy-start | bytes 1327108
  1.6 0.8 %copy-start.1 = (bf16[1,1,64,2,64]{4,3,2,1,0:T(2,128)(2,1)S(1)}, bf16[1,1,64,2,64]{4,3,2,1,0:T(2,128)(2,1)}, u32[]{:S(2)}) copy-start(bf16[1,1,64,2,64]{4,3,2,1,0:T(2,128)(2,1)} %param.5) | copy-start | bytes 49156
  5.1 13.0 %collective-permute-start = (f32[64,128]{1,0:T(8,128)S(1)}, f32[64,128]{1,0:T(8,128)S(1)}, u32[]{:S(2)}, u32[]{:S(2)}) collective-permute-start(f32[64,128]{1,0:T(8,128)S(1)} %dynamic-slice_bitcast_fusion), channel_id=1, source_target_pairs={{0,1},{1,0},{2,3},{3,2},{4,5},{5,4},{6,7},{7,6},{8,9},{9,8},{10,11... | collective-permute-start | bytes 98312 | tf_op jit(solution)/shard_map/ppermute | solution.py:94
  5.6 11.6 %all-to-all-start = ((bf16[1,4,32,1,256]{4,2,3,0,1:T(8,128)(2,1)}), bf16[1,4,32,1,256]{4,2,3,0,1:T(8,128)(2,1)S(1)}, u32[]{:S(2)}, u32[]{:S(2)}) async-start(bf16[1,4,32,1,256]{4,2,3,0,1:T(8,128)(2,1)} %bitcast), calls=%async_computation | async-start | bytes 131072 | tf_op jit(solution)/shard_map/all_to_all | solution.py:172
  11.5 0.8 %copy-start.2 = (bf16[256,64]{0,1:T(8,128)(2,1)S(1)}, bf16[256,64]{0,1:T(8,128)(2,1)}, u32[]{:S(2)}) copy-start(bf16[256,64]{0,1:T(8,128)(2,1)} %param.6) | copy-start | bytes 98308
  20.5 7.9 %collective-permute-start.1 = (bf16[256,128]{1,0:T(8,128)(2,1)S(1)}, bf16[256,128]{1,0:T(8,128)(2,1)S(1)}, u32[]{:S(2)}, u32[]{:S(2)}) collective-permute-start(bf16[256,128]{1,0:T(8,128)(2,1)S(1)} %pad_maximum_fusion.3), channel_id=1, source_target_pairs={{0,8},{4,12},{8,0},{12,4},{1,9},{5,13},{9,1},{13,5},{2,10},{6,14},... | collective-permute-start | bytes 196616 | tf_op jit(solution)/shard_map/ppermute | solution.py:149
  22.7 9.5 %all-to-all-start.1 = ((bf16[1,1,16,4,256]{4,2,1,0,3:T(8,128)(2,1)}), bf16[1,1,16,4,256]{4,2,1,0,3:T(8,128)(2,1)S(1)}, u32[]{:S(2)}, u32[]{:S(2)}) async-start(bf16[1,1,16,4,256]{4,2,1,0,3:T(8,128)(2,1)} %copy.81), calls=%async_computation.1 | async-start | bytes 65536 | tf_op jit(solution)/shard_map/all_to_all | solution.py:243
  28.8 4.5 %collective-permute-start.2 = (bf16[320,128]{1,0:T(8,128)(2,1)S(1)}, bf16[320,128]{1,0:T(8,128)(2,1)S(1)}, u32[]{:S(2)}, u32[]{:S(2)}) collective-permute-start(bf16[320,128]{1,0:T(8,128)(2,1)S(1)} %pad_maximum_fusion.2), channel_id=1, source_target_pairs={{0,4},{4,0},{8,12},{12,8},{1,5},{5,1},{9,13},{13,9},{2,6},{6,2},{1... | collective-permute-start | bytes 245768 | tf_op jit(solution)/shard_map/ppermute | solution.py:149
  33.6 1.7 %collective-permute-start.4 = (bf16[4,64,128]{2,1,0:T(8,128)(2,1)S(1)}, bf16[4,64,128]{2,1,0:T(8,128)(2,1)S(1)}, u32[]{:S(2)}, u32[]{:S(2)}) collective-permute-start(bf16[4,64,128]{2,1,0:T(8,128)(2,1)S(1)} %slice.298), channel_id=1, source_target_pairs={{0,1},{1,0},{2,3},{3,2},{4,5},{5,4},{6,7},{7,6},{8,9},{9,8},{10,11... | collective-permute-start | bytes 196616 | tf_op jit(solution)/shard_map/ppermute | solution.py:212
  33.7 6.1 %collective-permute-start.3 = (bf16[544,128]{1,0:T(8,128)(2,1)S(1)}, bf16[544,128]{1,0:T(8,128)(2,1)S(1)}, u32[]{:S(2)}, u32[]{:S(2)}) collective-permute-start(bf16[544,128]{1,0:T(8,128)(2,1)S(1)} %pad_maximum_fusion), channel_id=1, source_target_pairs={{0,2},{2,0},{1,3},{3,1},{4,6},{6,4},{5,7},{7,5},{8,10},{10,8},{9,1... | collective-permute-start | bytes 417800 | tf_op jit(solution)/shard_map/ppermute | solution.py:149
  39.9 1.3 %collective-permute-start.5 = (bf16[4,64,128]{2,1,0:T(8,128)(2,1)S(1)}, bf16[4,64,128]{2,1,0:T(8,128)(2,1)S(1)}, u32[]{:S(2)}, u32[]{:S(2)}) collective-permute-start(bf16[4,64,128]{2,1,0:T(8,128)(2,1)S(1)} %slice.301), channel_id=1, source_target_pairs={{0,1},{1,0},{2,3},{3,2},{4,5},{5,4},{6,7},{7,6},{8,9},{9,8},{10,11... | collective-permute-start | bytes 196616 | tf_op jit(solution)/shard_map/ppermute | solution.py:212

commit v14 on v10

--- a/solution.py
+++ b/solution.py
@@ -197,15 +197,23 @@
     gather_second = shards * (width + half_o) * voxels * 2 <= 1 << 22
     gather_second = gather_second and (grad_first.size // shards) % voxels == 0
     if gather_second:
+        own_half = lax.dynamic_slice_in_dim(
+            grid.reshape(width, voxels), pair_index * half_o, half_o, 0
+        )
         both, first_grad = fused_chain(
-            jnp.concatenate([grid.reshape(width, voxels), cot], axis=0),
-            grad_first,
-            ("space", "sub"),
+            jnp.concatenate([own_half, cot], axis=0), grad_first, ("space", "sub")
+        )
+        mine = both[:, :half_o]
+        other = lax.ppermute(mine, "ch", [(0, 1), (1, 0)])
+        hidden_all = jnp.where(
+            pair_index == 0,
+            jnp.concatenate([mine, other], axis=1),
+            jnp.concatenate([other, mine], axis=1),
         )
         second_grad = (
             second_grad_rows(
-                both[:, :width].reshape(both.shape[0], width, half_z, half_s, half_s),
-                both[:, width:],
+                hidden_all.reshape(both.shape[0], width, half_z, half_s, half_s),
+                both[:, half_o:],
                 ("space", "sub"),
                 second_weight.shape[0],
             )

time: 48.9 us -> 48.3 us (0.988)
  waiting for transfers between devices: 12.5 us -> 11.2 us
    ppermute x3, waiting for transfers between devices: 12.5 us -> 10.8 us  [fused_chain(): got = lax.ppermute(message, name, perm)]
  transfers between devices with their start and end apart: 6 -> 7, of which waited for: 3 -> 4; matrix products, arithmetic and copies ran while one was open for 13% -> 15% of each run, Pallas kernels for 0% -> 0%
where the time goes in v14:
time: 48.3 us; the launch traced here: 47.8 us
  starting transfers between devices  16.5 us (34%)
  waiting for transfers between devices  11.2 us (23%)
  local copies, waits for them, and re-layouts  9.92 us (21%)
  blocking collectives  3.68 us (8%)
  matrix products  2.84 us (6%)
  between operations  1.89 us (4%)
  other arithmetic  1.87 us (4%)
    ppermute x3, waiting for transfers between devices, fused_chain(): got = lax.ppermute(message, name, perm)  10.8 us
    all_to_all x1, starting transfers between devices, block(): lax.all_to_all(volumes, 'space', split_axis=1, concat_axis=3, tiled=True)  6.36 us
    all_to_all x1, starting transfers between devices, block(): lax.all_to_all(grad_sample.reshape(1, 1, half_c, depth, XY * XY), 'space'...  5.09 us
    ppermute x3, starting transfers between devices, fused_chain(): got = lax.ppermute(message, name, perm)  4.88 us
    unnamed x40, local copies, waits for them, and re-layouts  2.61 us
    all_gather x1, blocking collectives, block(): all_first = lax.all_gather(first_weight, 'ch', axis=1, tiled=True)  1.85 us
    all_gather x1, blocking collectives, block(): all_pre_grad = lax.all_gather(pre_grad, 'ch', axis=0, tiled=True)  1.83 us
    reshape x17, local copies, waits for them, and re-layouts, plane_stack(): windows.append(window.reshape(chans, depth * side * side))  1.8 us
  transfers between devices with their start and end apart: 7, of which 4 were waited for; matrix products, arithmetic and copies ran while one was open for 15% of the time, Pallas kernels for 0%

profile of v14, /device:TPU:0, one launch (start us, length us, event | category | flops | bytes accessed | tf_op | source)
XLA Modules:
  0.0 47.8 jit_solution(6783546476658018058)
XLA Ops:
  0.6 6.4 %all-to-all-start = ((bf16[1,4,32,1,256]{4,2,3,0,1:T(8,128)(2,1)}), bf16[1,4,32,1,256]{4,2,3,0,1:T(8,128)(2,1)S(1)}, u32[]{:S(2)}, u32[]{:S(2)}) async-start(bf16[1,4,32,1,256]{4,2,3,0,1:T(8,128)(2,1)} %bitcast.270), calls=%async_computation | async-start | bytes 131072 | tf_op jit(solution)/shard_map/all_to_all | solution.py:169
  7.0 0.9 %copy.60 = bf16[1,1,64,2,64]{2,4,3,1,0:T(8,128)(2,1)S(1)} copy(bf16[1,1,64,2,64]{4,3,2,1,0:T(2,128)(2,1)} %param.5) | data formatting | bytes 32768 | tf_op args[1]
  8.0 0.6 %copy-done.1 = bf16[1,1,64,2,64]{4,3,2,1,0:T(2,128)(2,1)S(1)} copy-done((bf16[1,1,64,2,64]{4,3,2,1,0:T(2,128)(2,1)S(1)}, bf16[1,1,64,2,64]{4,3,2,1,0:T(2,128)(2,1)}, u32[]{:S(2)}) %copy-start.1) | copy-done | bytes 16408
  8.7 0.2 copy-done
  10.3 0.3 fusion.31
  10.7 0.3 fusion.30
  11.1 0.3 fusion.2
  11.9 1.9 %all_gather.6 = bf16[256,128]{0,1:T(8,128)(2,1)S(1)} all-gather(bf16[256,64]{0,1:T(8,128)(2,1)S(1)} %copy-done.2), channel_id=1, replica_groups=mesh['groups'=2,'space'=4,'sub'=2,'ch'=2] {'ch'}, dimensions={1}, use_global_device_ids=true | all-gather | bytes 98304 | tf_op jit(solution)/shard_map/all_gather | solution.py:175
  14.2 0.2 copy.49
  14.4 0.2 reshape.286
  15.1 1.8 %all_gather.7 = bf16[128,128]{1,0:T(8,128)(2,1)S(1)} all-gather(bf16[64,128]{1,0:T(8,128)(2,1)S(1)} %fusion.20), channel_id=1, replica_groups=mesh['groups'=2,'space'=4,'sub'=2,'ch'=2] {'ch'}, dimensions={0}, use_global_device_ids=true | all-gather | bytes 49152 | tf_op jit(solution)/shard_map/all_gather | solution.py:226
  17.3 0.2 fusion.24
  17.7 0.2 fusion.27
  19.1 0.3 fusion
  19.3 0.3 copy.73
  19.6 0.7 %copy.74 = bf16[1,1,16,4,256]{4,2,1,0,3:T(8,128)(2,1)} copy(bf16[1,1,16,4,256]{2,4,3,1,0:T(8,128)(2,1)S(1)} %bitcast.194) | data formatting | bytes 65536 | tf_op jit(solution)/shard_map/convert_element_type | solution.py:233
  20.4 5.1 %all-to-all-start.1 = ((bf16[1,1,16,4,256]{4,2,1,0,3:T(8,128)(2,1)}), bf16[1,1,16,4,256]{4,2,1,0,3:T(8,128)(2,1)S(1)}, u32[]{:S(2)}, u32[]{:S(2)}) async-start(bf16[1,1,16,4,256]{4,2,1,0,3:T(8,128)(2,1)} %copy.74), calls=%async_computation.1 | async-start | bytes 65536 | tf_op jit(solution)/shard_map/all_to_all | solution.py:234
  25.7 3.0 %collective-permute-start.1 = (bf16[256,128]{1,0:T(8,128)(2,1)S(1)}, bf16[256,128]{1,0:T(8,128)(2,1)S(1)}, u32[]{:S(2)}, u32[]{:S(2)}) collective-permute-start(bf16[256,128]{1,0:T(8,128)(2,1)S(1)} %pad_maximum_fusion.4), channel_id=1, source_target_pairs={{0,8},{4,12},{8,0},{12,4},{1,9},{5,13},{9,1},{13,5},{2,10},{6,14},... | collective-permute-start | bytes 196616 | tf_op jit(solution)/shard_map/ppermute | solution.py:147
  28.7 4.0 %collective-permute-done.1 = bf16[256,128]{1,0:T(8,128)(2,1)S(1)} collective-permute-done((bf16[256,128]{1,0:T(8,128)(2,1)S(1)}, bf16[256,128]{1,0:T(8,128)(2,1)S(1)}, u32[]{:S(2)}, u32[]{:S(2)}) %collective-permute-start.1) | collective-permute-done | bytes 65568 | tf_op jit(solution)/shard_map/ppermute | solution.py:147
  33.0 0.3 collective-permute-start.2
  33.3 4.1 %collective-permute-done.2 = bf16[320,128]{1,0:T(8,128)(2,1)S(1)} collective-permute-done((bf16[320,128]{1,0:T(8,128)(2,1)S(1)}, bf16[320,128]{1,0:T(8,128)(2,1)S(1)}, u32[]{:S(2)}, u32[]{:S(2)}) %collective-permute-start.2) | collective-permute-done | bytes 81952 | tf_op jit(solution)/shard_map/ppermute | solution.py:147
  37.8 1.5 %collective-permute-start.3 = (bf16[544,128]{1,0:T(8,128)(2,1)S(1)}, bf16[544,128]{1,0:T(8,128)(2,1)S(1)}, u32[]{:S(2)}, u32[]{:S(2)}) collective-permute-start(bf16[544,128]{1,0:T(8,128)(2,1)S(1)} %pad_maximum_fusion.1), channel_id=1, source_target_pairs={{0,2},{2,0},{1,3},{3,1},{4,6},{6,4},{5,7},{7,5},{8,10},{10,8},{9,1... | collective-permute-start | bytes 417800 | tf_op jit(solution)/shard_map/ppermute | solution.py:147
  39.4 0.2 fusion.10
  39.5 0.7 %reshape.314 = bf16[1,1,64,2,64]{4,3,2,1,0:T(2,128)(2,1)} reshape(bf16[64,128]{1,0:T(8,128)(2,1)S(1)} %fusion.10) | data formatting | bytes 32768 | tf_op jit(solution)/shard_map/reshape | solution.py:183
  40.2 2.7 %collective-permute-done.3 = bf16[544,128]{1,0:T(8,128)(2,1)S(1)} collective-permute-done((bf16[544,128]{1,0:T(8,128)(2,1)S(1)}, bf16[544,128]{1,0:T(8,128)(2,1)S(1)}, u32[]{:S(2)}, u32[]{:S(2)}) %collective-permute-start.3) | collective-permute-done | bytes 139296 | tf_op jit(solution)/shard_map/ppermute | solution.py:147
  43.4 0.6 %fusion.22 = f32[32,64]{1,0:T(8,128)} fusion(f32[32,64]{1,0:T(8,128)S(1)} %reshape.363, f32[32,64]{1,0:T(8,128)S(1)} %reshape.362, f32[2,32,64]{2,1,0:T(8,128)S(1)} %fusion.18, s32[]{:T(128)S(6)} %select_n.177), kind=kLoop, calls=%fused_computation.146 | loop fusion | flops 4096 | bytes 32772 | tf_op jit(solution)/shard_map/add | solution.py:151
  44.0 0.4 collective-permute-done.4
  44.6 0.3 maximum_select_fusion
  45.0 0.2 fusion.7
  45.2 0.5 %pad_dynamic-slice_fusion = (bf16[8,128,2,8,8]{1,4,3,2,0:T(8,128)(2,1)S(1)}, bf16[8,128,2,8,8]{1,4,3,2,0:T(8,128)(2,1)S(1)}, bf16[8,128,2,8,8]{1,4,3,2,0:T(8,128)(2,1)S(1)}, bf16[8,128,2,8,8]{1,4,3,2,0:T(8,128)(2,1)S(1)}) fusion(s32[]{:T(128)S(6)} %select_n.211, s32[]{:T(128)S(6)} %select_n.214, s32[]{:T(128)S(6)} %select_n.216, ...), kind=kLoop, calls=%fused_computation | loop fusion | bytes 1310768 | tf_op jit(solution)/shard_map/dynamic_slice | solution.py:113
  46.5 0.8 %dynamic-slice_multiply_fusion = f32[432,64]{0,1:T(8,128)} fusion(f32[640,64]{0,1:T(8,128)S(1)} %fusion.3, s32[]{:T(128)S(6)} %select_n.217), kind=kLoop, calls=%fused_computation.81 | loop fusion | flops 27648 | bytes 221188 | tf_op jit(solution)/shard_map/mul | solution.py:214
  47.2 0.6 %copy.128 = bf16[1,4,16,1,256]{4,2,3,1,0:T(8,128)(2,1)} copy(bf16[1,4,16,1,256]{4,2,3,1,0:T(8,128)(2,1)S(1)} %bitcast.261) | data formatting | bytes 65536
  (124 shorter events, 6.4 us)
Async XLA Ops:
  0.6 13.4 %all-to-all-start = ((bf16[1,4,32,1,256]{4,2,3,0,1:T(8,128)(2,1)}), bf16[1,4,32,1,256]{4,2,3,0,1:T(8,128)(2,1)S(1)}, u32[]{:S(2)}, u32[]{:S(2)}) async-start(bf16[1,4,32,1,256]{4,2,3,0,1:T(8,128)(2,1)} %bitcast.270), calls=%async_computation | async-start | bytes 131072 | tf_op jit(solution)/shard_map/all_to_all | solution.py:169
  7.8 0.8 %copy-start.1 = (bf16[1,1,64,2,64]{4,3,2,1,0:T(2,128)(2,1)S(1)}, bf16[1,1,64,2,64]{4,3,2,1,0:T(2,128)(2,1)}, u32[]{:S(2)}) copy-start(bf16[1,1,64,2,64]{4,3,2,1,0:T(2,128)(2,1)} %param.5) | copy-start | bytes 49156
  7.9 1.0 %copy-start = (bf16[3456,64]{0,1:T(8,128)(2,1)S(1)}, bf16[3456,64]{0,1:T(8,128)(2,1)}, u32[]{:S(2)}) copy-start(bf16[3456,64]{0,1:T(8,128)(2,1)} %param.7) | copy-start | bytes 1327108
  11.1 0.8 %copy-start.2 = (bf16[256,64]{0,1:T(8,128)(2,1)S(1)}, bf16[256,64]{0,1:T(8,128)(2,1)}, u32[]{:S(2)}) copy-start(bf16[256,64]{0,1:T(8,128)(2,1)} %param.6) | copy-start | bytes 98308
  11.4 3.6 %collective-permute-start = (f32[64,128]{1,0:T(8,128)S(1)}, f32[64,128]{1,0:T(8,128)S(1)}, u32[]{:S(2)}, u32[]{:S(2)}) collective-permute-start(f32[64,128]{1,0:T(8,128)S(1)} %dynamic-slice_bitcast_fusion), channel_id=1, source_target_pairs={{0,1},{1,0},{2,3},{3,2},{4,5},{5,4},{6,7},{7,6},{8,9},{9,8},{10,11... | collective-permute-start | bytes 98312 | tf_op jit(solution)/shard_map/ppermute | solution.py:94
  20.4 19.9 %all-to-all-start.1 = ((bf16[1,1,16,4,256]{4,2,1,0,3:T(8,128)(2,1)}), bf16[1,1,16,4,256]{4,2,1,0,3:T(8,128)(2,1)S(1)}, u32[]{:S(2)}, u32[]{:S(2)}) async-start(bf16[1,1,16,4,256]{4,2,1,0,3:T(8,128)(2,1)} %copy.74), calls=%async_computation.1 | async-start | bytes 65536 | tf_op jit(solution)/shard_map/all_to_all | solution.py:234
  25.7 7.0 %collective-permute-start.1 = (bf16[256,128]{1,0:T(8,128)(2,1)S(1)}, bf16[256,128]{1,0:T(8,128)(2,1)S(1)}, u32[]{:S(2)}, u32[]{:S(2)}) collective-permute-start(bf16[256,128]{1,0:T(8,128)(2,1)S(1)} %pad_maximum_fusion.4), channel_id=1, source_target_pairs={{0,8},{4,12},{8,0},{12,4},{1,9},{5,13},{9,1},{13,5},{2,10},{6,14},... | collective-permute-start | bytes 196616 | tf_op jit(solution)/shard_map/ppermute | solution.py:147
  33.0 4.5 %collective-permute-start.2 = (bf16[320,128]{1,0:T(8,128)(2,1)S(1)}, bf16[320,128]{1,0:T(8,128)(2,1)S(1)}, u32[]{:S(2)}, u32[]{:S(2)}) collective-permute-start(bf16[320,128]{1,0:T(8,128)(2,1)S(1)} %pad_maximum_fusion.3), channel_id=1, source_target_pairs={{0,4},{4,0},{8,12},{12,8},{1,5},{5,1},{9,13},{13,9},{2,6},{6,2},{1... | collective-permute-start | bytes 245768 | tf_op jit(solution)/shard_map/ppermute | solution.py:147
  37.8 5.1 %collective-permute-start.3 = (bf16[544,128]{1,0:T(8,128)(2,1)S(1)}, bf16[544,128]{1,0:T(8,128)(2,1)S(1)}, u32[]{:S(2)}, u32[]{:S(2)}) collective-permute-start(bf16[544,128]{1,0:T(8,128)(2,1)S(1)} %pad_maximum_fusion.1), channel_id=1, source_target_pairs={{0,2},{2,0},{1,3},{3,1},{4,6},{6,4},{5,7},{7,5},{8,10},{10,8},{9,1... | collective-permute-start | bytes 417800 | tf_op jit(solution)/shard_map/ppermute | solution.py:147
  43.0 1.4 %collective-permute-start.4 = (bf16[8,64,128]{2,1,0:T(8,128)(2,1)S(1)}, bf16[8,64,128]{2,1,0:T(8,128)(2,1)S(1)}, u32[]{:S(2)}, u32[]{:S(2)}) collective-permute-start(bf16[8,64,128]{2,1,0:T(8,128)(2,1)S(1)} %slice.291), channel_id=1, source_target_pairs={{0,1},{1,0},{2,3},{3,2},{4,5},{5,4},{6,7},{7,6},{8,9},{9,8},{10,11... | collective-permute-start | bytes 393224 | tf_op jit(solution)/shard_map/ppermute | solution.py:207

commit v15 on v14

--- a/solution.py
+++ b/solution.py
@@ -223,7 +223,15 @@
         grad_second = conv_weight_grad(grid, cot) * factor
         first_grad = halving_scatter(grad_first, ("space", "sub"))
         second_grad = halving_scatter(grad_second, ("space", "sub"))
-    all_pre_grad = lax.all_gather(pre_grad, "ch", axis=0, tiled=True)
+    if lax.axis_size("ch") == 2:
+        other_grad = lax.ppermute(pre_grad, "ch", [(0, 1), (1, 0)])
+        all_pre_grad = jnp.where(
+            pair_index == 0,
+            jnp.concatenate([pre_grad, other_grad], axis=0),
+            jnp.concatenate([other_grad, pre_grad], axis=0),
+        )
+    else:
+        all_pre_grad = lax.all_gather(pre_grad, "ch", axis=0, tiled=True)
     first_rows = lax.dynamic_slice_in_dim(
         all_first.reshape(8, chans, width), pair_index * half_c, half_c, 1
     )

time: 48.3 us -> 42.6 us (0.88)
  waiting for transfers between devices: 11.2 us -> 7.09 us
  blocking collectives: 3.68 us -> 1.85 us
    ppermute x3, waiting for transfers between devices: 10.8 us -> 3.82 us  [fused_chain(): got = lax.ppermute(message, name, perm)]
    all_to_all x1, waiting for transfers between devices: 0.01 us -> 2.89 us  [block(): lax.all_to_all(grad_sample.reshape(1, 1, half_c, depth, XY * XY), 'space'...]
    all_gather x1 -> x0, blocking collectives: 1.83 us -> none  [block(): all_pre_grad = lax.all_gather(pre_grad, 'ch', axis=0, tiled=True)]
  transfers between devices with their start and end apart: 7 -> 8, of which waited for: 4 -> 3; matrix products, arithmetic and copies ran while one was open for 15% -> 24% of each run, Pallas kernels for 0% -> 0%
where the time goes in v15:
time: 42.6 us; the launch traced here: 42.2 us
  starting transfers between devices  16.7 us (39%)
  local copies, waits for them, and re-layouts  9.92 us (23%)
  waiting for transfers between devices  7.09 us (17%)
  matrix products  2.83 us (7%)
  between operations  1.92 us (5%)
  other arithmetic  1.88 us (4%)
  blocking collectives  1.85 us (4%)
    all_to_all x1, starting transfers between devices, block(): lax.all_to_all(volumes, 'space', split_axis=1, concat_axis=3, tiled=True)  6.36 us
    ppermute x3, starting transfers between devices, fused_chain(): got = lax.ppermute(message, name, perm)  5.33 us
    all_to_all x1, starting transfers between devices, block(): lax.all_to_all(grad_sample.reshape(1, 1, half_c, depth, XY * XY), 'space'...  4.65 us
    ppermute x3, waiting for transfers between devices, fused_chain(): got = lax.ppermute(message, name, perm)  3.82 us
    all_to_all x1, waiting for transfers between devices, block(): lax.all_to_all(grad_sample.reshape(1, 1, half_c, depth, XY * XY), 'space'...  2.89 us
    unnamed x40, local copies, waits for them, and re-layouts  2.61 us
    all_gather x1, blocking collectives, block(): all_first = lax.all_gather(first_weight, 'ch', axis=1, tiled=True)  1.85 us
    reshape x17, local copies, waits for them, and re-layouts, plane_stack(): windows.append(window.reshape(chans, depth * side * side))  1.8 us
  transfers between devices with their start and end apart: 8, of which 3 were waited for; matrix products, arithmetic and copies ran while one was open for 24% of the time, Pallas kernels for 0%

profile of v15, /device:TPU:0, one launch (start us, length us, event | category | flops | bytes accessed | tf_op | source)
XLA Modules:
  0.0 42.2 jit_solution(4801346677249558758)
XLA Ops:
  0.6 6.4 %all-to-all-start = ((bf16[1,4,32,1,256]{4,2,3,0,1:T(8,128)(2,1)}), bf16[1,4,32,1,256]{4,2,3,0,1:T(8,128)(2,1)S(1)}, u32[]{:S(2)}, u32[]{:S(2)}) async-start(bf16[1,4,32,1,256]{4,2,3,0,1:T(8,128)(2,1)} %bitcast.270), calls=%async_computation | async-start | bytes 131072 | tf_op jit(solution)/shard_map/all_to_all | solution.py:169
  7.0 0.9 %copy.60 = bf16[1,1,64,2,64]{2,4,3,1,0:T(8,128)(2,1)S(1)} copy(bf16[1,1,64,2,64]{4,3,2,1,0:T(2,128)(2,1)} %param.5) | data formatting | bytes 32768 | tf_op args[1]
  8.0 0.6 %copy-done.1 = bf16[1,1,64,2,64]{4,3,2,1,0:T(2,128)(2,1)S(1)} copy-done((bf16[1,1,64,2,64]{4,3,2,1,0:T(2,128)(2,1)S(1)}, bf16[1,1,64,2,64]{4,3,2,1,0:T(2,128)(2,1)}, u32[]{:S(2)}) %copy-start.1) | copy-done | bytes 16408
  8.7 0.2 copy-done
  10.3 0.3 fusion.32
  10.7 0.3 fusion.31
  11.1 0.3 fusion.2
  11.9 1.9 %all_gather.3 = bf16[256,128]{0,1:T(8,128)(2,1)S(1)} all-gather(bf16[256,64]{0,1:T(8,128)(2,1)S(1)} %copy-done.2), channel_id=1, replica_groups=mesh['groups'=2,'space'=4,'sub'=2,'ch'=2] {'ch'}, dimensions={1}, use_global_device_ids=true | all-gather | bytes 98304 | tf_op jit(solution)/shard_map/all_gather | solution.py:175
  14.2 0.2 copy.49
  14.4 0.2 reshape.286
  15.1 0.2 collective-permute-start.1
  15.7 0.2 fusion.25
  16.1 0.2 fusion.28
  17.6 3.0 %collective-permute-start.2 = (bf16[256,128]{1,0:T(8,128)(2,1)S(1)}, bf16[256,128]{1,0:T(8,128)(2,1)S(1)}, u32[]{:S(2)}, u32[]{:S(2)}) collective-permute-start(bf16[256,128]{1,0:T(8,128)(2,1)S(1)} %pad_maximum_fusion.4), channel_id=1, source_target_pairs={{0,8},{4,12},{8,0},{12,4},{1,9},{5,13},{9,1},{13,5},{2,10},{6,14},... | collective-permute-start | bytes 196616 | tf_op jit(solution)/shard_map/ppermute | solution.py:147
  20.8 3.8 %collective-permute-done.2 = bf16[256,128]{1,0:T(8,128)(2,1)S(1)} collective-permute-done((bf16[256,128]{1,0:T(8,128)(2,1)S(1)}, bf16[256,128]{1,0:T(8,128)(2,1)S(1)}, u32[]{:S(2)}, u32[]{:S(2)}) %collective-permute-start.2) | collective-permute-done | bytes 65568 | tf_op jit(solution)/shard_map/ppermute | solution.py:147
  24.9 0.8 %collective-permute-start.3 = (bf16[320,128]{1,0:T(8,128)(2,1)S(1)}, bf16[320,128]{1,0:T(8,128)(2,1)S(1)}, u32[]{:S(2)}, u32[]{:S(2)}) collective-permute-start(bf16[320,128]{1,0:T(8,128)(2,1)S(1)} %pad_maximum_fusion.3), channel_id=1, source_target_pairs={{0,4},{4,0},{8,12},{12,8},{1,5},{5,1},{9,13},{13,9},{2,6},{6,2},{1... | collective-permute-start | bytes 245768 | tf_op jit(solution)/shard_map/ppermute | solution.py:147
  25.7 0.2 fusion
  26.0 0.3 copy.73
  26.2 0.7 %copy.74 = bf16[1,1,16,4,256]{4,2,1,0,3:T(8,128)(2,1)} copy(bf16[1,1,16,4,256]{2,4,3,1,0:T(8,128)(2,1)S(1)} %bitcast.195) | data formatting | bytes 65536 | tf_op jit(solution)/shard_map/convert_element_type | solution.py:241
  27.0 4.6 %all-to-all-start.1 = ((bf16[1,1,16,4,256]{4,2,1,0,3:T(8,128)(2,1)}), bf16[1,1,16,4,256]{4,2,1,0,3:T(8,128)(2,1)S(1)}, u32[]{:S(2)}, u32[]{:S(2)}) async-start(bf16[1,1,16,4,256]{4,2,1,0,3:T(8,128)(2,1)} %copy.74), calls=%async_computation.1 | async-start | bytes 65536 | tf_op jit(solution)/shard_map/all_to_all | solution.py:242
  31.9 1.6 %collective-permute-start.4 = (bf16[544,128]{1,0:T(8,128)(2,1)S(1)}, bf16[544,128]{1,0:T(8,128)(2,1)S(1)}, u32[]{:S(2)}, u32[]{:S(2)}) collective-permute-start(bf16[544,128]{1,0:T(8,128)(2,1)S(1)} %pad_maximum_fusion.1), channel_id=1, source_target_pairs={{0,2},{2,0},{1,3},{3,1},{4,6},{6,4},{5,7},{7,5},{8,10},{10,8},{9,1... | collective-permute-start | bytes 417800 | tf_op jit(solution)/shard_map/ppermute | solution.py:147
  33.5 0.2 fusion.10
  33.7 0.7 %reshape.314 = bf16[1,1,64,2,64]{4,3,2,1,0:T(2,128)(2,1)} reshape(bf16[64,128]{1,0:T(8,128)(2,1)S(1)} %fusion.10) | data formatting | bytes 32768 | tf_op jit(solution)/shard_map/reshape | solution.py:183
  34.4 2.9 %all-to-all-done.1 = bf16[1,1,16,4,256]{4,2,1,0,3:T(8,128)(2,1)S(1)} async-done(((bf16[1,1,16,4,256]{4,2,1,0,3:T(8,128)(2,1)}), bf16[1,1,16,4,256]{4,2,1,0,3:T(8,128)(2,1)S(1)}, u32[]{:S(2)}, u32[]{:S(2)}) %all-to-all-start.1) | async-done | bytes 32800 | tf_op jit(solution)/shard_map/all_to_all | solution.py:242
  37.4 0.2 copy.76
  37.8 0.6 %fusion.23 = f32[32,64]{1,0:T(8,128)} fusion(f32[32,64]{1,0:T(8,128)S(1)} %reshape.363, f32[32,64]{1,0:T(8,128)S(1)} %reshape.362, f32[2,32,64]{2,1,0:T(8,128)S(1)} %fusion.19, s32[]{:T(128)S(6)} %select_n.187), kind=kLoop, calls=%fused_computation.148 | loop fusion | flops 4096 | bytes 32772 | tf_op jit(solution)/shard_map/add | solution.py:151
  38.4 0.4 collective-permute-done.5
  39.0 0.3 maximum_select_fusion
  39.4 0.2 fusion.7
  39.6 0.5 %pad_dynamic-slice_fusion = (bf16[8,128,2,8,8]{1,4,3,2,0:T(8,128)(2,1)S(1)}, bf16[8,128,2,8,8]{1,4,3,2,0:T(8,128)(2,1)S(1)}, bf16[8,128,2,8,8]{1,4,3,2,0:T(8,128)(2,1)S(1)}, bf16[8,128,2,8,8]{1,4,3,2,0:T(8,128)(2,1)S(1)}) fusion(s32[]{:T(128)S(6)} %select_n.221, s32[]{:T(128)S(6)} %select_n.224, s32[]{:T(128)S(6)} %select_n.226, ...), kind=kLoop, calls=%fused_computation | loop fusion | bytes 1310768 | tf_op jit(solution)/shard_map/dynamic_slice | solution.py:113
  40.8 0.8 %dynamic-slice_multiply_fusion = f32[432,64]{0,1:T(8,128)} fusion(f32[640,64]{0,1:T(8,128)S(1)} %fusion.3, s32[]{:T(128)S(6)} %select_n.227), kind=kLoop, calls=%fused_computation.81 | loop fusion | flops 27648 | bytes 221188 | tf_op jit(solution)/shard_map/mul | solution.py:214
  41.6 0.6 %copy.128 = bf16[1,4,16,1,256]{4,2,3,1,0:T(8,128)(2,1)} copy(bf16[1,4,16,1,256]{4,2,3,1,0:T(8,128)(2,1)S(1)} %bitcast.262) | data formatting | bytes 65536
  (126 shorter events, 6.2 us)
Async XLA Ops:
  0.6 13.4 %all-to-all-start = ((bf16[1,4,32,1,256]{4,2,3,0,1:T(8,128)(2,1)}), bf16[1,4,32,1,256]{4,2,3,0,1:T(8,128)(2,1)S(1)}, u32[]{:S(2)}, u32[]{:S(2)}) async-start(bf16[1,4,32,1,256]{4,2,3,0,1:T(8,128)(2,1)} %bitcast.270), calls=%async_computation | async-start | bytes 131072 | tf_op jit(solution)/shard_map/all_to_all | solution.py:169
  7.8 0.8 %copy-start.1 = (bf16[1,1,64,2,64]{4,3,2,1,0:T(2,128)(2,1)S(1)}, bf16[1,1,64,2,64]{4,3,2,1,0:T(2,128)(2,1)}, u32[]{:S(2)}) copy-start(bf16[1,1,64,2,64]{4,3,2,1,0:T(2,128)(2,1)} %param.5) | copy-start | bytes 49156
  7.9 1.0 %copy-start = (bf16[3456,64]{0,1:T(8,128)(2,1)S(1)}, bf16[3456,64]{0,1:T(8,128)(2,1)}, u32[]{:S(2)}) copy-start(bf16[3456,64]{0,1:T(8,128)(2,1)} %param.7) | copy-start | bytes 1327108
  11.1 0.8 %copy-start.2 = (bf16[256,64]{0,1:T(8,128)(2,1)S(1)}, bf16[256,64]{0,1:T(8,128)(2,1)}, u32[]{:S(2)}) copy-start(bf16[256,64]{0,1:T(8,128)(2,1)} %param.6) | copy-start | bytes 98308
  11.4 3.6 %collective-permute-start = (f32[64,128]{1,0:T(8,128)S(1)}, f32[64,128]{1,0:T(8,128)S(1)}, u32[]{:S(2)}, u32[]{:S(2)}) collective-permute-start(f32[64,128]{1,0:T(8,128)S(1)} %dynamic-slice_bitcast_fusion), channel_id=1, source_target_pairs={{0,1},{1,0},{2,3},{3,2},{4,5},{5,4},{6,7},{7,6},{8,9},{9,8},{10,11... | collective-permute-start | bytes 98312 | tf_op jit(solution)/shard_map/ppermute | solution.py:94
  15.1 5.5 %collective-permute-start.1 = (bf16[64,128]{1,0:T(8,128)(2,1)S(1)}, bf16[64,128]{1,0:T(8,128)(2,1)S(1)}, u32[]{:S(2)}, u32[]{:S(2)}) collective-permute-start(bf16[64,128]{1,0:T(8,128)(2,1)S(1)} %fusion.21), channel_id=1, source_target_pairs={{0,1},{1,0},{2,3},{3,2},{4,5},{5,4},{6,7},{7,6},{8,9},{9,8},{10,11... | collective-permute-start | bytes 49160 | tf_op jit(solution)/shard_map/ppermute | solution.py:227
  17.6 7.0 %collective-permute-start.2 = (bf16[256,128]{1,0:T(8,128)(2,1)S(1)}, bf16[256,128]{1,0:T(8,128)(2,1)S(1)}, u32[]{:S(2)}, u32[]{:S(2)}) collective-permute-start(bf16[256,128]{1,0:T(8,128)(2,1)S(1)} %pad_maximum_fusion.4), channel_id=1, source_target_pairs={{0,8},{4,12},{8,0},{12,4},{1,9},{5,13},{9,1},{13,5},{2,10},{6,14},... | collective-permute-start | bytes 196616 | tf_op jit(solution)/shard_map/ppermute | solution.py:147
  24.9 6.7 %collective-permute-start.3 = (bf16[320,128]{1,0:T(8,128)(2,1)S(1)}, bf16[320,128]{1,0:T(8,128)(2,1)S(1)}, u32[]{:S(2)}, u32[]{:S(2)}) collective-permute-start(bf16[320,128]{1,0:T(8,128)(2,1)S(1)} %pad_maximum_fusion.3), channel_id=1, source_target_pairs={{0,4},{4,0},{8,12},{12,8},{1,5},{5,1},{9,13},{13,9},{2,6},{6,2},{1... | collective-permute-start | bytes 245768 | tf_op jit(solution)/shard_map/ppermute | solution.py:147
  27.0 10.3 %all-to-all-start.1 = ((bf16[1,1,16,4,256]{4,2,1,0,3:T(8,128)(2,1)}), bf16[1,1,16,4,256]{4,2,1,0,3:T(8,128)(2,1)S(1)}, u32[]{:S(2)}, u32[]{:S(2)}) async-start(bf16[1,1,16,4,256]{4,2,1,0,3:T(8,128)(2,1)} %copy.74), calls=%async_computation.1 | async-start | bytes 65536 | tf_op jit(solution)/shard_map/all_to_all | solution.py:242
  31.9 5.3 %collective-permute-start.4 = (bf16[544,128]{1,0:T(8,128)(2,1)S(1)}, bf16[544,128]{1,0:T(8,128)(2,1)S(1)}, u32[]{:S(2)}, u32[]{:S(2)}) collective-permute-start(bf16[544,128]{1,0:T(8,128)(2,1)S(1)} %pad_maximum_fusion.1), channel_id=1, source_target_pairs={{0,2},{2,0},{1,3},{3,1},{4,6},{6,4},{5,7},{7,5},{8,10},{10,8},{9,1... | collective-permute-start | bytes 417800 | tf_op jit(solution)/shard_map/ppermute | solution.py:147
  37.4 1.4 %collective-permute-start.5 = (bf16[8,64,128]{2,1,0:T(8,128)(2,1)S(1)}, bf16[8,64,128]{2,1,0:T(8,128)(2,1)S(1)}, u32[]{:S(2)}, u32[]{:S(2)}) collective-permute-start(bf16[8,64,128]{2,1,0:T(8,128)(2,1)S(1)} %slice.291), channel_id=1, source_target_pairs={{0,1},{1,0},{2,3},{3,2},{4,5},{5,4},{6,7},{7,6},{8,9},{9,8},{10,11... | collective-permute-start | bytes 393224 | tf_op jit(solution)/shard_map/ppermute | solution.py:207
